TPU v7x, 512 devices: a whole 4x8x8 slice. The times are simulated.
512 devices in a mesh: seg: 32 (over y, x), sec: 16 (over z, core).
Axes of the slice: x: 4, y: 8, z: 8, core: 2. Of those that a mesh axis runs over, the one named last changes fastest.
Arguments:
- blocks: bfloat16 [32, 4, 16, 128, 128], P('seg', None, 'sec'), may hold values from -0.5 to 0.5
- left_edge: bfloat16 [16, 128], P('sec'), may hold values from -0.5 to 0.5
- right_edge: bfloat16 [16, 128], P('sec'), may hold values from -6 to 6
- occupation: int32 [1024, 32], P(None, 'seg'), may hold values from 0 to 3
- start_sector: int32 [1024], replicated, may hold values from 0 to 15
Outputs:
- amplitude: float32 [1024], replicated
All inputs are finite; a program needn't handle non-finite values.
Results may differ from a plain program's by a relative error of at most 0.015.
Values may be sent and summed in bfloat16 or wider, within the bound.
No kernel may reach another device: no remote copies, remote signals or barrier semaphores. Data moves between devices by JAX's collectives and lax.ppermute only.
A program may use at most 64 MiB of HBM per device.

v0:
```python
import jax
import jax.numpy as jnp
from jax import lax
from jax.sharding import PartitionSpec as P


def padded_2(block, sides, width, periodic):
    for axis, dim in sides:
        count = lax.axis_size(axis)
        forward = [(i, i + 1) for i in range(count - 1)]
        if periodic:
            forward.append((count - 1, 0))
        backward = [(target, source) for source, target in forward]
        low = lax.ppermute(
            lax.slice_in_dim(block, block.shape[dim] - width, None, axis=dim), axis, forward
        )
        high = lax.ppermute(lax.slice_in_dim(block, 0, width, axis=dim), axis, backward)
        block = jnp.concatenate([low, block, high], axis=dim)
    return block


def state_masks(occ_site):
    levels = jnp.arange(4, dtype=jnp.int32)
    return (occ_site[:, None] == levels[None, :]).astype(jnp.float32)


def forward_send(vector, block_site, occ_masks):
    products = jnp.einsum("ka,nab->knb", vector, block_site, preferred_element_type=jnp.float32)
    terms = products * occ_masks[:, :, None]
    kept_term = (terms[:, 0] + terms[:, 3]).astype(jnp.bfloat16)
    upward = terms[:, 1].astype(jnp.bfloat16)
    downward = terms[:, 2].astype(jnp.bfloat16)
    return (kept_term, jnp.stack([downward, upward]))


def backward_send(vector, block_site, occ_masks):
    return (vector, jnp.stack([vector, vector]))


def forward_take(kept_term, padded, block_site, occ_masks):
    total = (
        kept_term.astype(jnp.float32)
        + padded[0].astype(jnp.float32)
        + padded[3].astype(jnp.float32)
    )
    return total.astype(jnp.bfloat16)


def backward_take(kept_term, padded, block_site, occ_masks):
    stacked = jnp.stack([kept_term, padded[3], padded[0], kept_term], axis=1)
    products = jnp.einsum("nab,knb->kna", block_site, stacked, preferred_element_type=jnp.float32)
    return jnp.sum(products * occ_masks[:, :, None], axis=1).astype(jnp.bfloat16)


def per_device(blocks, left_edge, right_edge, occupation, start_sector):
    seg_count = lax.axis_size("seg")
    half_count = seg_count // 2
    seg_index = lax.axis_index("seg")
    sec_index = lax.axis_index("sec")
    is_left = seg_index < half_count
    chain_depth = jnp.where(is_left, seg_index, seg_count - 1 - seg_index)
    is_first = chain_depth == 0
    meet_lower = seg_index == half_count - 1
    meet_upper = seg_index == half_count
    conf_count = occupation.shape[0]
    sites_here = occupation.shape[1]
    sector_width = blocks.shape[-1]
    block_count = 1
    columns = jnp.arange(sector_width, dtype=jnp.int32)
    lower_cols = (columns < sector_width // 2).astype(jnp.float32)
    upper_cols = 1.0 - lower_cols
    local_blocks = blocks[:, :, 0]
    left_row = left_edge[0]
    right_row = right_edge[0]
    batch_rows = conf_count // block_count

    def initial():
        zero_row = jnp.zeros_like(left_row)
        initial_left = jnp.where(
            (start_sector == sec_index)[:, None], left_row[None, :], zero_row[None, :]
        )
        initial_right = jnp.broadcast_to(right_row[None, :], (batch_rows, sector_width))
        return jnp.where(is_left, initial_left, initial_right)

    def run_sites(vector):
        position = jnp.where(is_left, 0, sites_here - 1)
        block_site = lax.dynamic_index_in_dim(local_blocks, position, 0, keepdims=False)
        occ_site = lax.dynamic_index_in_dim(occupation, position, 1, keepdims=False)
        occ_masks = state_masks(occ_site)
        kept_term, outgoing = lax.cond(
            is_left, forward_send, backward_send, vector, block_site, occ_masks
        )
        padded = padded_2(outgoing, (("sec", 0),), 1, True)
        vector = lax.cond(
            is_left, forward_take, backward_take, kept_term, padded, block_site, occ_masks
        )
        return vector

    section_count = half_count + block_count - 1

    def section(section_index, state_pair):
        incoming, partial_value = state_pair
        batch_index = section_index - chain_depth
        is_valid = (batch_index >= 0) & (batch_index < block_count)
        vector = jnp.where(is_first, initial(), incoming)
        vector = run_sites(vector)
        padded = padded_2(vector[None], (("seg", 0),), 1, False)
        received = jnp.where(is_left, padded[0], padded[2])
        own_vals = vector.astype(jnp.float32)
        lower_part = jnp.sum(own_vals * padded[2].astype(jnp.float32) * lower_cols[None, :], axis=1)
        upper_part = jnp.sum(own_vals * padded[0].astype(jnp.float32) * upper_cols[None, :], axis=1)
        product = jnp.where(meet_lower, lower_part, upper_part)
        previous = partial_value
        store_here = (meet_lower | meet_upper) & is_valid
        partial_value = jnp.where(store_here, product, previous)
        return (received, partial_value)

    start_state = (
        jnp.zeros((batch_rows, sector_width), jnp.bfloat16),
        jnp.zeros((conf_count,), jnp.float32),
    )
    final_state = lax.fori_loop(0, section_count, section, start_state)
    return lax.psum(final_state[1], ("seg", "sec"))


def solution(mesh):
    in_specs = (
        P("seg", None, "sec", None, None),
        P("sec", None),
        P("sec", None),
        P(None, "seg"),
        P(),
    )
    out_specs = P()
    return jax.shard_map(
        per_device, mesh=mesh, in_specs=in_specs, out_specs=out_specs, check_vma=False
    )
```

profile of v0, /device:TPU:1, one launch (start us, length us, event | category | flops | bytes accessed | tf_op | source)
XLA Modules:
  0.0 528.2 jit_solution(16015874300515925806)
XLA Ops:
  0.0 413.8 %while.18 = (s32[]{:T(128)}, bf16[1024,128]{1,0:T(8,128)(2,1)S(1)}, f32[1024]{0:T(1024)S(1)}, pred[]{:T(512)}, pred[]{:T(512)}, /*index=5*/s32[]{:T(128)}, s32[1...) while((s32[]{:T(128)}, bf16[1024,128]{1,0:T(8,128)(2,1)S(1)}, ...), condition=%wide.region_8.9_spmd.clone, body=%wide.region_0.8_spmd.clone.sunk | while | flops 274213504 | bytes 16602105 | solution.py:122
  4.2 6.8 %collective-permute-start = (bf16[1,1024,128]{2,1,0:T(8,128)(2,1)S(1)}, bf16[1,1024,128]{2,1,0:T(8,128)(2,1)S(1)}, u32[]{:S(2)}, u32[]{:S(2)}) collective-permute-start(bf16[1,1024,128]{2,1,0:T(8,128)(2,1)S(1)} %get-tuple-element.627), channel_id=1, source_target_pairs={{1,0},{2,1},{3,2},{4,3},{5,4},{6,5},{7,6},{8,7},{9,8},{10,9},{11,1... | collective-permute-start | bytes 786440 | tf_op jit(solution)/shard_map/while/body/eval_jaxpr/ppermute | solution.py:17
  30.1 7.4 %collective-permute-start = (bf16[1,1024,128]{2,1,0:T(8,128)(2,1)S(1)}, bf16[1,1024,128]{2,1,0:T(8,128)(2,1)S(1)}, u32[]{:S(2)}, u32[]{:S(2)}) collective-permute-start(bf16[1,1024,128]{2,1,0:T(8,128)(2,1)S(1)} %get-tuple-element.627), channel_id=1, source_target_pairs={{1,0},{2,1},{3,2},{4,3},{5,4},{6,5},{7,6},{8,7},{9,8},{10,9},{11,1... | collective-permute-start | bytes 786440 | tf_op jit(solution)/shard_map/while/body/eval_jaxpr/ppermute | solution.py:17
  55.8 6.6 %collective-permute-start = (bf16[1,1024,128]{2,1,0:T(8,128)(2,1)S(1)}, bf16[1,1024,128]{2,1,0:T(8,128)(2,1)S(1)}, u32[]{:S(2)}, u32[]{:S(2)}) collective-permute-start(bf16[1,1024,128]{2,1,0:T(8,128)(2,1)S(1)} %get-tuple-element.627), channel_id=1, source_target_pairs={{1,0},{2,1},{3,2},{4,3},{5,4},{6,5},{7,6},{8,7},{9,8},{10,9},{11,1... | collective-permute-start | bytes 786440 | tf_op jit(solution)/shard_map/while/body/eval_jaxpr/ppermute | solution.py:17
  65.8 4.4 collective-permute-start.2
  82.1 6.6 %collective-permute-start = (bf16[1,1024,128]{2,1,0:T(8,128)(2,1)S(1)}, bf16[1,1024,128]{2,1,0:T(8,128)(2,1)S(1)}, u32[]{:S(2)}, u32[]{:S(2)}) collective-permute-start(bf16[1,1024,128]{2,1,0:T(8,128)(2,1)S(1)} %get-tuple-element.627), channel_id=1, source_target_pairs={{1,0},{2,1},{3,2},{4,3},{5,4},{6,5},{7,6},{8,7},{9,8},{10,9},{11,1... | collective-permute-start | bytes 786440 | tf_op jit(solution)/shard_map/while/body/eval_jaxpr/ppermute | solution.py:17
  107.9 6.4 %collective-permute-start = (bf16[1,1024,128]{2,1,0:T(8,128)(2,1)S(1)}, bf16[1,1024,128]{2,1,0:T(8,128)(2,1)S(1)}, u32[]{:S(2)}, u32[]{:S(2)}) collective-permute-start(bf16[1,1024,128]{2,1,0:T(8,128)(2,1)S(1)} %get-tuple-element.627), channel_id=1, source_target_pairs={{1,0},{2,1},{3,2},{4,3},{5,4},{6,5},{7,6},{8,7},{9,8},{10,9},{11,1... | collective-permute-start | bytes 786440 | tf_op jit(solution)/shard_map/while/body/eval_jaxpr/ppermute | solution.py:17
  133.2 6.4 %collective-permute-start = (bf16[1,1024,128]{2,1,0:T(8,128)(2,1)S(1)}, bf16[1,1024,128]{2,1,0:T(8,128)(2,1)S(1)}, u32[]{:S(2)}, u32[]{:S(2)}) collective-permute-start(bf16[1,1024,128]{2,1,0:T(8,128)(2,1)S(1)} %get-tuple-element.627), channel_id=1, source_target_pairs={{1,0},{2,1},{3,2},{4,3},{5,4},{6,5},{7,6},{8,7},{9,8},{10,9},{11,1... | collective-permute-start | bytes 786440 | tf_op jit(solution)/shard_map/while/body/eval_jaxpr/ppermute | solution.py:17
  158.5 6.3 %collective-permute-start = (bf16[1,1024,128]{2,1,0:T(8,128)(2,1)S(1)}, bf16[1,1024,128]{2,1,0:T(8,128)(2,1)S(1)}, u32[]{:S(2)}, u32[]{:S(2)}) collective-permute-start(bf16[1,1024,128]{2,1,0:T(8,128)(2,1)S(1)} %get-tuple-element.627), channel_id=1, source_target_pairs={{1,0},{2,1},{3,2},{4,3},{5,4},{6,5},{7,6},{8,7},{9,8},{10,9},{11,1... | collective-permute-start | bytes 786440 | tf_op jit(solution)/shard_map/while/body/eval_jaxpr/ppermute | solution.py:17
  183.7 6.3 %collective-permute-start = (bf16[1,1024,128]{2,1,0:T(8,128)(2,1)S(1)}, bf16[1,1024,128]{2,1,0:T(8,128)(2,1)S(1)}, u32[]{:S(2)}, u32[]{:S(2)}) collective-permute-start(bf16[1,1024,128]{2,1,0:T(8,128)(2,1)S(1)} %get-tuple-element.627), channel_id=1, source_target_pairs={{1,0},{2,1},{3,2},{4,3},{5,4},{6,5},{7,6},{8,7},{9,8},{10,9},{11,1... | collective-permute-start | bytes 786440 | tf_op jit(solution)/shard_map/while/body/eval_jaxpr/ppermute | solution.py:17
  208.9 6.2 %collective-permute-start = (bf16[1,1024,128]{2,1,0:T(8,128)(2,1)S(1)}, bf16[1,1024,128]{2,1,0:T(8,128)(2,1)S(1)}, u32[]{:S(2)}, u32[]{:S(2)}) collective-permute-start(bf16[1,1024,128]{2,1,0:T(8,128)(2,1)S(1)} %get-tuple-element.627), channel_id=1, source_target_pairs={{1,0},{2,1},{3,2},{4,3},{5,4},{6,5},{7,6},{8,7},{9,8},{10,9},{11,1... | collective-permute-start | bytes 786440 | tf_op jit(solution)/shard_map/while/body/eval_jaxpr/ppermute | solution.py:17
  234.1 6.2 %collective-permute-start = (bf16[1,1024,128]{2,1,0:T(8,128)(2,1)S(1)}, bf16[1,1024,128]{2,1,0:T(8,128)(2,1)S(1)}, u32[]{:S(2)}, u32[]{:S(2)}) collective-permute-start(bf16[1,1024,128]{2,1,0:T(8,128)(2,1)S(1)} %get-tuple-element.627), channel_id=1, source_target_pairs={{1,0},{2,1},{3,2},{4,3},{5,4},{6,5},{7,6},{8,7},{9,8},{10,9},{11,1... | collective-permute-start | bytes 786440 | tf_op jit(solution)/shard_map/while/body/eval_jaxpr/ppermute | solution.py:17
  259.2 6.2 %collective-permute-start = (bf16[1,1024,128]{2,1,0:T(8,128)(2,1)S(1)}, bf16[1,1024,128]{2,1,0:T(8,128)(2,1)S(1)}, u32[]{:S(2)}, u32[]{:S(2)}) collective-permute-start(bf16[1,1024,128]{2,1,0:T(8,128)(2,1)S(1)} %get-tuple-element.627), channel_id=1, source_target_pairs={{1,0},{2,1},{3,2},{4,3},{5,4},{6,5},{7,6},{8,7},{9,8},{10,9},{11,1... | collective-permute-start | bytes 786440 | tf_op jit(solution)/shard_map/while/body/eval_jaxpr/ppermute | solution.py:17
  284.8 6.2 %collective-permute-start = (bf16[1,1024,128]{2,1,0:T(8,128)(2,1)S(1)}, bf16[1,1024,128]{2,1,0:T(8,128)(2,1)S(1)}, u32[]{:S(2)}, u32[]{:S(2)}) collective-permute-start(bf16[1,1024,128]{2,1,0:T(8,128)(2,1)S(1)} %get-tuple-element.627), channel_id=1, source_target_pairs={{1,0},{2,1},{3,2},{4,3},{5,4},{6,5},{7,6},{8,7},{9,8},{10,9},{11,1... | collective-permute-start | bytes 786440 | tf_op jit(solution)/shard_map/while/body/eval_jaxpr/ppermute | solution.py:17
  294.4 6.0 %collective-permute-start.2 = (bf16[1,1024,128]{2,1,0:T(8,128)(2,1)S(1)}, bf16[1,1024,128]{2,1,0:T(8,128)(2,1)S(1)}, u32[]{:S(2)}, u32[]{:S(2)}) collective-permute-start(bf16[1,1024,128]{2,1,0:T(8,128)(2,1)S(1)} %bitcast.59), channel_id=1, source_target_pairs={{0,16},{16,32},{32,48},{48,64},{64,80},{80,96},{96,112},{112,128},... | collective-permute-start | bytes 786440 | tf_op jit(solution)/shard_map/while/body/eval_jaxpr/ppermute | solution.py:14
  312.3 6.4 %collective-permute-start = (bf16[1,1024,128]{2,1,0:T(8,128)(2,1)S(1)}, bf16[1,1024,128]{2,1,0:T(8,128)(2,1)S(1)}, u32[]{:S(2)}, u32[]{:S(2)}) collective-permute-start(bf16[1,1024,128]{2,1,0:T(8,128)(2,1)S(1)} %get-tuple-element.627), channel_id=1, source_target_pairs={{1,0},{2,1},{3,2},{4,3},{5,4},{6,5},{7,6},{8,7},{9,8},{10,9},{11,1... | collective-permute-start | bytes 786440 | tf_op jit(solution)/shard_map/while/body/eval_jaxpr/ppermute | solution.py:17
  322.2 4.7 collective-permute-start.2
  338.8 6.4 %collective-permute-start = (bf16[1,1024,128]{2,1,0:T(8,128)(2,1)S(1)}, bf16[1,1024,128]{2,1,0:T(8,128)(2,1)S(1)}, u32[]{:S(2)}, u32[]{:S(2)}) collective-permute-start(bf16[1,1024,128]{2,1,0:T(8,128)(2,1)S(1)} %get-tuple-element.627), channel_id=1, source_target_pairs={{1,0},{2,1},{3,2},{4,3},{5,4},{6,5},{7,6},{8,7},{9,8},{10,9},{11,1... | collective-permute-start | bytes 786440 | tf_op jit(solution)/shard_map/while/body/eval_jaxpr/ppermute | solution.py:17
  348.6 4.6 collective-permute-start.2
  365.2 6.4 %collective-permute-start = (bf16[1,1024,128]{2,1,0:T(8,128)(2,1)S(1)}, bf16[1,1024,128]{2,1,0:T(8,128)(2,1)S(1)}, u32[]{:S(2)}, u32[]{:S(2)}) collective-permute-start(bf16[1,1024,128]{2,1,0:T(8,128)(2,1)S(1)} %get-tuple-element.627), channel_id=1, source_target_pairs={{1,0},{2,1},{3,2},{4,3},{5,4},{6,5},{7,6},{8,7},{9,8},{10,9},{11,1... | collective-permute-start | bytes 786440 | tf_op jit(solution)/shard_map/while/body/eval_jaxpr/ppermute | solution.py:17
  375.0 4.7 collective-permute-start.2
  391.6 6.4 %collective-permute-start = (bf16[1,1024,128]{2,1,0:T(8,128)(2,1)S(1)}, bf16[1,1024,128]{2,1,0:T(8,128)(2,1)S(1)}, u32[]{:S(2)}, u32[]{:S(2)}) collective-permute-start(bf16[1,1024,128]{2,1,0:T(8,128)(2,1)S(1)} %get-tuple-element.627), channel_id=1, source_target_pairs={{1,0},{2,1},{3,2},{4,3},{5,4},{6,5},{7,6},{8,7},{9,8},{10,9},{11,1... | collective-permute-start | bytes 786440 | tf_op jit(solution)/shard_map/while/body/eval_jaxpr/ppermute | solution.py:17
  401.5 4.6 collective-permute-start.2
  413.8 114.3 %psum.7 = f32[1024]{0:T(1024)} all-reduce(f32[1024]{0:T(1024)S(1)} %get-tuple-element.425), channel_id=1, replica_groups=mesh['seg'=32,'sec'=16] {'seg','sec'}, use_global_device_ids=true, to_apply=%region_9.10 | all-reduce | flops 1024 | bytes 8192 | tf_op jit(solution)/shard_map/psum | solution.py:123
  (364 shorter events, 309.7 us)
Async XLA Ops:
  4.2 8.0 %collective-permute-start = (bf16[1,1024,128]{2,1,0:T(8,128)(2,1)S(1)}, bf16[1,1024,128]{2,1,0:T(8,128)(2,1)S(1)}, u32[]{:S(2)}, u32[]{:S(2)}) collective-permute-start(bf16[1,1024,128]{2,1,0:T(8,128)(2,1)S(1)} %get-tuple-element.627), channel_id=1, source_target_pairs={{1,0},{2,1},{3,2},{4,3},{5,4},{6,5},{7,6},{8,7},{9,8},{10,9},{11,1... | collective-permute-start | bytes 786440 | tf_op jit(solution)/shard_map/while/body/eval_jaxpr/ppermute | solution.py:17
  30.1 8.6 %collective-permute-start = (bf16[1,1024,128]{2,1,0:T(8,128)(2,1)S(1)}, bf16[1,1024,128]{2,1,0:T(8,128)(2,1)S(1)}, u32[]{:S(2)}, u32[]{:S(2)}) collective-permute-start(bf16[1,1024,128]{2,1,0:T(8,128)(2,1)S(1)} %get-tuple-element.627), channel_id=1, source_target_pairs={{1,0},{2,1},{3,2},{4,3},{5,4},{6,5},{7,6},{8,7},{9,8},{10,9},{11,1... | collective-permute-start | bytes 786440 | tf_op jit(solution)/shard_map/while/body/eval_jaxpr/ppermute | solution.py:17
  55.8 8.0 %collective-permute-start = (bf16[1,1024,128]{2,1,0:T(8,128)(2,1)S(1)}, bf16[1,1024,128]{2,1,0:T(8,128)(2,1)S(1)}, u32[]{:S(2)}, u32[]{:S(2)}) collective-permute-start(bf16[1,1024,128]{2,1,0:T(8,128)(2,1)S(1)} %get-tuple-element.627), channel_id=1, source_target_pairs={{1,0},{2,1},{3,2},{4,3},{5,4},{6,5},{7,6},{8,7},{9,8},{10,9},{11,1... | collective-permute-start | bytes 786440 | tf_op jit(solution)/shard_map/while/body/eval_jaxpr/ppermute | solution.py:17
  65.8 7.7 %collective-permute-start.2 = (bf16[1,1024,128]{2,1,0:T(8,128)(2,1)S(1)}, bf16[1,1024,128]{2,1,0:T(8,128)(2,1)S(1)}, u32[]{:S(2)}, u32[]{:S(2)}) collective-permute-start(bf16[1,1024,128]{2,1,0:T(8,128)(2,1)S(1)} %bitcast.59), channel_id=1, source_target_pairs={{0,16},{16,32},{32,48},{48,64},{64,80},{80,96},{96,112},{112,128},... | collective-permute-start | bytes 786440 | tf_op jit(solution)/shard_map/while/body/eval_jaxpr/ppermute | solution.py:14
  82.1 7.8 %collective-permute-start = (bf16[1,1024,128]{2,1,0:T(8,128)(2,1)S(1)}, bf16[1,1024,128]{2,1,0:T(8,128)(2,1)S(1)}, u32[]{:S(2)}, u32[]{:S(2)}) collective-permute-start(bf16[1,1024,128]{2,1,0:T(8,128)(2,1)S(1)} %get-tuple-element.627), channel_id=1, source_target_pairs={{1,0},{2,1},{3,2},{4,3},{5,4},{6,5},{7,6},{8,7},{9,8},{10,9},{11,1... | collective-permute-start | bytes 786440 | tf_op jit(solution)/shard_map/while/body/eval_jaxpr/ppermute | solution.py:17
  96.0 7.4 %collective-permute-start.3 = (bf16[1,1024,128]{2,1,0:T(8,128)(2,1)S(1)}, bf16[1,1024,128]{2,1,0:T(8,128)(2,1)S(1)}, u32[]{:S(2)}, u32[]{:S(2)}) collective-permute-start(bf16[1,1024,128]{2,1,0:T(8,128)(2,1)S(1)} %bitcast.60), channel_id=1, source_target_pairs={{16,0},{32,16},{48,32},{64,48},{80,64},{96,80},{112,96},{128,112},... | collective-permute-start | bytes 786440 | tf_op jit(solution)/shard_map/while/body/eval_jaxpr/ppermute | solution.py:17
  107.9 7.7 %collective-permute-start = (bf16[1,1024,128]{2,1,0:T(8,128)(2,1)S(1)}, bf16[1,1024,128]{2,1,0:T(8,128)(2,1)S(1)}, u32[]{:S(2)}, u32[]{:S(2)}) collective-permute-start(bf16[1,1024,128]{2,1,0:T(8,128)(2,1)S(1)} %get-tuple-element.627), channel_id=1, source_target_pairs={{1,0},{2,1},{3,2},{4,3},{5,4},{6,5},{7,6},{8,7},{9,8},{10,9},{11,1... | collective-permute-start | bytes 786440 | tf_op jit(solution)/shard_map/while/body/eval_jaxpr/ppermute | solution.py:17
  133.2 7.9 %collective-permute-start = (bf16[1,1024,128]{2,1,0:T(8,128)(2,1)S(1)}, bf16[1,1024,128]{2,1,0:T(8,128)(2,1)S(1)}, u32[]{:S(2)}, u32[]{:S(2)}) collective-permute-start(bf16[1,1024,128]{2,1,0:T(8,128)(2,1)S(1)} %get-tuple-element.627), channel_id=1, source_target_pairs={{1,0},{2,1},{3,2},{4,3},{5,4},{6,5},{7,6},{8,7},{9,8},{10,9},{11,1... | collective-permute-start | bytes 786440 | tf_op jit(solution)/shard_map/while/body/eval_jaxpr/ppermute | solution.py:17
  158.5 7.8 %collective-permute-start = (bf16[1,1024,128]{2,1,0:T(8,128)(2,1)S(1)}, bf16[1,1024,128]{2,1,0:T(8,128)(2,1)S(1)}, u32[]{:S(2)}, u32[]{:S(2)}) collective-permute-start(bf16[1,1024,128]{2,1,0:T(8,128)(2,1)S(1)} %get-tuple-element.627), channel_id=1, source_target_pairs={{1,0},{2,1},{3,2},{4,3},{5,4},{6,5},{7,6},{8,7},{9,8},{10,9},{11,1... | collective-permute-start | bytes 786440 | tf_op jit(solution)/shard_map/while/body/eval_jaxpr/ppermute | solution.py:17
  183.7 7.8 %collective-permute-start = (bf16[1,1024,128]{2,1,0:T(8,128)(2,1)S(1)}, bf16[1,1024,128]{2,1,0:T(8,128)(2,1)S(1)}, u32[]{:S(2)}, u32[]{:S(2)}) collective-permute-start(bf16[1,1024,128]{2,1,0:T(8,128)(2,1)S(1)} %get-tuple-element.627), channel_id=1, source_target_pairs={{1,0},{2,1},{3,2},{4,3},{5,4},{6,5},{7,6},{8,7},{9,8},{10,9},{11,1... | collective-permute-start | bytes 786440 | tf_op jit(solution)/shard_map/while/body/eval_jaxpr/ppermute | solution.py:17
  208.9 7.7 %collective-permute-start = (bf16[1,1024,128]{2,1,0:T(8,128)(2,1)S(1)}, bf16[1,1024,128]{2,1,0:T(8,128)(2,1)S(1)}, u32[]{:S(2)}, u32[]{:S(2)}) collective-permute-start(bf16[1,1024,128]{2,1,0:T(8,128)(2,1)S(1)} %get-tuple-element.627), channel_id=1, source_target_pairs={{1,0},{2,1},{3,2},{4,3},{5,4},{6,5},{7,6},{8,7},{9,8},{10,9},{11,1... | collective-permute-start | bytes 786440 | tf_op jit(solution)/shard_map/while/body/eval_jaxpr/ppermute | solution.py:17
  234.1 7.7 %collective-permute-start = (bf16[1,1024,128]{2,1,0:T(8,128)(2,1)S(1)}, bf16[1,1024,128]{2,1,0:T(8,128)(2,1)S(1)}, u32[]{:S(2)}, u32[]{:S(2)}) collective-permute-start(bf16[1,1024,128]{2,1,0:T(8,128)(2,1)S(1)} %get-tuple-element.627), channel_id=1, source_target_pairs={{1,0},{2,1},{3,2},{4,3},{5,4},{6,5},{7,6},{8,7},{9,8},{10,9},{11,1... | collective-permute-start | bytes 786440 | tf_op jit(solution)/shard_map/while/body/eval_jaxpr/ppermute | solution.py:17
  259.2 7.7 %collective-permute-start = (bf16[1,1024,128]{2,1,0:T(8,128)(2,1)S(1)}, bf16[1,1024,128]{2,1,0:T(8,128)(2,1)S(1)}, u32[]{:S(2)}, u32[]{:S(2)}) collective-permute-start(bf16[1,1024,128]{2,1,0:T(8,128)(2,1)S(1)} %get-tuple-element.627), channel_id=1, source_target_pairs={{1,0},{2,1},{3,2},{4,3},{5,4},{6,5},{7,6},{8,7},{9,8},{10,9},{11,1... | collective-permute-start | bytes 786440 | tf_op jit(solution)/shard_map/while/body/eval_jaxpr/ppermute | solution.py:17
  272.6 7.7 %collective-permute-start.3 = (bf16[1,1024,128]{2,1,0:T(8,128)(2,1)S(1)}, bf16[1,1024,128]{2,1,0:T(8,128)(2,1)S(1)}, u32[]{:S(2)}, u32[]{:S(2)}) collective-permute-start(bf16[1,1024,128]{2,1,0:T(8,128)(2,1)S(1)} %bitcast.60), channel_id=1, source_target_pairs={{16,0},{32,16},{48,32},{64,48},{80,64},{96,80},{112,96},{128,112},... | collective-permute-start | bytes 786440 | tf_op jit(solution)/shard_map/while/body/eval_jaxpr/ppermute | solution.py:17
  284.8 7.7 %collective-permute-start = (bf16[1,1024,128]{2,1,0:T(8,128)(2,1)S(1)}, bf16[1,1024,128]{2,1,0:T(8,128)(2,1)S(1)}, u32[]{:S(2)}, u32[]{:S(2)}) collective-permute-start(bf16[1,1024,128]{2,1,0:T(8,128)(2,1)S(1)} %get-tuple-element.627), channel_id=1, source_target_pairs={{1,0},{2,1},{3,2},{4,3},{5,4},{6,5},{7,6},{8,7},{9,8},{10,9},{11,1... | collective-permute-start | bytes 786440 | tf_op jit(solution)/shard_map/while/body/eval_jaxpr/ppermute | solution.py:17
  294.4 9.3 %collective-permute-start.2 = (bf16[1,1024,128]{2,1,0:T(8,128)(2,1)S(1)}, bf16[1,1024,128]{2,1,0:T(8,128)(2,1)S(1)}, u32[]{:S(2)}, u32[]{:S(2)}) collective-permute-start(bf16[1,1024,128]{2,1,0:T(8,128)(2,1)S(1)} %bitcast.59), channel_id=1, source_target_pairs={{0,16},{16,32},{32,48},{48,64},{64,80},{80,96},{96,112},{112,128},... | collective-permute-start | bytes 786440 | tf_op jit(solution)/shard_map/while/body/eval_jaxpr/ppermute | solution.py:14
  312.3 7.7 %collective-permute-start = (bf16[1,1024,128]{2,1,0:T(8,128)(2,1)S(1)}, bf16[1,1024,128]{2,1,0:T(8,128)(2,1)S(1)}, u32[]{:S(2)}, u32[]{:S(2)}) collective-permute-start(bf16[1,1024,128]{2,1,0:T(8,128)(2,1)S(1)} %get-tuple-element.627), channel_id=1, source_target_pairs={{1,0},{2,1},{3,2},{4,3},{5,4},{6,5},{7,6},{8,7},{9,8},{10,9},{11,1... | collective-permute-start | bytes 786440 | tf_op jit(solution)/shard_map/while/body/eval_jaxpr/ppermute | solution.py:17
  322.2 8.0 %collective-permute-start.2 = (bf16[1,1024,128]{2,1,0:T(8,128)(2,1)S(1)}, bf16[1,1024,128]{2,1,0:T(8,128)(2,1)S(1)}, u32[]{:S(2)}, u32[]{:S(2)}) collective-permute-start(bf16[1,1024,128]{2,1,0:T(8,128)(2,1)S(1)} %bitcast.59), channel_id=1, source_target_pairs={{0,16},{16,32},{32,48},{48,64},{64,80},{80,96},{96,112},{112,128},... | collective-permute-start | bytes 786440 | tf_op jit(solution)/shard_map/while/body/eval_jaxpr/ppermute | solution.py:14
  338.8 7.7 %collective-permute-start = (bf16[1,1024,128]{2,1,0:T(8,128)(2,1)S(1)}, bf16[1,1024,128]{2,1,0:T(8,128)(2,1)S(1)}, u32[]{:S(2)}, u32[]{:S(2)}) collective-permute-start(bf16[1,1024,128]{2,1,0:T(8,128)(2,1)S(1)} %get-tuple-element.627), channel_id=1, source_target_pairs={{1,0},{2,1},{3,2},{4,3},{5,4},{6,5},{7,6},{8,7},{9,8},{10,9},{11,1... | collective-permute-start | bytes 786440 | tf_op jit(solution)/shard_map/while/body/eval_jaxpr/ppermute | solution.py:17
  348.6 7.9 %collective-permute-start.2 = (bf16[1,1024,128]{2,1,0:T(8,128)(2,1)S(1)}, bf16[1,1024,128]{2,1,0:T(8,128)(2,1)S(1)}, u32[]{:S(2)}, u32[]{:S(2)}) collective-permute-start(bf16[1,1024,128]{2,1,0:T(8,128)(2,1)S(1)} %bitcast.59), channel_id=1, source_target_pairs={{0,16},{16,32},{32,48},{48,64},{64,80},{80,96},{96,112},{112,128},... | collective-permute-start | bytes 786440 | tf_op jit(solution)/shard_map/while/body/eval_jaxpr/ppermute | solution.py:14
  365.2 7.7 %collective-permute-start = (bf16[1,1024,128]{2,1,0:T(8,128)(2,1)S(1)}, bf16[1,1024,128]{2,1,0:T(8,128)(2,1)S(1)}, u32[]{:S(2)}, u32[]{:S(2)}) collective-permute-start(bf16[1,1024,128]{2,1,0:T(8,128)(2,1)S(1)} %get-tuple-element.627), channel_id=1, source_target_pairs={{1,0},{2,1},{3,2},{4,3},{5,4},{6,5},{7,6},{8,7},{9,8},{10,9},{11,1... | collective-permute-start | bytes 786440 | tf_op jit(solution)/shard_map/while/body/eval_jaxpr/ppermute | solution.py:17
  375.0 7.9 %collective-permute-start.2 = (bf16[1,1024,128]{2,1,0:T(8,128)(2,1)S(1)}, bf16[1,1024,128]{2,1,0:T(8,128)(2,1)S(1)}, u32[]{:S(2)}, u32[]{:S(2)}) collective-permute-start(bf16[1,1024,128]{2,1,0:T(8,128)(2,1)S(1)} %bitcast.59), channel_id=1, source_target_pairs={{0,16},{16,32},{32,48},{48,64},{64,80},{80,96},{96,112},{112,128},... | collective-permute-start | bytes 786440 | tf_op jit(solution)/shard_map/while/body/eval_jaxpr/ppermute | solution.py:14
  391.6 7.7 %collective-permute-start = (bf16[1,1024,128]{2,1,0:T(8,128)(2,1)S(1)}, bf16[1,1024,128]{2,1,0:T(8,128)(2,1)S(1)}, u32[]{:S(2)}, u32[]{:S(2)}) collective-permute-start(bf16[1,1024,128]{2,1,0:T(8,128)(2,1)S(1)} %get-tuple-element.627), channel_id=1, source_target_pairs={{1,0},{2,1},{3,2},{4,3},{5,4},{6,5},{7,6},{8,7},{9,8},{10,9},{11,1... | collective-permute-start | bytes 786440 | tf_op jit(solution)/shard_map/while/body/eval_jaxpr/ppermute | solution.py:17
  401.5 7.9 %collective-permute-start.2 = (bf16[1,1024,128]{2,1,0:T(8,128)(2,1)S(1)}, bf16[1,1024,128]{2,1,0:T(8,128)(2,1)S(1)}, u32[]{:S(2)}, u32[]{:S(2)}) collective-permute-start(bf16[1,1024,128]{2,1,0:T(8,128)(2,1)S(1)} %bitcast.59), channel_id=1, source_target_pairs={{0,16},{16,32},{32,48},{48,64},{64,80},{80,96},{96,112},{112,128},... | collective-permute-start | bytes 786440 | tf_op jit(solution)/shard_map/while/body/eval_jaxpr/ppermute | solution.py:14
  (40 other events, 224.7 us)
where the time goes:
time: 531 us; the launch traced here: 528 us
  starting transfers between devices  188 us (35%)
  waiting for transfers between devices  150 us (28%)
  blocking collectives  114 us (21%)
  other arithmetic  45.8 us (9%)
  matrix products  26 us (5%)
    ppermute x32, starting transfers between devices, padded_2(): lax.ppermute(lax.slice_in_dim(block, 0, width, axis=dim), axis, backward)  124 us
    psum x1, blocking collectives, per_device(): return lax.psum(final_state[1], ('seg', 'sec'))  114 us
    ppermute x32, waiting for transfers between devices, padded_2(): lax.ppermute(lax.slice_in_dim(block, 0, width, axis=dim), axis, backward)  86.9 us
    ppermute x32, starting transfers between devices, padded_2(): lax.ppermute(lax.slice_in_dim(block, block.shape[dim] - width, None, axis...  64.2 us
    ppermute x32, waiting for transfers between devices, padded_2(): lax.ppermute(lax.slice_in_dim(block, block.shape[dim] - width, None, axis...  63 us
    dot_general x16, matrix products, forward_send(): jnp.einsum('ka,nab->knb', vector, block_site, preferred_element_type=jnp....  26 us
    select_n x16, other arithmetic, section(): vector = jnp.where(is_first, initial(), incoming)  14 us
    convert_element_type x16, other arithmetic, state_masks(): return (occ_site[:, None] == levels[None, :]).astype(jnp.float32)  11.1 us
  transfers between devices with their start and end apart: 64, of which 64 were waited for; matrix products, arithmetic and copies ran while one was open for 0% of the time, Pallas kernels for 0%

commit v1 on v0

v1 whole, which is shorter than its diff:
```python
import jax
import jax.numpy as jnp
from jax import lax
from jax.sharding import PartitionSpec as P


def per_device(blocks, left_edge, right_edge, occupation, start_sector):
    seg_count = lax.axis_size("seg")
    sec_count = lax.axis_size("sec")
    half_count = seg_count // 2
    seg_index = lax.axis_index("seg")
    sec_index = lax.axis_index("sec")
    is_left = seg_index < half_count
    depth = jnp.where(is_left, seg_index, seg_count - 1 - seg_index)

    conf_count = occupation.shape[0]
    sites = seg_count * occupation.shape[1]
    group = conf_count // sec_count
    width = blocks.shape[-1]
    local_states = blocks.shape[1]

    site_blocks = lax.all_gather(blocks[0], "sec", axis=1, tiled=True)
    nsec = site_blocks.shape[1]
    lefts = lax.all_gather(left_edge, "sec", axis=0, tiled=True)
    rights = lax.all_gather(right_edge, "sec", axis=0, tiled=True)

    row0 = sec_index * group
    occ_mine = lax.dynamic_slice_in_dim(occupation, row0, group, axis=0)
    occ_group = lax.all_gather(occ_mine, "seg", axis=1, tiled=True)
    start_group = lax.dynamic_slice_in_dim(start_sector, row0, group, axis=0)

    charge = jnp.array([0, 1, -1, 0], dtype=jnp.int32)
    steps = charge[occ_group]
    site_ids = jnp.arange(sites, dtype=jnp.int32)
    before = jnp.sum(jnp.where(site_ids[None, :] < seg_index, steps, 0), axis=1)
    total = jnp.sum(steps, axis=1)
    sector_here = jnp.mod(start_group + before, nsec)
    sector_end = jnp.mod(start_group + total, nsec)
    occ_here = occ_mine[:, 0]

    sector_hot = (sector_here[:, None] == jnp.arange(nsec, dtype=jnp.int32)[None, :]).astype(
        jnp.bfloat16
    )
    state_hot = (occ_here[:, None] == jnp.arange(local_states, dtype=jnp.int32)[None, :]).astype(
        jnp.float32
    )

    oriented = lax.cond(
        is_left,
        lambda b: b,
        lambda b: jnp.swapaxes(b, 2, 3),
        site_blocks,
    )

    def apply(vector):
        spread = vector[:, None, :] * sector_hot[:, :, None]
        products = jnp.einsum(
            "kqa,nqab->knb", spread, oriented, preferred_element_type=jnp.float32
        )
        return jnp.sum(products * state_hot[:, :, None], axis=1).astype(jnp.bfloat16)

    first_left = jnp.take(lefts, start_group, axis=0)
    first_right = jnp.take(rights, sector_end, axis=0)
    first = jnp.where(is_left, first_left, first_right)
    vector = jnp.where(depth == 0, first, jnp.zeros_like(first))

    chain = [(j, j + 1) for j in range(half_count - 1)] + [
        (j, j - 1) for j in range(half_count + 1, seg_count)
    ]
    for step in range(half_count):
        vector = apply(vector)
        if step < half_count - 1:
            vector = lax.ppermute(vector, "seg", chain)

    meet = [(half_count - 1, half_count), (half_count, half_count - 1)]
    other = lax.ppermute(vector, "seg", meet)
    amp = jnp.sum(vector.astype(jnp.float32) * other.astype(jnp.float32), axis=1)
    amp = jnp.where(seg_index == half_count - 1, amp, jnp.zeros_like(amp))
    gathered = lax.all_gather(amp, "sec", axis=0, tiled=True)
    return lax.psum(gathered, "seg")


def solution(mesh):
    in_specs = (
        P("seg", None, "sec", None, None),
        P("sec", None),
        P("sec", None),
        P(None, "seg"),
        P(),
    )
    out_specs = P()
    return jax.shard_map(
        per_device, mesh=mesh, in_specs=in_specs, out_specs=out_specs, check_vma=False
    )
```

time: 531 us -> 320 us (0.60)
  the two profiles are of different devices: /device:TPU:1 before, /device:TPU:32 now
where the time goes in v1:
time: 320 us; the launch traced here: 318 us
  blocking collectives  168 us (52%)
  waiting for transfers between devices  89.3 us (28%)
  starting transfers between devices  23.7 us (7%)
  between operations  14.4 us (4%)
  matrix products  12.1 us (4%)
  local copies, waits for them, and re-layouts  7.99 us (2%)
    ppermute x15, waiting for transfers between devices, per_device(): vector = lax.ppermute(vector, 'seg', chain)  86.5 us
    psum x1, blocking collectives, per_device(): return lax.psum(gathered, 'seg')  72.6 us
    all_gather x1, blocking collectives, per_device(): occ_group = lax.all_gather(occ_mine, 'seg', axis=1, tiled=True)  34.2 us
    unnamed x1, blocking collectives  23.5 us
    all_gather x1, blocking collectives, per_device(): rights = lax.all_gather(right_edge, 'sec', axis=0, tiled=True)  23.3 us
    ppermute x15, starting transfers between devices, per_device(): vector = lax.ppermute(vector, 'seg', chain)  19.4 us
    all_gather x1, blocking collectives, per_device(): lefts = lax.all_gather(left_edge, 'sec', axis=0, tiled=True)  14.6 us
    dot_general x16, matrix products, apply(): jnp.einsum('kqa,nqab->knb', spread, oriented, preferred_element_type=jnp....  12.1 us
  transfers between devices with their start and end apart: 17, of which 16 were waited for; matrix products, arithmetic and copies ran while one was open for 2% of the time, Pallas kernels for 0%

profile of v1, /device:TPU:32, one launch (start us, length us, event | category | flops | bytes accessed | tf_op | source)
XLA Modules:
  0.0 317.6 jit_solution(7298248449602463857)
XLA Ops:
  8.2 23.3 %all-gather.2 = bf16[16,1,128]{2,1,0:T(2,128)(2,1)S(1)} all-gather(bf16[1,1,128]{2,1,0:T(2,128)(2,1)} %bitcast.200), channel_id=1, replica_groups=mesh['seg'=32,'sec'=16] {'sec'}, dimensions={0}, use_global_device_ids=true | all-gather | bytes 4352 | tf_op jit(solution)/shard_map/all_gather | solution.py:25
  31.6 14.6 %all-gather.1 = bf16[16,1,128]{2,1,0:T(2,128)(2,1)S(1)} all-gather(bf16[1,1,128]{2,1,0:T(2,128)(2,1)} %bitcast.201), channel_id=1, replica_groups=mesh['seg'=32,'sec'=16] {'sec'}, dimensions={0}, use_global_device_ids=true | all-gather | bytes 4352 | tf_op jit(solution)/shard_map/all_gather | solution.py:24
  46.9 34.2 %all-gather.3 = s32[32,1,64]{2,1,0:T(1,128)S(1)} all-gather(s32[1,1,64]{2,1,0:T(1,128)S(1)} %get-tuple-element.18), channel_id=1, replica_groups=mesh['seg'=32,'sec'=16] {'seg'}, dimensions={0}, use_global_device_ids=true | all-gather | bytes 8448 | tf_op jit(solution)/shard_map/all_gather | solution.py:29
  84.2 3.1 conditional.1
  84.2 3.1 copy.34
  89.3 4.3 %collective-permute-done = bf16[64,128]{1,0:T(8,128)(2,1)S(1)} collective-permute-done((bf16[64,128]{1,0:T(8,128)(2,1)S(1)}, bf16[64,128]{1,0:T(8,128)(2,1)S(1)}, u32[]{:S(2)}, u32[]{:S(2)}) %collective-permute-start) | collective-permute-done | bytes 16416 | tf_op jit(solution)/shard_map/ppermute | solution.py:73
  95.7 4.3 %collective-permute-done.1 = bf16[64,128]{1,0:T(8,128)(2,1)S(1)} collective-permute-done((bf16[64,128]{1,0:T(8,128)(2,1)S(1)}, bf16[64,128]{1,0:T(8,128)(2,1)S(1)}, u32[]{:S(2)}, u32[]{:S(2)}) %collective-permute-start.1) | collective-permute-done | bytes 16416 | tf_op jit(solution)/shard_map/ppermute | solution.py:73
  102.1 4.3 %collective-permute-done.2 = bf16[64,128]{1,0:T(8,128)(2,1)S(1)} collective-permute-done((bf16[64,128]{1,0:T(8,128)(2,1)S(1)}, bf16[64,128]{1,0:T(8,128)(2,1)S(1)}, u32[]{:S(2)}, u32[]{:S(2)}) %collective-permute-start.2) | collective-permute-done | bytes 16416 | tf_op jit(solution)/shard_map/ppermute | solution.py:73
  108.5 4.3 %collective-permute-done.3 = bf16[64,128]{1,0:T(8,128)(2,1)S(1)} collective-permute-done((bf16[64,128]{1,0:T(8,128)(2,1)S(1)}, bf16[64,128]{1,0:T(8,128)(2,1)S(1)}, u32[]{:S(2)}, u32[]{:S(2)}) %collective-permute-start.3) | collective-permute-done | bytes 16416 | tf_op jit(solution)/shard_map/ppermute | solution.py:73
  114.9 4.8 %collective-permute-done.4 = bf16[64,128]{1,0:T(8,128)(2,1)S(1)} collective-permute-done((bf16[64,128]{1,0:T(8,128)(2,1)S(1)}, bf16[64,128]{1,0:T(8,128)(2,1)S(1)}, u32[]{:S(2)}, u32[]{:S(2)}) %collective-permute-start.4) | collective-permute-done | bytes 16416 | tf_op jit(solution)/shard_map/ppermute | solution.py:73
  121.7 6.4 %collective-permute-done.5 = bf16[64,128]{1,0:T(8,128)(2,1)S(1)} collective-permute-done((bf16[64,128]{1,0:T(8,128)(2,1)S(1)}, bf16[64,128]{1,0:T(8,128)(2,1)S(1)}, u32[]{:S(2)}, u32[]{:S(2)}) %collective-permute-start.5) | collective-permute-done | bytes 16416 | tf_op jit(solution)/shard_map/ppermute | solution.py:73
  130.2 6.4 %collective-permute-done.6 = bf16[64,128]{1,0:T(8,128)(2,1)S(1)} collective-permute-done((bf16[64,128]{1,0:T(8,128)(2,1)S(1)}, bf16[64,128]{1,0:T(8,128)(2,1)S(1)}, u32[]{:S(2)}, u32[]{:S(2)}) %collective-permute-start.6) | collective-permute-done | bytes 16416 | tf_op jit(solution)/shard_map/ppermute | solution.py:73
  138.7 6.4 %collective-permute-done.7 = bf16[64,128]{1,0:T(8,128)(2,1)S(1)} collective-permute-done((bf16[64,128]{1,0:T(8,128)(2,1)S(1)}, bf16[64,128]{1,0:T(8,128)(2,1)S(1)}, u32[]{:S(2)}, u32[]{:S(2)}) %collective-permute-start.7) | collective-permute-done | bytes 16416 | tf_op jit(solution)/shard_map/ppermute | solution.py:73
  147.2 6.5 %collective-permute-done.8 = bf16[64,128]{1,0:T(8,128)(2,1)S(1)} collective-permute-done((bf16[64,128]{1,0:T(8,128)(2,1)S(1)}, bf16[64,128]{1,0:T(8,128)(2,1)S(1)}, u32[]{:S(2)}, u32[]{:S(2)}) %collective-permute-start.8) | collective-permute-done | bytes 16416 | tf_op jit(solution)/shard_map/ppermute | solution.py:73
  155.8 6.3 %collective-permute-done.9 = bf16[64,128]{1,0:T(8,128)(2,1)S(1)} collective-permute-done((bf16[64,128]{1,0:T(8,128)(2,1)S(1)}, bf16[64,128]{1,0:T(8,128)(2,1)S(1)}, u32[]{:S(2)}, u32[]{:S(2)}) %collective-permute-start.9) | collective-permute-done | bytes 16416 | tf_op jit(solution)/shard_map/ppermute | solution.py:73
  164.2 6.4 %collective-permute-done.10 = bf16[64,128]{1,0:T(8,128)(2,1)S(1)} collective-permute-done((bf16[64,128]{1,0:T(8,128)(2,1)S(1)}, bf16[64,128]{1,0:T(8,128)(2,1)S(1)}, u32[]{:S(2)}, u32[]{:S(2)}) %collective-permute-start.10) | collective-permute-done | bytes 16416 | tf_op jit(solution)/shard_map/ppermute | solution.py:73
  172.7 6.4 %collective-permute-done.11 = bf16[64,128]{1,0:T(8,128)(2,1)S(1)} collective-permute-done((bf16[64,128]{1,0:T(8,128)(2,1)S(1)}, bf16[64,128]{1,0:T(8,128)(2,1)S(1)}, u32[]{:S(2)}, u32[]{:S(2)}) %collective-permute-start.11) | collective-permute-done | bytes 16416 | tf_op jit(solution)/shard_map/ppermute | solution.py:73
  181.2 6.4 %collective-permute-done.12 = bf16[64,128]{1,0:T(8,128)(2,1)S(1)} collective-permute-done((bf16[64,128]{1,0:T(8,128)(2,1)S(1)}, bf16[64,128]{1,0:T(8,128)(2,1)S(1)}, u32[]{:S(2)}, u32[]{:S(2)}) %collective-permute-start.12) | collective-permute-done | bytes 16416 | tf_op jit(solution)/shard_map/ppermute | solution.py:73
  189.7 6.4 %collective-permute-done.13 = bf16[64,128]{1,0:T(8,128)(2,1)S(1)} collective-permute-done((bf16[64,128]{1,0:T(8,128)(2,1)S(1)}, bf16[64,128]{1,0:T(8,128)(2,1)S(1)}, u32[]{:S(2)}, u32[]{:S(2)}) %collective-permute-start.13) | collective-permute-done | bytes 16416 | tf_op jit(solution)/shard_map/ppermute | solution.py:73
  198.2 6.4 %collective-permute-done.14 = bf16[64,128]{1,0:T(8,128)(2,1)S(1)} collective-permute-done((bf16[64,128]{1,0:T(8,128)(2,1)S(1)}, bf16[64,128]{1,0:T(8,128)(2,1)S(1)}, u32[]{:S(2)}, u32[]{:S(2)}) %collective-permute-start.14) | collective-permute-done | bytes 16416 | tf_op jit(solution)/shard_map/ppermute | solution.py:73
  205.4 4.3 %collective-permute-start.15 = (bf16[64,128]{1,0:T(8,128)(2,1)S(1)}, bf16[64,128]{1,0:T(8,128)(2,1)S(1)}, u32[]{:S(2)}, u32[]{:S(2)}) collective-permute-start(bf16[64,128]{1,0:T(8,128)(2,1)S(1)} %fusion.16), channel_id=1, source_target_pairs={{240,256},{256,240},{241,257},{257,241},{242,258},{258,242},{243,2... | collective-permute-start | bytes 49160 | tf_op jit(solution)/shard_map/ppermute | solution.py:76
  211.7 2.7 collective-permute-done.15
  214.6 23.5 %all-reduce = f32[1024]{0:T(1024)S(1)} all-reduce(f32[1024]{0:T(1024)S(1)} %fusion.100), channel_id=1, replica_groups=mesh['seg'=32,'sec'=16] {'sec'}, use_global_device_ids=true, to_apply=%add | all-reduce | flops 1024 | bytes 8192
  238.2 72.6 %psum.7 = f32[1024]{0:T(1024)} all-reduce(f32[1024]{0:T(1024)S(1)} %all-reduce), channel_id=1, replica_groups=mesh['seg'=32,'sec'=16] {'seg'}, use_global_device_ids=true, to_apply=%region_21.23 | all-reduce | flops 1024 | bytes 8192 | tf_op jit(solution)/shard_map/psum | solution.py:80
  (52 shorter events, 38.4 us)
Async XLA Ops:
  6.5 77.6 %all-gather.6.cloned.1.call-start = ((), (), s32[]{:S(2)}) async-start(), calls=%async_computation | async-start | bytes 2228224 | tf_op jit(solution)/shard_map/all_gather | solution.py:22
  88.0 5.6 %collective-permute-start = (bf16[64,128]{1,0:T(8,128)(2,1)S(1)}, bf16[64,128]{1,0:T(8,128)(2,1)S(1)}, u32[]{:S(2)}, u32[]{:S(2)}) collective-permute-start(bf16[64,128]{1,0:T(8,128)(2,1)S(1)} %fusion.31), channel_id=1, source_target_pairs={{0,16},{16,32},{32,48},{48,64},{64,80},{80,96},{96,112},{112,128},... | collective-permute-start | bytes 49160 | tf_op jit(solution)/shard_map/ppermute | solution.py:73
  94.4 5.6 %collective-permute-start.1 = (bf16[64,128]{1,0:T(8,128)(2,1)S(1)}, bf16[64,128]{1,0:T(8,128)(2,1)S(1)}, u32[]{:S(2)}, u32[]{:S(2)}) collective-permute-start(bf16[64,128]{1,0:T(8,128)(2,1)S(1)} %fusion.30), channel_id=1, source_target_pairs={{0,16},{16,32},{32,48},{48,64},{64,80},{80,96},{96,112},{112,128},... | collective-permute-start | bytes 49160 | tf_op jit(solution)/shard_map/ppermute | solution.py:73
  100.8 5.6 %collective-permute-start.2 = (bf16[64,128]{1,0:T(8,128)(2,1)S(1)}, bf16[64,128]{1,0:T(8,128)(2,1)S(1)}, u32[]{:S(2)}, u32[]{:S(2)}) collective-permute-start(bf16[64,128]{1,0:T(8,128)(2,1)S(1)} %fusion.29), channel_id=1, source_target_pairs={{0,16},{16,32},{32,48},{48,64},{64,80},{80,96},{96,112},{112,128},... | collective-permute-start | bytes 49160 | tf_op jit(solution)/shard_map/ppermute | solution.py:73
  107.2 5.6 %collective-permute-start.3 = (bf16[64,128]{1,0:T(8,128)(2,1)S(1)}, bf16[64,128]{1,0:T(8,128)(2,1)S(1)}, u32[]{:S(2)}, u32[]{:S(2)}) collective-permute-start(bf16[64,128]{1,0:T(8,128)(2,1)S(1)} %fusion.28), channel_id=1, source_target_pairs={{0,16},{16,32},{32,48},{48,64},{64,80},{80,96},{96,112},{112,128},... | collective-permute-start | bytes 49160 | tf_op jit(solution)/shard_map/ppermute | solution.py:73
  113.6 6.1 %collective-permute-start.4 = (bf16[64,128]{1,0:T(8,128)(2,1)S(1)}, bf16[64,128]{1,0:T(8,128)(2,1)S(1)}, u32[]{:S(2)}, u32[]{:S(2)}) collective-permute-start(bf16[64,128]{1,0:T(8,128)(2,1)S(1)} %fusion.27), channel_id=1, source_target_pairs={{0,16},{16,32},{32,48},{48,64},{64,80},{80,96},{96,112},{112,128},... | collective-permute-start | bytes 49160 | tf_op jit(solution)/shard_map/ppermute | solution.py:73
  120.4 7.7 %collective-permute-start.5 = (bf16[64,128]{1,0:T(8,128)(2,1)S(1)}, bf16[64,128]{1,0:T(8,128)(2,1)S(1)}, u32[]{:S(2)}, u32[]{:S(2)}) collective-permute-start(bf16[64,128]{1,0:T(8,128)(2,1)S(1)} %fusion.26), channel_id=1, source_target_pairs={{0,16},{16,32},{32,48},{48,64},{64,80},{80,96},{96,112},{112,128},... | collective-permute-start | bytes 49160 | tf_op jit(solution)/shard_map/ppermute | solution.py:73
  128.9 7.7 %collective-permute-start.6 = (bf16[64,128]{1,0:T(8,128)(2,1)S(1)}, bf16[64,128]{1,0:T(8,128)(2,1)S(1)}, u32[]{:S(2)}, u32[]{:S(2)}) collective-permute-start(bf16[64,128]{1,0:T(8,128)(2,1)S(1)} %fusion.25), channel_id=1, source_target_pairs={{0,16},{16,32},{32,48},{48,64},{64,80},{80,96},{96,112},{112,128},... | collective-permute-start | bytes 49160 | tf_op jit(solution)/shard_map/ppermute | solution.py:73
  137.4 7.7 %collective-permute-start.7 = (bf16[64,128]{1,0:T(8,128)(2,1)S(1)}, bf16[64,128]{1,0:T(8,128)(2,1)S(1)}, u32[]{:S(2)}, u32[]{:S(2)}) collective-permute-start(bf16[64,128]{1,0:T(8,128)(2,1)S(1)} %fusion.24), channel_id=1, source_target_pairs={{0,16},{16,32},{32,48},{48,64},{64,80},{80,96},{96,112},{112,128},... | collective-permute-start | bytes 49160 | tf_op jit(solution)/shard_map/ppermute | solution.py:73
  145.9 7.8 %collective-permute-start.8 = (bf16[64,128]{1,0:T(8,128)(2,1)S(1)}, bf16[64,128]{1,0:T(8,128)(2,1)S(1)}, u32[]{:S(2)}, u32[]{:S(2)}) collective-permute-start(bf16[64,128]{1,0:T(8,128)(2,1)S(1)} %fusion.23), channel_id=1, source_target_pairs={{0,16},{16,32},{32,48},{48,64},{64,80},{80,96},{96,112},{112,128},... | collective-permute-start | bytes 49160 | tf_op jit(solution)/shard_map/ppermute | solution.py:73
  154.5 7.6 %collective-permute-start.9 = (bf16[64,128]{1,0:T(8,128)(2,1)S(1)}, bf16[64,128]{1,0:T(8,128)(2,1)S(1)}, u32[]{:S(2)}, u32[]{:S(2)}) collective-permute-start(bf16[64,128]{1,0:T(8,128)(2,1)S(1)} %fusion.22), channel_id=1, source_target_pairs={{0,16},{16,32},{32,48},{48,64},{64,80},{80,96},{96,112},{112,128},... | collective-permute-start | bytes 49160 | tf_op jit(solution)/shard_map/ppermute | solution.py:73
  162.9 7.7 %collective-permute-start.10 = (bf16[64,128]{1,0:T(8,128)(2,1)S(1)}, bf16[64,128]{1,0:T(8,128)(2,1)S(1)}, u32[]{:S(2)}, u32[]{:S(2)}) collective-permute-start(bf16[64,128]{1,0:T(8,128)(2,1)S(1)} %fusion.21), channel_id=1, source_target_pairs={{0,16},{16,32},{32,48},{48,64},{64,80},{80,96},{96,112},{112,128},... | collective-permute-start | bytes 49160 | tf_op jit(solution)/shard_map/ppermute | solution.py:73
  171.4 7.7 %collective-permute-start.11 = (bf16[64,128]{1,0:T(8,128)(2,1)S(1)}, bf16[64,128]{1,0:T(8,128)(2,1)S(1)}, u32[]{:S(2)}, u32[]{:S(2)}) collective-permute-start(bf16[64,128]{1,0:T(8,128)(2,1)S(1)} %fusion.20), channel_id=1, source_target_pairs={{0,16},{16,32},{32,48},{48,64},{64,80},{80,96},{96,112},{112,128},... | collective-permute-start | bytes 49160 | tf_op jit(solution)/shard_map/ppermute | solution.py:73
  179.9 7.7 %collective-permute-start.12 = (bf16[64,128]{1,0:T(8,128)(2,1)S(1)}, bf16[64,128]{1,0:T(8,128)(2,1)S(1)}, u32[]{:S(2)}, u32[]{:S(2)}) collective-permute-start(bf16[64,128]{1,0:T(8,128)(2,1)S(1)} %fusion.19), channel_id=1, source_target_pairs={{0,16},{16,32},{32,48},{48,64},{64,80},{80,96},{96,112},{112,128},... | collective-permute-start | bytes 49160 | tf_op jit(solution)/shard_map/ppermute | solution.py:73
  188.4 7.7 %collective-permute-start.13 = (bf16[64,128]{1,0:T(8,128)(2,1)S(1)}, bf16[64,128]{1,0:T(8,128)(2,1)S(1)}, u32[]{:S(2)}, u32[]{:S(2)}) collective-permute-start(bf16[64,128]{1,0:T(8,128)(2,1)S(1)} %fusion.18), channel_id=1, source_target_pairs={{0,16},{16,32},{32,48},{48,64},{64,80},{80,96},{96,112},{112,128},... | collective-permute-start | bytes 49160 | tf_op jit(solution)/shard_map/ppermute | solution.py:73
  196.9 7.7 %collective-permute-start.14 = (bf16[64,128]{1,0:T(8,128)(2,1)S(1)}, bf16[64,128]{1,0:T(8,128)(2,1)S(1)}, u32[]{:S(2)}, u32[]{:S(2)}) collective-permute-start(bf16[64,128]{1,0:T(8,128)(2,1)S(1)} %fusion.17), channel_id=1, source_target_pairs={{0,16},{16,32},{32,48},{48,64},{64,80},{80,96},{96,112},{112,128},... | collective-permute-start | bytes 49160 | tf_op jit(solution)/shard_map/ppermute | solution.py:73
  205.4 9.0 %collective-permute-start.15 = (bf16[64,128]{1,0:T(8,128)(2,1)S(1)}, bf16[64,128]{1,0:T(8,128)(2,1)S(1)}, u32[]{:S(2)}, u32[]{:S(2)}) collective-permute-start(bf16[64,128]{1,0:T(8,128)(2,1)S(1)} %fusion.16), channel_id=1, source_target_pairs={{240,256},{256,240},{241,257},{257,241},{242,258},{258,242},{243,2... | collective-permute-start | bytes 49160 | tf_op jit(solution)/shard_map/ppermute | solution.py:76
Sparse Core Ops, SparseCore 0:
  9.5 47.2 all-gather.5

commit v2 on v1

--- a/solution.py
+++ b/solution.py
@@ -2,6 +2,14 @@
 import jax.numpy as jnp
 from jax import lax
 from jax.sharding import PartitionSpec as P
+
+
+def exchange_rounds(value, axis, partner_sets):
+    total = value
+    for pairs in partner_sets:
+        if pairs:
+            total = total + lax.ppermute(value, axis, pairs)
+    return total
 
 
 def per_device(blocks, left_edge, right_edge, occupation, start_sector):
@@ -19,10 +27,15 @@
     width = blocks.shape[-1]
     local_states = blocks.shape[1]
 
-    site_blocks = lax.all_gather(blocks[0], "sec", axis=1, tiled=True)
-    nsec = site_blocks.shape[1]
-    lefts = lax.all_gather(left_edge, "sec", axis=0, tiled=True)
-    rights = lax.all_gather(right_edge, "sec", axis=0, tiled=True)
+    rows = blocks[0, :, 0].reshape(local_states * width, width)
+    pad = jnp.zeros((14, width), blocks.dtype)
+    packed = jnp.concatenate([rows, left_edge, right_edge, pad], axis=0)
+    gathered = lax.all_gather(packed, "sec", axis=0, tiled=False)
+    nsec = gathered.shape[0]
+    body = local_states * width
+    site_blocks = gathered[:, :body].reshape(nsec, local_states, width, width)
+    lefts = gathered[:, body]
+    rights = gathered[:, body + 1]
 
     row0 = sec_index * group
     occ_mine = lax.dynamic_slice_in_dim(occupation, row0, group, axis=0)
@@ -55,7 +68,7 @@
     def apply(vector):
         spread = vector[:, None, :] * sector_hot[:, :, None]
         products = jnp.einsum(
-            "kqa,nqab->knb", spread, oriented, preferred_element_type=jnp.float32
+            "kqa,qnab->knb", spread, oriented, preferred_element_type=jnp.float32
         )
         return jnp.sum(products * state_hot[:, :, None], axis=1).astype(jnp.bfloat16)
 
@@ -72,12 +85,43 @@
         if step < half_count - 1:
             vector = lax.ppermute(vector, "seg", chain)
 
-    meet = [(half_count - 1, half_count), (half_count, half_count - 1)]
-    other = lax.ppermute(vector, "seg", meet)
+    low, high = half_count - 1, half_count
+    other = lax.ppermute(vector, "seg", [(low, high), (high, low)])
     amp = jnp.sum(vector.astype(jnp.float32) * other.astype(jnp.float32), axis=1)
-    amp = jnp.where(seg_index == half_count - 1, amp, jnp.zeros_like(amp))
-    gathered = lax.all_gather(amp, "sec", axis=0, tiled=True)
-    return lax.psum(gathered, "seg")
+    at_meet = (seg_index == low) | (seg_index == high)
+    amp = jnp.where(at_meet, amp, jnp.zeros_like(amp))
+
+    pieces = amp[None, :]
+    span = 1
+    while span < sec_count:
+        own_slot = (sec_index // span) % 4
+        parts = [pieces]
+        for t in (1, 2, 3):
+            pairs = [(i, i ^ (t * span)) for i in range(sec_count)]
+            parts.append(lax.ppermute(pieces, "sec", pairs))
+        slots = []
+        for r in range(4):
+            chosen = jnp.zeros_like(pieces)
+            for t in range(4):
+                chosen = chosen + jnp.where(own_slot ^ t == r, parts[t], jnp.zeros_like(pieces))
+            slots.append(chosen)
+        pieces = jnp.concatenate(slots, axis=0)
+        span *= 4
+    full = pieces.reshape(conf_count)
+
+    def outward(offset, holders):
+        pairs = []
+        for h in holders:
+            target = h - offset if h <= low else h + offset
+            if 0 <= target < seg_count:
+                pairs.append((h, target))
+        return pairs
+
+    holders = [low, high]
+    for offsets in ((1, 2, 3), (4, 8, 12)):
+        full = exchange_rounds(full, "seg", [outward(o, holders) for o in offsets])
+        holders = sorted(set(holders) | {t for o in offsets for _, t in outward(o, holders)})
+    return full
 
 
 def solution(mesh):

time: 320 us -> 244 us (0.76)
  the two profiles are of different devices: /device:TPU:32 before, /device:TPU:1 now
where the time goes in v2:
time: 244 us; the launch traced here: 242 us
  starting transfers between devices  115 us (47%)
  waiting for transfers between devices  55.7 us (23%)
  blocking collectives  31.5 us (13%)
  between operations  14 us (6%)
  matrix products  12.1 us (5%)
  local copies, waits for them, and re-layouts  9.17 us (4%)
  other arithmetic  4.27 us (2%)
    ppermute x15, starting transfers between devices, per_device(): vector = lax.ppermute(vector, 'seg', chain)  75 us
    ppermute x6, starting transfers between devices, per_device(): parts.append(lax.ppermute(pieces, 'sec', pairs))  35.1 us
    all_gather x1, blocking collectives, per_device(): occ_group = lax.all_gather(occ_mine, 'seg', axis=1, tiled=True)  31.5 us
    ppermute x6, waiting for transfers between devices, exchange_rounds(): total = total + lax.ppermute(value, axis, pairs)  22.2 us
    all_gather x1, waiting for transfers between devices, per_device(): gathered = lax.all_gather(packed, 'sec', axis=0, tiled=False)  16.1 us
    ppermute x15, waiting for transfers between devices, per_device(): vector = lax.ppermute(vector, 'seg', chain)  12.8 us
    dot_general x16, matrix products, apply(): jnp.einsum('kqa,qnab->knb', spread, oriented, preferred_element_type=jnp....  12.1 us
  transfers between devices with their start and end apart: 29, of which 20 were waited for; matrix products, arithmetic and copies ran while one was open for 1% of the time, Pallas kernels for 0%

profile of v2, /device:TPU:1, one launch (start us, length us, event | category | flops | bytes accessed | tf_op | source)
XLA Modules:
  0.0 242.1 jit_solution(17951691260832447901)
XLA Ops:
  9.1 31.5 %all-gather.1 = s32[32,1,64]{2,1,0:T(1,128)S(1)} all-gather(s32[1,1,64]{2,1,0:T(1,128)S(1)} %get-tuple-element.25), channel_id=1, replica_groups=mesh['seg'=32,'sec'=16] {'seg'}, dimensions={0}, use_global_device_ids=true | all-gather | bytes 8448 | tf_op jit(solution)/shard_map/all_gather | solution.py:42
  42.3 16.1 %all-gather.4.cloned.1.call-done = bf16[8448,128]{1,0:T(8,128)(2,1)} async-done(((bf16[528,128]{1,0:T(8,128)(2,1)}), bf16[8448,128]{1,0:T(8,128)(2,1)}) %all-gather.4.cloned.1.call-update) | async-done | bytes 2162704 | tf_op jit(solution)/shard_map/all_gather | solution.py:33
  59.3 3.1 %slice.23 = bf16[16,512,128]{2,1,0:T(8,128)(2,1)} slice(bf16[16,528,128]{2,1,0:T(8,128)(2,1)} %bitcast.198), slice={[0:16], [0:512], [0:128]} | slice | bytes 4194304 | tf_op jit(solution)/shard_map/slice | solution.py:36
  63.7 3.1 %conditional.1 = (bf16[16,4,128,128]{2,3,0,1:T(8,128)(2,1)S(1)}) conditional(s32[]{:T(128)} %convert_element_type.72, bf16[16,4,128,128]{3,2,1,0:T(8,128)(2,1)} %bitcast.10, bf16[16,4,128,128]{3,2,1,0:T(8,128)(2,1)} %bitcast.10), branch_computations={%region_2.4_spmd, %region_3.5_spmd} | conditional | bytes 4194312 | solution.py:61
  67.6 3.1 %collective-permute-start = (bf16[64,128]{1,0:T(8,128)(2,1)S(1)}, bf16[64,128]{1,0:T(8,128)(2,1)S(1)}, u32[]{:S(2)}, u32[]{:S(2)}) collective-permute-start(bf16[64,128]{1,0:T(8,128)(2,1)S(1)} %fusion.31), channel_id=1, source_target_pairs={{0,16},{16,32},{32,48},{48,64},{64,80},{80,96},{96,112},{112,128},... | collective-permute-start | bytes 49160 | tf_op jit(solution)/shard_map/ppermute | solution.py:86
  72.3 3.6 %collective-permute-start.1 = (bf16[64,128]{1,0:T(8,128)(2,1)S(1)}, bf16[64,128]{1,0:T(8,128)(2,1)S(1)}, u32[]{:S(2)}, u32[]{:S(2)}) collective-permute-start(bf16[64,128]{1,0:T(8,128)(2,1)S(1)} %fusion.30), channel_id=1, source_target_pairs={{0,16},{16,32},{32,48},{48,64},{64,80},{80,96},{96,112},{112,128},... | collective-permute-start | bytes 49160 | tf_op jit(solution)/shard_map/ppermute | solution.py:86
  77.5 3.6 %collective-permute-start.2 = (bf16[64,128]{1,0:T(8,128)(2,1)S(1)}, bf16[64,128]{1,0:T(8,128)(2,1)S(1)}, u32[]{:S(2)}, u32[]{:S(2)}) collective-permute-start(bf16[64,128]{1,0:T(8,128)(2,1)S(1)} %fusion.29), channel_id=1, source_target_pairs={{0,16},{16,32},{32,48},{48,64},{64,80},{80,96},{96,112},{112,128},... | collective-permute-start | bytes 49160 | tf_op jit(solution)/shard_map/ppermute | solution.py:86
  82.8 3.6 %collective-permute-start.3 = (bf16[64,128]{1,0:T(8,128)(2,1)S(1)}, bf16[64,128]{1,0:T(8,128)(2,1)S(1)}, u32[]{:S(2)}, u32[]{:S(2)}) collective-permute-start(bf16[64,128]{1,0:T(8,128)(2,1)S(1)} %fusion.28), channel_id=1, source_target_pairs={{0,16},{16,32},{32,48},{48,64},{64,80},{80,96},{96,112},{112,128},... | collective-permute-start | bytes 49160 | tf_op jit(solution)/shard_map/ppermute | solution.py:86
  88.0 3.7 %collective-permute-start.4 = (bf16[64,128]{1,0:T(8,128)(2,1)S(1)}, bf16[64,128]{1,0:T(8,128)(2,1)S(1)}, u32[]{:S(2)}, u32[]{:S(2)}) collective-permute-start(bf16[64,128]{1,0:T(8,128)(2,1)S(1)} %fusion.27), channel_id=1, source_target_pairs={{0,16},{16,32},{32,48},{48,64},{64,80},{80,96},{96,112},{112,128},... | collective-permute-start | bytes 49160 | tf_op jit(solution)/shard_map/ppermute | solution.py:86
  93.4 5.7 %collective-permute-start.5 = (bf16[64,128]{1,0:T(8,128)(2,1)S(1)}, bf16[64,128]{1,0:T(8,128)(2,1)S(1)}, u32[]{:S(2)}, u32[]{:S(2)}) collective-permute-start(bf16[64,128]{1,0:T(8,128)(2,1)S(1)} %fusion.26), channel_id=1, source_target_pairs={{0,16},{16,32},{32,48},{48,64},{64,80},{80,96},{96,112},{112,128},... | collective-permute-start | bytes 49160 | tf_op jit(solution)/shard_map/ppermute | solution.py:86
  100.7 5.7 %collective-permute-start.6 = (bf16[64,128]{1,0:T(8,128)(2,1)S(1)}, bf16[64,128]{1,0:T(8,128)(2,1)S(1)}, u32[]{:S(2)}, u32[]{:S(2)}) collective-permute-start(bf16[64,128]{1,0:T(8,128)(2,1)S(1)} %fusion.25), channel_id=1, source_target_pairs={{0,16},{16,32},{32,48},{48,64},{64,80},{80,96},{96,112},{112,128},... | collective-permute-start | bytes 49160 | tf_op jit(solution)/shard_map/ppermute | solution.py:86
  108.1 5.7 %collective-permute-start.7 = (bf16[64,128]{1,0:T(8,128)(2,1)S(1)}, bf16[64,128]{1,0:T(8,128)(2,1)S(1)}, u32[]{:S(2)}, u32[]{:S(2)}) collective-permute-start(bf16[64,128]{1,0:T(8,128)(2,1)S(1)} %fusion.24), channel_id=1, source_target_pairs={{0,16},{16,32},{32,48},{48,64},{64,80},{80,96},{96,112},{112,128},... | collective-permute-start | bytes 49160 | tf_op jit(solution)/shard_map/ppermute | solution.py:86
  115.4 5.7 %collective-permute-start.8 = (bf16[64,128]{1,0:T(8,128)(2,1)S(1)}, bf16[64,128]{1,0:T(8,128)(2,1)S(1)}, u32[]{:S(2)}, u32[]{:S(2)}) collective-permute-start(bf16[64,128]{1,0:T(8,128)(2,1)S(1)} %fusion.23), channel_id=1, source_target_pairs={{0,16},{16,32},{32,48},{48,64},{64,80},{80,96},{96,112},{112,128},... | collective-permute-start | bytes 49160 | tf_op jit(solution)/shard_map/ppermute | solution.py:86
  122.8 5.7 %collective-permute-start.9 = (bf16[64,128]{1,0:T(8,128)(2,1)S(1)}, bf16[64,128]{1,0:T(8,128)(2,1)S(1)}, u32[]{:S(2)}, u32[]{:S(2)}) collective-permute-start(bf16[64,128]{1,0:T(8,128)(2,1)S(1)} %fusion.22), channel_id=1, source_target_pairs={{0,16},{16,32},{32,48},{48,64},{64,80},{80,96},{96,112},{112,128},... | collective-permute-start | bytes 49160 | tf_op jit(solution)/shard_map/ppermute | solution.py:86
  130.1 5.7 %collective-permute-start.10 = (bf16[64,128]{1,0:T(8,128)(2,1)S(1)}, bf16[64,128]{1,0:T(8,128)(2,1)S(1)}, u32[]{:S(2)}, u32[]{:S(2)}) collective-permute-start(bf16[64,128]{1,0:T(8,128)(2,1)S(1)} %fusion.21), channel_id=1, source_target_pairs={{0,16},{16,32},{32,48},{48,64},{64,80},{80,96},{96,112},{112,128},... | collective-permute-start | bytes 49160 | tf_op jit(solution)/shard_map/ppermute | solution.py:86
  137.5 5.7 %collective-permute-start.11 = (bf16[64,128]{1,0:T(8,128)(2,1)S(1)}, bf16[64,128]{1,0:T(8,128)(2,1)S(1)}, u32[]{:S(2)}, u32[]{:S(2)}) collective-permute-start(bf16[64,128]{1,0:T(8,128)(2,1)S(1)} %fusion.20), channel_id=1, source_target_pairs={{0,16},{16,32},{32,48},{48,64},{64,80},{80,96},{96,112},{112,128},... | collective-permute-start | bytes 49160 | tf_op jit(solution)/shard_map/ppermute | solution.py:86
  144.8 5.7 %collective-permute-start.12 = (bf16[64,128]{1,0:T(8,128)(2,1)S(1)}, bf16[64,128]{1,0:T(8,128)(2,1)S(1)}, u32[]{:S(2)}, u32[]{:S(2)}) collective-permute-start(bf16[64,128]{1,0:T(8,128)(2,1)S(1)} %fusion.19), channel_id=1, source_target_pairs={{0,16},{16,32},{32,48},{48,64},{64,80},{80,96},{96,112},{112,128},... | collective-permute-start | bytes 49160 | tf_op jit(solution)/shard_map/ppermute | solution.py:86
  152.2 5.7 %collective-permute-start.13 = (bf16[64,128]{1,0:T(8,128)(2,1)S(1)}, bf16[64,128]{1,0:T(8,128)(2,1)S(1)}, u32[]{:S(2)}, u32[]{:S(2)}) collective-permute-start(bf16[64,128]{1,0:T(8,128)(2,1)S(1)} %fusion.18), channel_id=1, source_target_pairs={{0,16},{16,32},{32,48},{48,64},{64,80},{80,96},{96,112},{112,128},... | collective-permute-start | bytes 49160 | tf_op jit(solution)/shard_map/ppermute | solution.py:86
  159.5 5.7 %collective-permute-start.14 = (bf16[64,128]{1,0:T(8,128)(2,1)S(1)}, bf16[64,128]{1,0:T(8,128)(2,1)S(1)}, u32[]{:S(2)}, u32[]{:S(2)}) collective-permute-start(bf16[64,128]{1,0:T(8,128)(2,1)S(1)} %fusion.17), channel_id=1, source_target_pairs={{0,16},{16,32},{32,48},{48,64},{64,80},{80,96},{96,112},{112,128},... | collective-permute-start | bytes 49160 | tf_op jit(solution)/shard_map/ppermute | solution.py:86
  167.8 18.3 %collective-permute-start.16 = (f32[1,64]{1,0:T(1,128)S(1)}, f32[1,64]{1,0:T(1,128)S(1)}, u32[]{:S(2)}, u32[]{:S(2)}) collective-permute-start(f32[1,64]{1,0:T(1,128)S(1)} %fusion.103), channel_id=1, source_target_pairs={{0,1},{1,0},{2,3},{3,2},{4,5},{5,4},{6,7},{7,6},{8,9},{9,8},{10,11... | collective-permute-start | bytes 776 | tf_op jit(solution)/shard_map/ppermute | solution.py:101
  193.5 3.9 %collective-permute-start.19 = (f32[4,64]{1,0:T(4,128)S(1)}, f32[4,64]{1,0:T(4,128)S(1)}, u32[]{:S(2)}, u32[]{:S(2)}) collective-permute-start(f32[4,64]{1,0:T(4,128)S(1)} %pad_maximum_fusion.1), channel_id=1, source_target_pairs={{0,4},{1,5},{2,6},{3,7},{4,0},{5,1},{6,2},{7,3},{8,12},{9,13},{10,... | collective-permute-start | bytes 3080 | tf_op jit(solution)/shard_map/ppermute | solution.py:101
  197.4 3.8 %collective-permute-start.20 = (f32[4,64]{1,0:T(4,128)S(1)}, f32[4,64]{1,0:T(4,128)S(1)}, u32[]{:S(2)}, u32[]{:S(2)}) collective-permute-start(f32[4,64]{1,0:T(4,128)S(1)} %pad_maximum_fusion.1), channel_id=1, source_target_pairs={{0,8},{1,9},{2,10},{3,11},{4,12},{5,13},{6,14},{7,15},{8,0},{9,1},... | collective-permute-start | bytes 3080 | tf_op jit(solution)/shard_map/ppermute | solution.py:101
  201.2 3.7 %collective-permute-start.21 = (f32[4,64]{1,0:T(4,128)S(1)}, f32[4,64]{1,0:T(4,128)S(1)}, u32[]{:S(2)}, u32[]{:S(2)}) collective-permute-start(f32[4,64]{1,0:T(4,128)S(1)} %pad_maximum_fusion.1), channel_id=1, source_target_pairs={{0,12},{1,13},{2,14},{3,15},{4,8},{5,9},{6,10},{7,11},{8,4},{9,5},... | collective-permute-start | bytes 3080 | tf_op jit(solution)/shard_map/ppermute | solution.py:101
  212.5 22.2 %collective-permute-done.27 = f32[1024]{0:T(1024)S(1)} collective-permute-done((f32[1024]{0:T(1024)S(1)}, f32[1024]{0:T(1024)S(1)}, u32[]{:S(2)}, u32[]{:S(2)}) %collective-permute-start.27) | collective-permute-done | bytes 4128 | tf_op jit(solution)/shard_map/ppermute | solution.py:11
  (82 shorter events, 50.5 us)
Async XLA Ops:
  6.5 51.9 %all-gather.4.cloned.1.call-start = ((), (), s32[]{:S(2)}) async-start(), calls=%async_computation | async-start | bytes 2297856 | tf_op jit(solution)/shard_map/all_gather | solution.py:33
  67.6 3.9 %collective-permute-start = (bf16[64,128]{1,0:T(8,128)(2,1)S(1)}, bf16[64,128]{1,0:T(8,128)(2,1)S(1)}, u32[]{:S(2)}, u32[]{:S(2)}) collective-permute-start(bf16[64,128]{1,0:T(8,128)(2,1)S(1)} %fusion.31), channel_id=1, source_target_pairs={{0,16},{16,32},{32,48},{48,64},{64,80},{80,96},{96,112},{112,128},... | collective-permute-start | bytes 49160 | tf_op jit(solution)/shard_map/ppermute | solution.py:86
  72.3 4.5 %collective-permute-start.1 = (bf16[64,128]{1,0:T(8,128)(2,1)S(1)}, bf16[64,128]{1,0:T(8,128)(2,1)S(1)}, u32[]{:S(2)}, u32[]{:S(2)}) collective-permute-start(bf16[64,128]{1,0:T(8,128)(2,1)S(1)} %fusion.30), channel_id=1, source_target_pairs={{0,16},{16,32},{32,48},{48,64},{64,80},{80,96},{96,112},{112,128},... | collective-permute-start | bytes 49160 | tf_op jit(solution)/shard_map/ppermute | solution.py:86
  77.5 4.5 %collective-permute-start.2 = (bf16[64,128]{1,0:T(8,128)(2,1)S(1)}, bf16[64,128]{1,0:T(8,128)(2,1)S(1)}, u32[]{:S(2)}, u32[]{:S(2)}) collective-permute-start(bf16[64,128]{1,0:T(8,128)(2,1)S(1)} %fusion.29), channel_id=1, source_target_pairs={{0,16},{16,32},{32,48},{48,64},{64,80},{80,96},{96,112},{112,128},... | collective-permute-start | bytes 49160 | tf_op jit(solution)/shard_map/ppermute | solution.py:86
  82.8 4.5 %collective-permute-start.3 = (bf16[64,128]{1,0:T(8,128)(2,1)S(1)}, bf16[64,128]{1,0:T(8,128)(2,1)S(1)}, u32[]{:S(2)}, u32[]{:S(2)}) collective-permute-start(bf16[64,128]{1,0:T(8,128)(2,1)S(1)} %fusion.28), channel_id=1, source_target_pairs={{0,16},{16,32},{32,48},{48,64},{64,80},{80,96},{96,112},{112,128},... | collective-permute-start | bytes 49160 | tf_op jit(solution)/shard_map/ppermute | solution.py:86
  88.0 4.6 %collective-permute-start.4 = (bf16[64,128]{1,0:T(8,128)(2,1)S(1)}, bf16[64,128]{1,0:T(8,128)(2,1)S(1)}, u32[]{:S(2)}, u32[]{:S(2)}) collective-permute-start(bf16[64,128]{1,0:T(8,128)(2,1)S(1)} %fusion.27), channel_id=1, source_target_pairs={{0,16},{16,32},{32,48},{48,64},{64,80},{80,96},{96,112},{112,128},... | collective-permute-start | bytes 49160 | tf_op jit(solution)/shard_map/ppermute | solution.py:86
  93.4 6.6 %collective-permute-start.5 = (bf16[64,128]{1,0:T(8,128)(2,1)S(1)}, bf16[64,128]{1,0:T(8,128)(2,1)S(1)}, u32[]{:S(2)}, u32[]{:S(2)}) collective-permute-start(bf16[64,128]{1,0:T(8,128)(2,1)S(1)} %fusion.26), channel_id=1, source_target_pairs={{0,16},{16,32},{32,48},{48,64},{64,80},{80,96},{96,112},{112,128},... | collective-permute-start | bytes 49160 | tf_op jit(solution)/shard_map/ppermute | solution.py:86
  100.7 6.6 %collective-permute-start.6 = (bf16[64,128]{1,0:T(8,128)(2,1)S(1)}, bf16[64,128]{1,0:T(8,128)(2,1)S(1)}, u32[]{:S(2)}, u32[]{:S(2)}) collective-permute-start(bf16[64,128]{1,0:T(8,128)(2,1)S(1)} %fusion.25), channel_id=1, source_target_pairs={{0,16},{16,32},{32,48},{48,64},{64,80},{80,96},{96,112},{112,128},... | collective-permute-start | bytes 49160 | tf_op jit(solution)/shard_map/ppermute | solution.py:86
  108.1 6.6 %collective-permute-start.7 = (bf16[64,128]{1,0:T(8,128)(2,1)S(1)}, bf16[64,128]{1,0:T(8,128)(2,1)S(1)}, u32[]{:S(2)}, u32[]{:S(2)}) collective-permute-start(bf16[64,128]{1,0:T(8,128)(2,1)S(1)} %fusion.24), channel_id=1, source_target_pairs={{0,16},{16,32},{32,48},{48,64},{64,80},{80,96},{96,112},{112,128},... | collective-permute-start | bytes 49160 | tf_op jit(solution)/shard_map/ppermute | solution.py:86
  115.4 6.6 %collective-permute-start.8 = (bf16[64,128]{1,0:T(8,128)(2,1)S(1)}, bf16[64,128]{1,0:T(8,128)(2,1)S(1)}, u32[]{:S(2)}, u32[]{:S(2)}) collective-permute-start(bf16[64,128]{1,0:T(8,128)(2,1)S(1)} %fusion.23), channel_id=1, source_target_pairs={{0,16},{16,32},{32,48},{48,64},{64,80},{80,96},{96,112},{112,128},... | collective-permute-start | bytes 49160 | tf_op jit(solution)/shard_map/ppermute | solution.py:86
  122.8 6.6 %collective-permute-start.9 = (bf16[64,128]{1,0:T(8,128)(2,1)S(1)}, bf16[64,128]{1,0:T(8,128)(2,1)S(1)}, u32[]{:S(2)}, u32[]{:S(2)}) collective-permute-start(bf16[64,128]{1,0:T(8,128)(2,1)S(1)} %fusion.22), channel_id=1, source_target_pairs={{0,16},{16,32},{32,48},{48,64},{64,80},{80,96},{96,112},{112,128},... | collective-permute-start | bytes 49160 | tf_op jit(solution)/shard_map/ppermute | solution.py:86
  130.1 6.6 %collective-permute-start.10 = (bf16[64,128]{1,0:T(8,128)(2,1)S(1)}, bf16[64,128]{1,0:T(8,128)(2,1)S(1)}, u32[]{:S(2)}, u32[]{:S(2)}) collective-permute-start(bf16[64,128]{1,0:T(8,128)(2,1)S(1)} %fusion.21), channel_id=1, source_target_pairs={{0,16},{16,32},{32,48},{48,64},{64,80},{80,96},{96,112},{112,128},... | collective-permute-start | bytes 49160 | tf_op jit(solution)/shard_map/ppermute | solution.py:86
  137.5 6.6 %collective-permute-start.11 = (bf16[64,128]{1,0:T(8,128)(2,1)S(1)}, bf16[64,128]{1,0:T(8,128)(2,1)S(1)}, u32[]{:S(2)}, u32[]{:S(2)}) collective-permute-start(bf16[64,128]{1,0:T(8,128)(2,1)S(1)} %fusion.20), channel_id=1, source_target_pairs={{0,16},{16,32},{32,48},{48,64},{64,80},{80,96},{96,112},{112,128},... | collective-permute-start | bytes 49160 | tf_op jit(solution)/shard_map/ppermute | solution.py:86
  144.8 6.6 %collective-permute-start.12 = (bf16[64,128]{1,0:T(8,128)(2,1)S(1)}, bf16[64,128]{1,0:T(8,128)(2,1)S(1)}, u32[]{:S(2)}, u32[]{:S(2)}) collective-permute-start(bf16[64,128]{1,0:T(8,128)(2,1)S(1)} %fusion.19), channel_id=1, source_target_pairs={{0,16},{16,32},{32,48},{48,64},{64,80},{80,96},{96,112},{112,128},... | collective-permute-start | bytes 49160 | tf_op jit(solution)/shard_map/ppermute | solution.py:86
  152.2 6.6 %collective-permute-start.13 = (bf16[64,128]{1,0:T(8,128)(2,1)S(1)}, bf16[64,128]{1,0:T(8,128)(2,1)S(1)}, u32[]{:S(2)}, u32[]{:S(2)}) collective-permute-start(bf16[64,128]{1,0:T(8,128)(2,1)S(1)} %fusion.18), channel_id=1, source_target_pairs={{0,16},{16,32},{32,48},{48,64},{64,80},{80,96},{96,112},{112,128},... | collective-permute-start | bytes 49160 | tf_op jit(solution)/shard_map/ppermute | solution.py:86
  159.5 6.6 %collective-permute-start.14 = (bf16[64,128]{1,0:T(8,128)(2,1)S(1)}, bf16[64,128]{1,0:T(8,128)(2,1)S(1)}, u32[]{:S(2)}, u32[]{:S(2)}) collective-permute-start(bf16[64,128]{1,0:T(8,128)(2,1)S(1)} %fusion.17), channel_id=1, source_target_pairs={{0,16},{16,32},{32,48},{48,64},{64,80},{80,96},{96,112},{112,128},... | collective-permute-start | bytes 49160 | tf_op jit(solution)/shard_map/ppermute | solution.py:86
  167.8 23.8 %collective-permute-start.16 = (f32[1,64]{1,0:T(1,128)S(1)}, f32[1,64]{1,0:T(1,128)S(1)}, u32[]{:S(2)}, u32[]{:S(2)}) collective-permute-start(f32[1,64]{1,0:T(1,128)S(1)} %fusion.103), channel_id=1, source_target_pairs={{0,1},{1,0},{2,3},{3,2},{4,5},{5,4},{6,7},{7,6},{8,9},{9,8},{10,11... | collective-permute-start | bytes 776 | tf_op jit(solution)/shard_map/ppermute | solution.py:101
  186.0 5.5 %collective-permute-start.17 = (f32[1,64]{1,0:T(1,128)S(1)}, f32[1,64]{1,0:T(1,128)S(1)}, u32[]{:S(2)}, u32[]{:S(2)}) collective-permute-start(f32[1,64]{1,0:T(1,128)S(1)} %fusion.103), channel_id=1, source_target_pairs={{0,2},{1,3},{2,0},{3,1},{4,6},{5,7},{6,4},{7,5},{8,10},{9,11},{10,... | collective-permute-start | bytes 776 | tf_op jit(solution)/shard_map/ppermute | solution.py:101
  188.6 4.9 %collective-permute-start.18 = (f32[1,64]{1,0:T(1,128)S(1)}, f32[1,64]{1,0:T(1,128)S(1)}, u32[]{:S(2)}, u32[]{:S(2)}) collective-permute-start(f32[1,64]{1,0:T(1,128)S(1)} %fusion.103), channel_id=1, source_target_pairs={{0,3},{1,2},{2,1},{3,0},{4,7},{5,6},{6,5},{7,4},{8,11},{9,10},{10,... | collective-permute-start | bytes 776 | tf_op jit(solution)/shard_map/ppermute | solution.py:101
  193.5 11.4 %collective-permute-start.19 = (f32[4,64]{1,0:T(4,128)S(1)}, f32[4,64]{1,0:T(4,128)S(1)}, u32[]{:S(2)}, u32[]{:S(2)}) collective-permute-start(f32[4,64]{1,0:T(4,128)S(1)} %pad_maximum_fusion.1), channel_id=1, source_target_pairs={{0,4},{1,5},{2,6},{3,7},{4,0},{5,1},{6,2},{7,3},{8,12},{9,13},{10,... | collective-permute-start | bytes 3080 | tf_op jit(solution)/shard_map/ppermute | solution.py:101
  197.4 8.2 %collective-permute-start.20 = (f32[4,64]{1,0:T(4,128)S(1)}, f32[4,64]{1,0:T(4,128)S(1)}, u32[]{:S(2)}, u32[]{:S(2)}) collective-permute-start(f32[4,64]{1,0:T(4,128)S(1)} %pad_maximum_fusion.1), channel_id=1, source_target_pairs={{0,8},{1,9},{2,10},{3,11},{4,12},{5,13},{6,14},{7,15},{8,0},{9,1},... | collective-permute-start | bytes 3080 | tf_op jit(solution)/shard_map/ppermute | solution.py:101
  201.2 6.4 %collective-permute-start.21 = (f32[4,64]{1,0:T(4,128)S(1)}, f32[4,64]{1,0:T(4,128)S(1)}, u32[]{:S(2)}, u32[]{:S(2)}) collective-permute-start(f32[4,64]{1,0:T(4,128)S(1)} %pad_maximum_fusion.1), channel_id=1, source_target_pairs={{0,12},{1,13},{2,14},{3,15},{4,8},{5,9},{6,10},{7,11},{8,4},{9,5},... | collective-permute-start | bytes 3080 | tf_op jit(solution)/shard_map/ppermute | solution.py:101
  209.8 2.6 %collective-permute-start.25 = (f32[1024]{0:T(1024)S(1)}, f32[1024]{0:T(1024)S(1)}, u32[]{:S(2)}, u32[]{:S(2)}) collective-permute-start(f32[1024]{0:T(1024)S(1)} %add_add_fusion.1), channel_id=1, source_target_pairs={{192,128},{208,144},{224,160},{240,176},{256,320},{272,336},{288,3... | collective-permute-start | bytes 12296 | tf_op jit(solution)/shard_map/ppermute | solution.py:11
  211.2 23.5 %collective-permute-start.27 = (f32[1024]{0:T(1024)S(1)}, f32[1024]{0:T(1024)S(1)}, u32[]{:S(2)}, u32[]{:S(2)}) collective-permute-start(f32[1024]{0:T(1024)S(1)} %add_add_fusion.1), channel_id=1, source_target_pairs={{192,0},{208,16},{224,32},{240,48},{256,448},{272,464},{288,480},{... | collective-permute-start | bytes 12296 | tf_op jit(solution)/shard_map/ppermute | solution.py:11
  (5 other events, 6.8 us)
Sparse Core Ops, SparseCore 0:
  9.5 48.9 all-gather.3

commit v3 on v2

v3 whole, which is shorter than its diff:
```python
import jax
import jax.numpy as jnp
from jax import lax
from jax.sharding import PartitionSpec as P


def spread_pairs(holders, count, fan):
    have = sorted(holders)
    rounds = []
    while len(have) < count:
        missing = [i for i in range(count) if i not in have]
        perms = []
        for _ in range(fan):
            pairs = []
            for h in have:
                if not missing:
                    break
                target = min(missing, key=lambda m: (abs(m - h), m))
                missing.remove(target)
                pairs.append((h, target))
            if pairs:
                perms.append(pairs)
        rounds.append(perms)
        have = sorted(set(have) | {t for perm in perms for _, t in perm})
    return rounds


def per_device(blocks, left_edge, right_edge, occupation, start_sector):
    seg_count = lax.axis_size("seg")
    sec_count = lax.axis_size("sec")
    half_count = seg_count // 2
    seg_index = lax.axis_index("seg")
    sec_index = lax.axis_index("sec")
    is_left = seg_index < half_count
    partner = seg_index ^ 1
    depth = jnp.where(is_left, seg_index // 2, (seg_count - 1 - seg_index) // 2)

    conf_count = occupation.shape[0]
    sites = seg_count * occupation.shape[1]
    group = conf_count // sec_count
    width = blocks.shape[-1]
    local_states = blocks.shape[1]

    rows = blocks[0, :, 0].reshape(local_states * width, width)
    pad = jnp.zeros((14, width), blocks.dtype)
    packed = jnp.concatenate([rows, left_edge, right_edge, pad], axis=0)
    gathered = lax.all_gather(packed, "sec", axis=0, tiled=False)
    nsec = gathered.shape[0]
    body = local_states * width
    lefts = gathered[:, body]
    rights = gathered[:, body + 1]

    feed = [(2 * m + 1, 2 * m) for m in range(half_count // 2)] + [
        (2 * m, 2 * m + 1) for m in range(half_count // 2, seg_count // 2)
    ]
    partner_gathered = lax.ppermute(gathered[:, :body], "seg", feed)

    def arrange(transpose):
        def build(own, other):
            pair = []
            for part in (own[:, :body], other):
                part = part.reshape(nsec, local_states, width, width)
                pair.append(jnp.swapaxes(part, 2, 3) if transpose else part)
            return tuple(pair)

        return build

    oriented = lax.cond(is_left, arrange(False), arrange(True), gathered, partner_gathered)

    row0 = sec_index * group
    occ_mine = lax.dynamic_slice_in_dim(occupation, row0, group, axis=0)
    occ_group = lax.all_gather(occ_mine, "seg", axis=1, tiled=True)
    start_group = lax.dynamic_slice_in_dim(start_sector, row0, group, axis=0)

    charge = jnp.array([0, 1, -1, 0], dtype=jnp.int32)
    steps = charge[occ_group]
    site_ids = jnp.arange(sites, dtype=jnp.int32)
    total = jnp.sum(steps, axis=1)
    sector_end = jnp.mod(start_group + total, nsec)
    sector_ids = jnp.arange(nsec, dtype=jnp.int32)
    state_ids = jnp.arange(local_states, dtype=jnp.int32)

    def site_masks(site):
        before = jnp.sum(jnp.where(site_ids[None, :] < site, steps, 0), axis=1)
        sector = jnp.mod(start_group + before, nsec)
        occ = jnp.sum(jnp.where(site_ids[None, :] == site, occ_group, 0), axis=1)
        sector_hot = (sector[:, None] == sector_ids[None, :]).astype(jnp.bfloat16)
        state_hot = (occ[:, None] == state_ids[None, :]).astype(jnp.float32)
        return sector_hot, state_hot

    masks = [site_masks(seg_index), site_masks(partner)]

    def apply(vector, which):
        sector_hot, state_hot = masks[which]
        spread = vector[:, None, :] * sector_hot[:, :, None]
        products = jnp.einsum(
            "kqa,qnab->knb", spread, oriented[which], preferred_element_type=jnp.float32
        )
        return jnp.sum(products * state_hot[:, :, None], axis=1).astype(jnp.bfloat16)

    first_left = jnp.take(lefts, start_group, axis=0)
    first_right = jnp.take(rights, sector_end, axis=0)
    first = jnp.where(is_left, first_left, first_right)
    vector = jnp.where(depth == 0, first, jnp.zeros_like(first))

    chain = [(j, j + 2) for j in range(0, half_count - 2, 2)] + [
        (j, j - 2) for j in range(half_count + 3, seg_count, 2)
    ]
    chain_steps = half_count // 2
    for step in range(chain_steps):
        vector = apply(vector, 0)
        vector = apply(vector, 1)
        if step < chain_steps - 1:
            vector = lax.ppermute(vector, "seg", chain)

    low, high = half_count - 2, half_count + 1
    other = lax.ppermute(vector, "seg", [(low, high), (high, low)])
    amp = jnp.sum(vector.astype(jnp.float32) * other.astype(jnp.float32), axis=1)
    at_meet = (seg_index == low) | (seg_index == high)
    amp = jnp.where(at_meet, amp, jnp.zeros_like(amp))

    pieces = amp[None, :]
    span = 1
    while span < sec_count:
        own_slot = (sec_index // span) % 4
        parts = [pieces]
        for t in (1, 2, 3):
            pairs = [(i, i ^ (t * span)) for i in range(sec_count)]
            parts.append(lax.ppermute(pieces, "sec", pairs))
        slots = []
        for r in range(4):
            chosen = jnp.zeros_like(pieces)
            for t in range(4):
                chosen = chosen + jnp.where(own_slot ^ t == r, parts[t], jnp.zeros_like(pieces))
            slots.append(chosen)
        pieces = jnp.concatenate(slots, axis=0)
        span *= 4
    full = pieces.reshape(conf_count)

    for perms in spread_pairs([low, high], seg_count, 3):
        received = [lax.ppermute(full, "seg", pairs) for pairs in perms]
        for value in received:
            full = full + value
    return full


def solution(mesh):
    in_specs = (
        P("seg", None, "sec", None, None),
        P("sec", None),
        P("sec", None),
        P(None, "seg"),
        P(),
    )
    out_specs = P()
    return jax.shard_map(
        per_device, mesh=mesh, in_specs=in_specs, out_specs=out_specs, check_vma=False
    )
```

time: 244 us -> 252 us (1.033)
  the two profiles are of different devices: /device:TPU:1 before, /device:TPU:14 now
where the time goes in v3:
time: 252 us; the launch traced here: 251 us
  waiting for transfers between devices  127 us (50%)
  blocking collectives  35 us (14%)
  starting transfers between devices  33.8 us (13%)
  matrix products  24.8 us (10%)
  between operations  14.1 us (6%)
  local copies, waits for them, and re-layouts  13.3 us (5%)
  other arithmetic  3.55 us (1%)
    ppermute x6, waiting for transfers between devices, per_device(): received = [lax.ppermute(full, 'seg', pairs) for pairs in perms]  65.8 us
    ppermute x1, waiting for transfers between devices, per_device(): partner_gathered = lax.ppermute(gathered[:, :body], 'seg', feed)  42.7 us
    all_gather x1, blocking collectives, per_device(): occ_group = lax.all_gather(occ_mine, 'seg', axis=1, tiled=True)  35 us
    dot_general x16, matrix products, apply(): jnp.einsum('kqa,qnab->knb', spread, oriented[which], preferred_element_ty...  24.8 us
    ppermute x6, starting transfers between devices, per_device(): parts.append(lax.ppermute(pieces, 'sec', pairs))  19.8 us
    all_gather x1, waiting for transfers between devices, per_device(): gathered = lax.all_gather(packed, 'sec', axis=0, tiled=False)  12.5 us
    cond x2, local copies, waits for them, and re-layouts, per_device(): lax.cond(is_left, arrange(False), arrange(True), gathered, partner_gathered)  6.99 us
    ppermute x6, waiting for transfers between devices, per_device(): parts.append(lax.ppermute(pieces, 'sec', pairs))  5.8 us
  transfers between devices with their start and end apart: 22, of which 6 were waited for; matrix products, arithmetic and copies ran while one was open for 1% of the time, Pallas kernels for 0%

profile of v3, /device:TPU:14, one launch (start us, length us, event | category | flops | bytes accessed | tf_op | source)
XLA Modules:
  0.0 251.5 jit_solution(7035472506170108517)
XLA Ops:
  8.5 35.0 %all-gather.1 = s32[32,1,64]{2,1,0:T(1,128)S(1)} all-gather(s32[1,1,64]{2,1,0:T(1,128)S(1)} %dynamic-slice_bitcast_fusion), channel_id=1, replica_groups=mesh['seg'=32,'sec'=16] {'seg'}, dimensions={0}, use_global_device_ids=true | all-gather | bytes 8448 | tf_op jit(solution)/shard_map/all_gather | solution.py:72
  44.4 12.5 %all-gather.4.cloned.1.call-done = bf16[8448,128]{1,0:T(8,128)(2,1)} async-done(((bf16[528,128]{1,0:T(8,128)(2,1)}), bf16[8448,128]{1,0:T(8,128)(2,1)}) %all-gather.4.cloned.1.call-update) | async-done | bytes 2162704 | tf_op jit(solution)/shard_map/all_gather | solution.py:47
  56.9 3.3 %slice.29 = bf16[16,512,128]{2,1,0:T(8,128)(2,1)} slice(bf16[16,528,128]{2,1,0:T(8,128)(2,1)} %bitcast.201), slice={[0:16], [0:512], [0:128]} | slice | bytes 4194304 | tf_op jit(solution)/shard_map/slice | solution.py:56
  60.2 4.1 %collective-permute-start = (bf16[16,512,128]{2,1,0:T(8,128)(2,1)}, bf16[16,512,128]{2,1,0:T(8,128)(2,1)}, u32[]{:S(2)}, u32[]{:S(2)}) collective-permute-start(bf16[16,512,128]{2,1,0:T(8,128)(2,1)} %slice.29), channel_id=1, source_target_pairs={{16,0},{48,32},{80,64},{112,96},{144,128},{176,160},{208,192},{240... | collective-permute-start | bytes 6291464 | tf_op jit(solution)/shard_map/ppermute | solution.py:56
  65.8 42.7 %collective-permute-done = bf16[16,512,128]{2,1,0:T(8,128)(2,1)} collective-permute-done((bf16[16,512,128]{2,1,0:T(8,128)(2,1)}, bf16[16,512,128]{2,1,0:T(8,128)(2,1)}, u32[]{:S(2)}, u32[]{:S(2)}) %collective-permute-start) | collective-permute-done | bytes 2097184 | tf_op jit(solution)/shard_map/ppermute | solution.py:56
  108.5 8.5 %conditional.1 = (bf16[16,4,128,128]{2,3,0,1:T(8,128)(2,1)S(1)}, bf16[16,4,128,128]{2,3,0,1:T(8,128)(2,1)}) conditional(s32[]{:T(128)} %convert_element_type.118, (bf16[16,528,128]{2,1,0:T(8,128)(2,1)S(1)}, bf16[16,512,128]{2,1,0:T(8,128)(2,1)}) %tuple.44, (bf16[16,528,128]{2,1,0:T(8,128)(2,1)S(1)}, bf16[16,512,128]{2,1,0:T(8,128)(2,1)}) %tuple.45), branch_computations={%region_2.4_spmd, %region_3.5_spmd} | conditional | bytes 12582928 | solution.py:68
  110.1 3.0 %copy.106 = bf16[16,4,128,128]{2,3,0,1:T(8,128)(2,1)S(1)} copy(bf16[16,4,128,128]{3,2,1,0:T(8,128)(2,1)} %bitcast.206) | data formatting | bytes 4194304 | tf_op jit(solution)/shard_map/cond | solution.py:68
  113.1 4.0 %copy.108 = bf16[16,4,128,128]{2,3,0,1:T(8,128)(2,1)} copy(bf16[16,4,128,128]{3,2,1,0:T(8,128)(2,1)} %bitcast.5) | data formatting | bytes 4194304 | tf_op jit(solution)/shard_map/cond | solution.py:68
  117.8 2.3 fusion.30
  121.6 2.3 fusion.28
  125.4 2.3 fusion.26
  129.2 2.3 fusion.24
  133.0 2.3 fusion.22
  136.8 2.3 fusion.20
  140.6 2.3 fusion.18
  144.4 2.3 fusion.16
  149.6 2.8 %collective-permute-start.10 = (f32[1,64]{1,0:T(1,128)S(1)}, f32[1,64]{1,0:T(1,128)S(1)}, u32[]{:S(2)}, u32[]{:S(2)}) collective-permute-start(f32[1,64]{1,0:T(1,128)S(1)} %fusion.104), channel_id=1, source_target_pairs={{0,2},{1,3},{2,0},{3,1},{4,6},{5,7},{6,4},{7,5},{8,10},{9,11},{10,... | collective-permute-start | bytes 776 | tf_op jit(solution)/shard_map/ppermute | solution.py:129
  152.4 2.8 %collective-permute-start.11 = (f32[1,64]{1,0:T(1,128)S(1)}, f32[1,64]{1,0:T(1,128)S(1)}, u32[]{:S(2)}, u32[]{:S(2)}) collective-permute-start(f32[1,64]{1,0:T(1,128)S(1)} %fusion.104), channel_id=1, source_target_pairs={{0,3},{1,2},{2,1},{3,0},{4,7},{5,6},{6,5},{7,4},{8,11},{9,10},{10,... | collective-permute-start | bytes 776 | tf_op jit(solution)/shard_map/ppermute | solution.py:129
  155.3 2.0 collective-permute-done.11
  157.3 4.0 %collective-permute-start.14 = (f32[4,64]{1,0:T(4,128)S(1)}, f32[4,64]{1,0:T(4,128)S(1)}, u32[]{:S(2)}, u32[]{:S(2)}) collective-permute-start(f32[4,64]{1,0:T(4,128)S(1)} %pad_maximum_fusion.1), channel_id=1, source_target_pairs={{0,12},{1,13},{2,14},{3,15},{4,8},{5,9},{6,10},{7,11},{8,4},{9,5},... | collective-permute-start | bytes 3080 | tf_op jit(solution)/shard_map/ppermute | solution.py:129
  161.3 5.7 %collective-permute-start.13 = (f32[4,64]{1,0:T(4,128)S(1)}, f32[4,64]{1,0:T(4,128)S(1)}, u32[]{:S(2)}, u32[]{:S(2)}) collective-permute-start(f32[4,64]{1,0:T(4,128)S(1)} %pad_maximum_fusion.1), channel_id=1, source_target_pairs={{0,8},{1,9},{2,10},{3,11},{4,12},{5,13},{6,14},{7,15},{8,0},{9,1},... | collective-permute-start | bytes 3080 | tf_op jit(solution)/shard_map/ppermute | solution.py:129
  167.0 2.5 %collective-permute-start.12 = (f32[4,64]{1,0:T(4,128)S(1)}, f32[4,64]{1,0:T(4,128)S(1)}, u32[]{:S(2)}, u32[]{:S(2)}) collective-permute-start(f32[4,64]{1,0:T(4,128)S(1)} %pad_maximum_fusion.1), channel_id=1, source_target_pairs={{0,4},{1,5},{2,6},{3,7},{4,0},{5,1},{6,2},{7,3},{8,12},{9,13},{10,... | collective-permute-start | bytes 3080 | tf_op jit(solution)/shard_map/ppermute | solution.py:129
  170.7 2.7 %collective-permute-done.12 = f32[4,64]{1,0:T(4,128)S(1)} collective-permute-done((f32[4,64]{1,0:T(4,128)S(1)}, f32[4,64]{1,0:T(4,128)S(1)}, u32[]{:S(2)}, u32[]{:S(2)}) %collective-permute-start.12) | collective-permute-done | bytes 1056 | tf_op jit(solution)/shard_map/ppermute | solution.py:129
  178.2 65.8 %collective-permute-done.19 = f32[1024]{0:T(1024)S(1)} collective-permute-done((f32[1024]{0:T(1024)S(1)}, f32[1024]{0:T(1024)S(1)}, u32[]{:S(2)}, u32[]{:S(2)}) %collective-permute-start.19) | collective-permute-done | bytes 4128 | tf_op jit(solution)/shard_map/ppermute | solution.py:141
  (79 shorter events, 25.6 us)
Async XLA Ops:
  6.5 1.8 copy-start
  6.5 50.4 %all-gather.4.cloned.1.call-start = ((), (), s32[]{:S(2)}) async-start(), calls=%async_computation | async-start | bytes 2297856 | tf_op jit(solution)/shard_map/all_gather | solution.py:47
  56.9 7.5 %copy-start.1 = (bf16[8448,128]{1,0:T(8,128)(2,1)S(1)}, bf16[8448,128]{1,0:T(8,128)(2,1)}, u32[]{:S(2)}) copy-start(bf16[8448,128]{1,0:T(8,128)(2,1)} %all-gather.4.cloned.1.call-done) | copy-start | bytes 6488068
  60.2 48.3 %collective-permute-start = (bf16[16,512,128]{2,1,0:T(8,128)(2,1)}, bf16[16,512,128]{2,1,0:T(8,128)(2,1)}, u32[]{:S(2)}, u32[]{:S(2)}) collective-permute-start(bf16[16,512,128]{2,1,0:T(8,128)(2,1)} %slice.29), channel_id=1, source_target_pairs={{16,0},{48,32},{80,64},{112,96},{144,128},{176,160},{208,192},{240... | collective-permute-start | bytes 6291464 | tf_op jit(solution)/shard_map/ppermute | solution.py:56
  120.2 0.7 collective-permute-start.1
  124.0 0.7 collective-permute-start.2
  127.8 0.7 collective-permute-start.3
  131.6 0.7 collective-permute-start.4
  135.4 0.7 collective-permute-start.5
  139.2 0.7 collective-permute-start.6
  143.0 0.7 collective-permute-start.7
  146.8 0.7 collective-permute-start.8
  147.6 7.6 %collective-permute-start.9 = (f32[1,64]{1,0:T(1,128)S(1)}, f32[1,64]{1,0:T(1,128)S(1)}, u32[]{:S(2)}, u32[]{:S(2)}) collective-permute-start(f32[1,64]{1,0:T(1,128)S(1)} %fusion.104), channel_id=1, source_target_pairs={{0,1},{1,0},{2,3},{3,2},{4,5},{5,4},{6,7},{7,6},{8,9},{9,8},{10,11... | collective-permute-start | bytes 776 | tf_op jit(solution)/shard_map/ppermute | solution.py:129
  149.6 5.7 %collective-permute-start.10 = (f32[1,64]{1,0:T(1,128)S(1)}, f32[1,64]{1,0:T(1,128)S(1)}, u32[]{:S(2)}, u32[]{:S(2)}) collective-permute-start(f32[1,64]{1,0:T(1,128)S(1)} %fusion.104), channel_id=1, source_target_pairs={{0,2},{1,3},{2,0},{3,1},{4,6},{5,7},{6,4},{7,5},{8,10},{9,11},{10,... | collective-permute-start | bytes 776 | tf_op jit(solution)/shard_map/ppermute | solution.py:129
  152.4 4.9 %collective-permute-start.11 = (f32[1,64]{1,0:T(1,128)S(1)}, f32[1,64]{1,0:T(1,128)S(1)}, u32[]{:S(2)}, u32[]{:S(2)}) collective-permute-start(f32[1,64]{1,0:T(1,128)S(1)} %fusion.104), channel_id=1, source_target_pairs={{0,3},{1,2},{2,1},{3,0},{4,7},{5,6},{6,5},{7,4},{8,11},{9,10},{10,... | collective-permute-start | bytes 776 | tf_op jit(solution)/shard_map/ppermute | solution.py:129
  157.3 12.3 %collective-permute-start.14 = (f32[4,64]{1,0:T(4,128)S(1)}, f32[4,64]{1,0:T(4,128)S(1)}, u32[]{:S(2)}, u32[]{:S(2)}) collective-permute-start(f32[4,64]{1,0:T(4,128)S(1)} %pad_maximum_fusion.1), channel_id=1, source_target_pairs={{0,12},{1,13},{2,14},{3,15},{4,8},{5,9},{6,10},{7,11},{8,4},{9,5},... | collective-permute-start | bytes 3080 | tf_op jit(solution)/shard_map/ppermute | solution.py:129
  161.3 9.4 %collective-permute-start.13 = (f32[4,64]{1,0:T(4,128)S(1)}, f32[4,64]{1,0:T(4,128)S(1)}, u32[]{:S(2)}, u32[]{:S(2)}) collective-permute-start(f32[4,64]{1,0:T(4,128)S(1)} %pad_maximum_fusion.1), channel_id=1, source_target_pairs={{0,8},{1,9},{2,10},{3,11},{4,12},{5,13},{6,14},{7,15},{8,0},{9,1},... | collective-permute-start | bytes 3080 | tf_op jit(solution)/shard_map/ppermute | solution.py:129
  167.0 6.4 %collective-permute-start.12 = (f32[4,64]{1,0:T(4,128)S(1)}, f32[4,64]{1,0:T(4,128)S(1)}, u32[]{:S(2)}, u32[]{:S(2)}) collective-permute-start(f32[4,64]{1,0:T(4,128)S(1)} %pad_maximum_fusion.1), channel_id=1, source_target_pairs={{0,4},{1,5},{2,6},{3,7},{4,0},{5,1},{6,2},{7,3},{8,12},{9,13},{10,... | collective-permute-start | bytes 3080 | tf_op jit(solution)/shard_map/ppermute | solution.py:129
  173.5 2.0 collective-permute-start.17
  174.2 1.4 collective-permute-start.16
  174.9 0.7 collective-permute-start.15
  175.6 2.6 %collective-permute-start.20 = (f32[1024]{0:T(1024)S(1)}, f32[1024]{0:T(1024)S(1)}, u32[]{:S(2)}, u32[]{:S(2)}) collective-permute-start(f32[1024]{0:T(1024)S(1)} %add_add_fusion.1), channel_id=1, source_target_pairs={{192,64},{208,48},{224,32},{240,16},{256,464},{272,480},{288,496},... | collective-permute-start | bytes 12296 | tf_op jit(solution)/shard_map/ppermute | solution.py:141
  176.2 67.8 %collective-permute-start.19 = (f32[1024]{0:T(1024)S(1)}, f32[1024]{0:T(1024)S(1)}, u32[]{:S(2)}, u32[]{:S(2)}) collective-permute-start(f32[1024]{0:T(1024)S(1)} %add_add_fusion.1), channel_id=1, source_target_pairs={{192,128},{208,112},{224,96},{240,80},{256,400},{272,416},{288,432... | collective-permute-start | bytes 12296 | tf_op jit(solution)/shard_map/ppermute | solution.py:141
  177.5 66.5 %collective-permute-start.18 = (f32[1024]{0:T(1024)S(1)}, f32[1024]{0:T(1024)S(1)}, u32[]{:S(2)}, u32[]{:S(2)}) collective-permute-start(f32[1024]{0:T(1024)S(1)} %add_add_fusion.1), channel_id=1, source_target_pairs={{192,176},{208,160},{224,144},{240,320},{256,336},{272,352},{288,3... | collective-permute-start | bytes 12296 | tf_op jit(solution)/shard_map/ppermute | solution.py:141
Sparse Core Ops, SparseCore 0:
  9.5 47.4 all-gather.3

commit v4 on v2

--- a/solution.py
+++ b/solution.py
@@ -33,7 +33,6 @@
     gathered = lax.all_gather(packed, "sec", axis=0, tiled=False)
     nsec = gathered.shape[0]
     body = local_states * width
-    site_blocks = gathered[:, :body].reshape(nsec, local_states, width, width)
     lefts = gathered[:, body]
     rights = gathered[:, body + 1]
 
@@ -58,12 +57,14 @@
         jnp.float32
     )
 
-    oriented = lax.cond(
-        is_left,
-        lambda b: b,
-        lambda b: jnp.swapaxes(b, 2, 3),
-        site_blocks,
-    )
+    def arrange(transpose):
+        def build(rows_all):
+            site_blocks = rows_all[:, :body].reshape(nsec, local_states, width, width)
+            return jnp.swapaxes(site_blocks, 2, 3) if transpose else site_blocks
+
+        return build
+
+    oriented = lax.cond(is_left, arrange(False), arrange(True), gathered)
 
     def apply(vector):
         spread = vector[:, None, :] * sector_hot[:, :, None]
@@ -91,23 +92,9 @@
     at_meet = (seg_index == low) | (seg_index == high)
     amp = jnp.where(at_meet, amp, jnp.zeros_like(amp))
 
-    pieces = amp[None, :]
-    span = 1
-    while span < sec_count:
-        own_slot = (sec_index // span) % 4
-        parts = [pieces]
-        for t in (1, 2, 3):
-            pairs = [(i, i ^ (t * span)) for i in range(sec_count)]
-            parts.append(lax.ppermute(pieces, "sec", pairs))
-        slots = []
-        for r in range(4):
-            chosen = jnp.zeros_like(pieces)
-            for t in range(4):
-                chosen = chosen + jnp.where(own_slot ^ t == r, parts[t], jnp.zeros_like(pieces))
-            slots.append(chosen)
-        pieces = jnp.concatenate(slots, axis=0)
-        span *= 4
-    full = pieces.reshape(conf_count)
+    tile = jnp.zeros((8, width), jnp.float32).at[0, :group].set(amp)
+    tiles = lax.all_gather(tile, "sec", axis=0, tiled=False)
+    full = tiles[:, 0, :group].reshape(conf_count)
 
     def outward(offset, holders):
         pairs = []

time: 244 us -> 233 us (0.955)
  starting transfers between devices: 115 us -> 80.3 us
  blocking collectives: 31.5 us -> 63.5 us
  waiting for transfers between devices: 55.7 us -> 47.2 us
    ppermute x6 -> x0, starting transfers between devices: 35.1 us -> none  [per_device(): parts.append(lax.ppermute(pieces, 'sec', pairs))]
    all_gather x0 -> x1, blocking collectives: none -> 32 us  [per_device(): tiles = lax.all_gather(tile, 'sec', axis=0, tiled=False)]
    ppermute x6 -> x0, waiting for transfers between devices: 4.62 us -> none  [per_device(): parts.append(lax.ppermute(pieces, 'sec', pairs))]
    ppermute x6, waiting for transfers between devices: 22.2 us -> 18.3 us  [exchange_rounds(): total = total + lax.ppermute(value, axis, pairs)]
  transfers between devices with their start and end apart: 29 -> 23, of which waited for: 20 -> 17; matrix products, arithmetic and copies ran while one was open for 1% -> 1% of each run, Pallas kernels for 0% -> 0%
where the time goes in v4:
time: 233 us; the launch traced here: 230 us
  starting transfers between devices  80.3 us (34%)
  blocking collectives  63.5 us (27%)
  waiting for transfers between devices  47.2 us (20%)
  between operations  13.8 us (6%)
  matrix products  12 us (5%)
  local copies, waits for them, and re-layouts  9.19 us (4%)
  other arithmetic  4.19 us (2%)
    ppermute x15, starting transfers between devices, per_device(): vector = lax.ppermute(vector, 'seg', chain)  75 us
    all_gather x1, blocking collectives, per_device(): tiles = lax.all_gather(tile, 'sec', axis=0, tiled=False)  32 us
    all_gather x1, blocking collectives, per_device(): occ_group = lax.all_gather(occ_mine, 'seg', axis=1, tiled=True)  31.5 us
    ppermute x6, waiting for transfers between devices, exchange_rounds(): total = total + lax.ppermute(value, axis, pairs)  18.3 us
    all_gather x1, waiting for transfers between devices, per_device(): gathered = lax.all_gather(packed, 'sec', axis=0, tiled=False)  16.1 us
    ppermute x15, waiting for transfers between devices, per_device(): vector = lax.ppermute(vector, 'seg', chain)  12.8 us
    dot_general x16, matrix products, apply(): jnp.einsum('kqa,qnab->knb', spread, oriented, preferred_element_type=jnp....  12 us
  transfers between devices with their start and end apart: 23, of which 17 were waited for; matrix products, arithmetic and copies ran while one was open for 1% of the time, Pallas kernels for 0%

profile of v4, /device:TPU:1, one launch (start us, length us, event | category | flops | bytes accessed | tf_op | source)
XLA Modules:
  0.0 230.2 jit_solution(6304477805895355106)
XLA Ops:
  6.6 1.7 maximum_maximum_fusion
  9.1 31.5 %all-gather.1 = s32[32,1,64]{2,1,0:T(1,128)S(1)} all-gather(s32[1,1,64]{2,1,0:T(1,128)S(1)} %get-tuple-element.33), channel_id=1, replica_groups=mesh['seg'=32,'sec'=16] {'seg'}, dimensions={0}, use_global_device_ids=true | all-gather | bytes 8448 | tf_op jit(solution)/shard_map/all_gather | solution.py:41
  42.3 16.1 %all-gather.4.cloned.1.call-done = bf16[8448,128]{1,0:T(8,128)(2,1)} async-done(((bf16[528,128]{1,0:T(8,128)(2,1)}), bf16[8448,128]{1,0:T(8,128)(2,1)}) %all-gather.4.cloned.1.call-update) | async-done | bytes 2162704 | tf_op jit(solution)/shard_map/all_gather | solution.py:33
  59.3 6.2 %conditional.1 = (bf16[16,4,128,128]{2,3,0,1:T(8,128)(2,1)S(1)}) conditional(s32[]{:T(128)} %convert_element_type.72, bf16[16,528,128]{2,1,0:T(8,128)(2,1)} %bitcast.196, bf16[16,528,128]{2,1,0:T(8,128)(2,1)} %bitcast.197), branch_computations={%region_2.4_spmd, %region_3.5_spmd} | conditional | bytes 10485792 | solution.py:67
  59.3 3.1 %slice.27 = bf16[16,512,128]{2,1,0:T(8,128)(2,1)} slice(bf16[16,528,128]{2,1,0:T(8,128)(2,1)} %param.5), slice={[0:16], [0:512], [0:128]} | slice | bytes 4194304 | tf_op jit(solution)/shard_map/cond/branch_1_fun/slice | solution.py:62
  62.4 3.0 %copy.101 = bf16[16,4,128,128]{2,3,0,1:T(8,128)(2,1)S(1)} copy(bf16[16,4,128,128]{3,2,1,0:T(8,128)(2,1)} %bitcast.199) | data formatting | bytes 4194304 | tf_op jit(solution)/shard_map/cond | solution.py:67
  67.6 3.1 %collective-permute-start = (bf16[64,128]{1,0:T(8,128)(2,1)S(1)}, bf16[64,128]{1,0:T(8,128)(2,1)S(1)}, u32[]{:S(2)}, u32[]{:S(2)}) collective-permute-start(bf16[64,128]{1,0:T(8,128)(2,1)S(1)} %fusion.31), channel_id=1, source_target_pairs={{0,16},{16,32},{32,48},{48,64},{64,80},{80,96},{96,112},{112,128},... | collective-permute-start | bytes 49160 | tf_op jit(solution)/shard_map/ppermute | solution.py:87
  72.3 3.6 %collective-permute-start.1 = (bf16[64,128]{1,0:T(8,128)(2,1)S(1)}, bf16[64,128]{1,0:T(8,128)(2,1)S(1)}, u32[]{:S(2)}, u32[]{:S(2)}) collective-permute-start(bf16[64,128]{1,0:T(8,128)(2,1)S(1)} %fusion.30), channel_id=1, source_target_pairs={{0,16},{16,32},{32,48},{48,64},{64,80},{80,96},{96,112},{112,128},... | collective-permute-start | bytes 49160 | tf_op jit(solution)/shard_map/ppermute | solution.py:87
  77.6 3.6 %collective-permute-start.2 = (bf16[64,128]{1,0:T(8,128)(2,1)S(1)}, bf16[64,128]{1,0:T(8,128)(2,1)S(1)}, u32[]{:S(2)}, u32[]{:S(2)}) collective-permute-start(bf16[64,128]{1,0:T(8,128)(2,1)S(1)} %fusion.29), channel_id=1, source_target_pairs={{0,16},{16,32},{32,48},{48,64},{64,80},{80,96},{96,112},{112,128},... | collective-permute-start | bytes 49160 | tf_op jit(solution)/shard_map/ppermute | solution.py:87
  82.8 3.6 %collective-permute-start.3 = (bf16[64,128]{1,0:T(8,128)(2,1)S(1)}, bf16[64,128]{1,0:T(8,128)(2,1)S(1)}, u32[]{:S(2)}, u32[]{:S(2)}) collective-permute-start(bf16[64,128]{1,0:T(8,128)(2,1)S(1)} %fusion.28), channel_id=1, source_target_pairs={{0,16},{16,32},{32,48},{48,64},{64,80},{80,96},{96,112},{112,128},... | collective-permute-start | bytes 49160 | tf_op jit(solution)/shard_map/ppermute | solution.py:87
  88.0 3.7 %collective-permute-start.4 = (bf16[64,128]{1,0:T(8,128)(2,1)S(1)}, bf16[64,128]{1,0:T(8,128)(2,1)S(1)}, u32[]{:S(2)}, u32[]{:S(2)}) collective-permute-start(bf16[64,128]{1,0:T(8,128)(2,1)S(1)} %fusion.27), channel_id=1, source_target_pairs={{0,16},{16,32},{32,48},{48,64},{64,80},{80,96},{96,112},{112,128},... | collective-permute-start | bytes 49160 | tf_op jit(solution)/shard_map/ppermute | solution.py:87
  93.4 5.7 %collective-permute-start.5 = (bf16[64,128]{1,0:T(8,128)(2,1)S(1)}, bf16[64,128]{1,0:T(8,128)(2,1)S(1)}, u32[]{:S(2)}, u32[]{:S(2)}) collective-permute-start(bf16[64,128]{1,0:T(8,128)(2,1)S(1)} %fusion.26), channel_id=1, source_target_pairs={{0,16},{16,32},{32,48},{48,64},{64,80},{80,96},{96,112},{112,128},... | collective-permute-start | bytes 49160 | tf_op jit(solution)/shard_map/ppermute | solution.py:87
  100.7 5.7 %collective-permute-start.6 = (bf16[64,128]{1,0:T(8,128)(2,1)S(1)}, bf16[64,128]{1,0:T(8,128)(2,1)S(1)}, u32[]{:S(2)}, u32[]{:S(2)}) collective-permute-start(bf16[64,128]{1,0:T(8,128)(2,1)S(1)} %fusion.25), channel_id=1, source_target_pairs={{0,16},{16,32},{32,48},{48,64},{64,80},{80,96},{96,112},{112,128},... | collective-permute-start | bytes 49160 | tf_op jit(solution)/shard_map/ppermute | solution.py:87
  108.1 5.7 %collective-permute-start.7 = (bf16[64,128]{1,0:T(8,128)(2,1)S(1)}, bf16[64,128]{1,0:T(8,128)(2,1)S(1)}, u32[]{:S(2)}, u32[]{:S(2)}) collective-permute-start(bf16[64,128]{1,0:T(8,128)(2,1)S(1)} %fusion.24), channel_id=1, source_target_pairs={{0,16},{16,32},{32,48},{48,64},{64,80},{80,96},{96,112},{112,128},... | collective-permute-start | bytes 49160 | tf_op jit(solution)/shard_map/ppermute | solution.py:87
  115.4 5.7 %collective-permute-start.8 = (bf16[64,128]{1,0:T(8,128)(2,1)S(1)}, bf16[64,128]{1,0:T(8,128)(2,1)S(1)}, u32[]{:S(2)}, u32[]{:S(2)}) collective-permute-start(bf16[64,128]{1,0:T(8,128)(2,1)S(1)} %fusion.23), channel_id=1, source_target_pairs={{0,16},{16,32},{32,48},{48,64},{64,80},{80,96},{96,112},{112,128},... | collective-permute-start | bytes 49160 | tf_op jit(solution)/shard_map/ppermute | solution.py:87
  122.8 5.7 %collective-permute-start.9 = (bf16[64,128]{1,0:T(8,128)(2,1)S(1)}, bf16[64,128]{1,0:T(8,128)(2,1)S(1)}, u32[]{:S(2)}, u32[]{:S(2)}) collective-permute-start(bf16[64,128]{1,0:T(8,128)(2,1)S(1)} %fusion.22), channel_id=1, source_target_pairs={{0,16},{16,32},{32,48},{48,64},{64,80},{80,96},{96,112},{112,128},... | collective-permute-start | bytes 49160 | tf_op jit(solution)/shard_map/ppermute | solution.py:87
  130.1 5.7 %collective-permute-start.10 = (bf16[64,128]{1,0:T(8,128)(2,1)S(1)}, bf16[64,128]{1,0:T(8,128)(2,1)S(1)}, u32[]{:S(2)}, u32[]{:S(2)}) collective-permute-start(bf16[64,128]{1,0:T(8,128)(2,1)S(1)} %fusion.21), channel_id=1, source_target_pairs={{0,16},{16,32},{32,48},{48,64},{64,80},{80,96},{96,112},{112,128},... | collective-permute-start | bytes 49160 | tf_op jit(solution)/shard_map/ppermute | solution.py:87
  137.5 5.7 %collective-permute-start.11 = (bf16[64,128]{1,0:T(8,128)(2,1)S(1)}, bf16[64,128]{1,0:T(8,128)(2,1)S(1)}, u32[]{:S(2)}, u32[]{:S(2)}) collective-permute-start(bf16[64,128]{1,0:T(8,128)(2,1)S(1)} %fusion.20), channel_id=1, source_target_pairs={{0,16},{16,32},{32,48},{48,64},{64,80},{80,96},{96,112},{112,128},... | collective-permute-start | bytes 49160 | tf_op jit(solution)/shard_map/ppermute | solution.py:87
  144.8 5.7 %collective-permute-start.12 = (bf16[64,128]{1,0:T(8,128)(2,1)S(1)}, bf16[64,128]{1,0:T(8,128)(2,1)S(1)}, u32[]{:S(2)}, u32[]{:S(2)}) collective-permute-start(bf16[64,128]{1,0:T(8,128)(2,1)S(1)} %fusion.19), channel_id=1, source_target_pairs={{0,16},{16,32},{32,48},{48,64},{64,80},{80,96},{96,112},{112,128},... | collective-permute-start | bytes 49160 | tf_op jit(solution)/shard_map/ppermute | solution.py:87
  152.2 5.7 %collective-permute-start.13 = (bf16[64,128]{1,0:T(8,128)(2,1)S(1)}, bf16[64,128]{1,0:T(8,128)(2,1)S(1)}, u32[]{:S(2)}, u32[]{:S(2)}) collective-permute-start(bf16[64,128]{1,0:T(8,128)(2,1)S(1)} %fusion.18), channel_id=1, source_target_pairs={{0,16},{16,32},{32,48},{48,64},{64,80},{80,96},{96,112},{112,128},... | collective-permute-start | bytes 49160 | tf_op jit(solution)/shard_map/ppermute | solution.py:87
  159.5 5.7 %collective-permute-start.14 = (bf16[64,128]{1,0:T(8,128)(2,1)S(1)}, bf16[64,128]{1,0:T(8,128)(2,1)S(1)}, u32[]{:S(2)}, u32[]{:S(2)}) collective-permute-start(bf16[64,128]{1,0:T(8,128)(2,1)S(1)} %fusion.17), channel_id=1, source_target_pairs={{0,16},{16,32},{32,48},{48,64},{64,80},{80,96},{96,112},{112,128},... | collective-permute-start | bytes 49160 | tf_op jit(solution)/shard_map/ppermute | solution.py:87
  167.7 32.0 %all_gather.22 = f32[16,8,128]{2,1,0:T(8,128)S(1)} all-gather(f32[1,8,128]{2,1,0:T(8,128)S(1)} %scatter.4), channel_id=1, replica_groups=mesh['seg'=32,'sec'=16] {'sec'}, dimensions={0}, use_global_device_ids=true | all-gather | bytes 69632 | tf_op jit(solution)/shard_map/all_gather | solution.py:96
  201.8 1.3 collective-permute-start.21
  204.5 18.3 %collective-permute-done.21 = f32[1024]{0:T(1024)S(1)} collective-permute-done((f32[1024]{0:T(1024)S(1)}, f32[1024]{0:T(1024)S(1)}, u32[]{:S(2)}, u32[]{:S(2)}) %collective-permute-start.21) | collective-permute-done | bytes 4128 | tf_op jit(solution)/shard_map/ppermute | solution.py:11
  (67 shorter events, 34.3 us)
Async XLA Ops:
  6.5 51.9 %all-gather.4.cloned.1.call-start = ((), (), s32[]{:S(2)}) async-start(), calls=%async_computation | async-start | bytes 2297856 | tf_op jit(solution)/shard_map/all_gather | solution.py:33
  67.6 4.0 %collective-permute-start = (bf16[64,128]{1,0:T(8,128)(2,1)S(1)}, bf16[64,128]{1,0:T(8,128)(2,1)S(1)}, u32[]{:S(2)}, u32[]{:S(2)}) collective-permute-start(bf16[64,128]{1,0:T(8,128)(2,1)S(1)} %fusion.31), channel_id=1, source_target_pairs={{0,16},{16,32},{32,48},{48,64},{64,80},{80,96},{96,112},{112,128},... | collective-permute-start | bytes 49160 | tf_op jit(solution)/shard_map/ppermute | solution.py:87
  72.3 4.5 %collective-permute-start.1 = (bf16[64,128]{1,0:T(8,128)(2,1)S(1)}, bf16[64,128]{1,0:T(8,128)(2,1)S(1)}, u32[]{:S(2)}, u32[]{:S(2)}) collective-permute-start(bf16[64,128]{1,0:T(8,128)(2,1)S(1)} %fusion.30), channel_id=1, source_target_pairs={{0,16},{16,32},{32,48},{48,64},{64,80},{80,96},{96,112},{112,128},... | collective-permute-start | bytes 49160 | tf_op jit(solution)/shard_map/ppermute | solution.py:87
  77.6 4.5 %collective-permute-start.2 = (bf16[64,128]{1,0:T(8,128)(2,1)S(1)}, bf16[64,128]{1,0:T(8,128)(2,1)S(1)}, u32[]{:S(2)}, u32[]{:S(2)}) collective-permute-start(bf16[64,128]{1,0:T(8,128)(2,1)S(1)} %fusion.29), channel_id=1, source_target_pairs={{0,16},{16,32},{32,48},{48,64},{64,80},{80,96},{96,112},{112,128},... | collective-permute-start | bytes 49160 | tf_op jit(solution)/shard_map/ppermute | solution.py:87
  82.8 4.5 %collective-permute-start.3 = (bf16[64,128]{1,0:T(8,128)(2,1)S(1)}, bf16[64,128]{1,0:T(8,128)(2,1)S(1)}, u32[]{:S(2)}, u32[]{:S(2)}) collective-permute-start(bf16[64,128]{1,0:T(8,128)(2,1)S(1)} %fusion.28), channel_id=1, source_target_pairs={{0,16},{16,32},{32,48},{48,64},{64,80},{80,96},{96,112},{112,128},... | collective-permute-start | bytes 49160 | tf_op jit(solution)/shard_map/ppermute | solution.py:87
  88.0 4.6 %collective-permute-start.4 = (bf16[64,128]{1,0:T(8,128)(2,1)S(1)}, bf16[64,128]{1,0:T(8,128)(2,1)S(1)}, u32[]{:S(2)}, u32[]{:S(2)}) collective-permute-start(bf16[64,128]{1,0:T(8,128)(2,1)S(1)} %fusion.27), channel_id=1, source_target_pairs={{0,16},{16,32},{32,48},{48,64},{64,80},{80,96},{96,112},{112,128},... | collective-permute-start | bytes 49160 | tf_op jit(solution)/shard_map/ppermute | solution.py:87
  93.4 6.6 %collective-permute-start.5 = (bf16[64,128]{1,0:T(8,128)(2,1)S(1)}, bf16[64,128]{1,0:T(8,128)(2,1)S(1)}, u32[]{:S(2)}, u32[]{:S(2)}) collective-permute-start(bf16[64,128]{1,0:T(8,128)(2,1)S(1)} %fusion.26), channel_id=1, source_target_pairs={{0,16},{16,32},{32,48},{48,64},{64,80},{80,96},{96,112},{112,128},... | collective-permute-start | bytes 49160 | tf_op jit(solution)/shard_map/ppermute | solution.py:87
  100.7 6.6 %collective-permute-start.6 = (bf16[64,128]{1,0:T(8,128)(2,1)S(1)}, bf16[64,128]{1,0:T(8,128)(2,1)S(1)}, u32[]{:S(2)}, u32[]{:S(2)}) collective-permute-start(bf16[64,128]{1,0:T(8,128)(2,1)S(1)} %fusion.25), channel_id=1, source_target_pairs={{0,16},{16,32},{32,48},{48,64},{64,80},{80,96},{96,112},{112,128},... | collective-permute-start | bytes 49160 | tf_op jit(solution)/shard_map/ppermute | solution.py:87
  108.1 6.6 %collective-permute-start.7 = (bf16[64,128]{1,0:T(8,128)(2,1)S(1)}, bf16[64,128]{1,0:T(8,128)(2,1)S(1)}, u32[]{:S(2)}, u32[]{:S(2)}) collective-permute-start(bf16[64,128]{1,0:T(8,128)(2,1)S(1)} %fusion.24), channel_id=1, source_target_pairs={{0,16},{16,32},{32,48},{48,64},{64,80},{80,96},{96,112},{112,128},... | collective-permute-start | bytes 49160 | tf_op jit(solution)/shard_map/ppermute | solution.py:87
  115.4 6.6 %collective-permute-start.8 = (bf16[64,128]{1,0:T(8,128)(2,1)S(1)}, bf16[64,128]{1,0:T(8,128)(2,1)S(1)}, u32[]{:S(2)}, u32[]{:S(2)}) collective-permute-start(bf16[64,128]{1,0:T(8,128)(2,1)S(1)} %fusion.23), channel_id=1, source_target_pairs={{0,16},{16,32},{32,48},{48,64},{64,80},{80,96},{96,112},{112,128},... | collective-permute-start | bytes 49160 | tf_op jit(solution)/shard_map/ppermute | solution.py:87
  122.8 6.6 %collective-permute-start.9 = (bf16[64,128]{1,0:T(8,128)(2,1)S(1)}, bf16[64,128]{1,0:T(8,128)(2,1)S(1)}, u32[]{:S(2)}, u32[]{:S(2)}) collective-permute-start(bf16[64,128]{1,0:T(8,128)(2,1)S(1)} %fusion.22), channel_id=1, source_target_pairs={{0,16},{16,32},{32,48},{48,64},{64,80},{80,96},{96,112},{112,128},... | collective-permute-start | bytes 49160 | tf_op jit(solution)/shard_map/ppermute | solution.py:87
  130.1 6.6 %collective-permute-start.10 = (bf16[64,128]{1,0:T(8,128)(2,1)S(1)}, bf16[64,128]{1,0:T(8,128)(2,1)S(1)}, u32[]{:S(2)}, u32[]{:S(2)}) collective-permute-start(bf16[64,128]{1,0:T(8,128)(2,1)S(1)} %fusion.21), channel_id=1, source_target_pairs={{0,16},{16,32},{32,48},{48,64},{64,80},{80,96},{96,112},{112,128},... | collective-permute-start | bytes 49160 | tf_op jit(solution)/shard_map/ppermute | solution.py:87
  137.5 6.6 %collective-permute-start.11 = (bf16[64,128]{1,0:T(8,128)(2,1)S(1)}, bf16[64,128]{1,0:T(8,128)(2,1)S(1)}, u32[]{:S(2)}, u32[]{:S(2)}) collective-permute-start(bf16[64,128]{1,0:T(8,128)(2,1)S(1)} %fusion.20), channel_id=1, source_target_pairs={{0,16},{16,32},{32,48},{48,64},{64,80},{80,96},{96,112},{112,128},... | collective-permute-start | bytes 49160 | tf_op jit(solution)/shard_map/ppermute | solution.py:87
  144.8 6.6 %collective-permute-start.12 = (bf16[64,128]{1,0:T(8,128)(2,1)S(1)}, bf16[64,128]{1,0:T(8,128)(2,1)S(1)}, u32[]{:S(2)}, u32[]{:S(2)}) collective-permute-start(bf16[64,128]{1,0:T(8,128)(2,1)S(1)} %fusion.19), channel_id=1, source_target_pairs={{0,16},{16,32},{32,48},{48,64},{64,80},{80,96},{96,112},{112,128},... | collective-permute-start | bytes 49160 | tf_op jit(solution)/shard_map/ppermute | solution.py:87
  152.2 6.6 %collective-permute-start.13 = (bf16[64,128]{1,0:T(8,128)(2,1)S(1)}, bf16[64,128]{1,0:T(8,128)(2,1)S(1)}, u32[]{:S(2)}, u32[]{:S(2)}) collective-permute-start(bf16[64,128]{1,0:T(8,128)(2,1)S(1)} %fusion.18), channel_id=1, source_target_pairs={{0,16},{16,32},{32,48},{48,64},{64,80},{80,96},{96,112},{112,128},... | collective-permute-start | bytes 49160 | tf_op jit(solution)/shard_map/ppermute | solution.py:87
  159.5 6.6 %collective-permute-start.14 = (bf16[64,128]{1,0:T(8,128)(2,1)S(1)}, bf16[64,128]{1,0:T(8,128)(2,1)S(1)}, u32[]{:S(2)}, u32[]{:S(2)}) collective-permute-start(bf16[64,128]{1,0:T(8,128)(2,1)S(1)} %fusion.17), channel_id=1, source_target_pairs={{0,16},{16,32},{32,48},{48,64},{64,80},{80,96},{96,112},{112,128},... | collective-permute-start | bytes 49160 | tf_op jit(solution)/shard_map/ppermute | solution.py:87
  166.9 0.7 collective-permute-start.15
  199.8 2.0 collective-permute-start.18
  200.5 1.4 collective-permute-start.17
  201.1 0.7 collective-permute-start.16
  201.8 20.9 %collective-permute-start.21 = (f32[1024]{0:T(1024)S(1)}, f32[1024]{0:T(1024)S(1)}, u32[]{:S(2)}, u32[]{:S(2)}) collective-permute-start(f32[1024]{0:T(1024)S(1)} %add_add_fusion.1), channel_id=1, source_target_pairs={{192,0},{208,16},{224,32},{240,48},{256,448},{272,464},{288,480},{... | collective-permute-start | bytes 12296 | tf_op jit(solution)/shard_map/ppermute | solution.py:11
  203.1 19.6 %collective-permute-start.20 = (f32[1024]{0:T(1024)S(1)}, f32[1024]{0:T(1024)S(1)}, u32[]{:S(2)}, u32[]{:S(2)}) collective-permute-start(f32[1024]{0:T(1024)S(1)} %add_add_fusion.1), channel_id=1, source_target_pairs={{192,64},{208,80},{224,96},{240,112},{256,384},{272,400},{288,416}... | collective-permute-start | bytes 12296 | tf_op jit(solution)/shard_map/ppermute | solution.py:11
  203.8 18.9 %collective-permute-start.19 = (f32[1024]{0:T(1024)S(1)}, f32[1024]{0:T(1024)S(1)}, u32[]{:S(2)}, u32[]{:S(2)}) collective-permute-start(f32[1024]{0:T(1024)S(1)} %add_add_fusion.1), channel_id=1, source_target_pairs={{192,128},{208,144},{224,160},{240,176},{256,320},{272,336},{288,3... | collective-permute-start | bytes 12296 | tf_op jit(solution)/shard_map/ppermute | solution.py:11
Sparse Core Ops, SparseCore 0:
  9.5 48.9 all-gather.3

commit v5 on v4

--- a/solution.py
+++ b/solution.py
@@ -78,13 +78,11 @@
     first = jnp.where(is_left, first_left, first_right)
     vector = jnp.where(depth == 0, first, jnp.zeros_like(first))
 
-    chain = [(j, j + 1) for j in range(half_count - 1)] + [
-        (j, j - 1) for j in range(half_count + 1, seg_count)
-    ]
     for step in range(half_count):
         vector = apply(vector)
         if step < half_count - 1:
-            vector = lax.ppermute(vector, "seg", chain)
+            hop = [(step, step + 1), (seg_count - 1 - step, seg_count - 2 - step)]
+            vector = lax.ppermute(vector, "seg", hop)
 
     low, high = half_count - 1, half_count
     other = lax.ppermute(vector, "seg", [(low, high), (high, low)])

time: 233 us -> 187 us (0.80)
  starting transfers between devices: 80.3 us -> 17.6 us
  waiting for transfers between devices: 47.2 us -> 79.1 us
  blocking collectives: 63.5 us -> 48.2 us
    ppermute x15, starting transfers between devices: 75 us -> 12.4 us  [per_device(): vector = lax.ppermute(vector, 'seg', hop)]
    ppermute x6, waiting for transfers between devices: 18.3 us -> 62.1 us  [exchange_rounds(): total = total + lax.ppermute(value, axis, pairs)]
    all_gather x1, blocking collectives: 32 us -> 16.6 us  [per_device(): tiles = lax.all_gather(tile, 'sec', axis=0, tiled=False)]
    ppermute x15, waiting for transfers between devices: 12.8 us -> 0.89 us  [per_device(): vector = lax.ppermute(vector, 'seg', hop)]
  transfers between devices with their start and end apart: 23 -> 23, of which waited for: 17 -> 3; matrix products, arithmetic and copies ran while one was open for 1% -> 1% of each run, Pallas kernels for 0% -> 0%
where the time goes in v5:
time: 187 us; the launch traced here: 184 us
  waiting for transfers between devices  79.1 us (42%)
  blocking collectives  48.2 us (26%)
  starting transfers between devices  17.6 us (9%)
  between operations  13.9 us (7%)
  matrix products  12 us (6%)
  local copies, waits for them, and re-layouts  9.19 us (5%)
  other arithmetic  4.19 us (2%)
    ppermute x6, waiting for transfers between devices, exchange_rounds(): total = total + lax.ppermute(value, axis, pairs)  62.1 us
    all_gather x1, blocking collectives, per_device(): occ_group = lax.all_gather(occ_mine, 'seg', axis=1, tiled=True)  31.5 us
    all_gather x1, blocking collectives, per_device(): tiles = lax.all_gather(tile, 'sec', axis=0, tiled=False)  16.6 us
    all_gather x1, waiting for transfers between devices, per_device(): gathered = lax.all_gather(packed, 'sec', axis=0, tiled=False)  16.1 us
    ppermute x15, starting transfers between devices, per_device(): vector = lax.ppermute(vector, 'seg', hop)  12.4 us
    dot_general x16, matrix products, apply(): jnp.einsum('kqa,qnab->knb', spread, oriented, preferred_element_type=jnp....  12 us
    ppermute x6, starting transfers between devices, exchange_rounds(): total = total + lax.ppermute(value, axis, pairs)  4.59 us
  transfers between devices with their start and end apart: 23, of which 3 were waited for; matrix products, arithmetic and copies ran while one was open for 1% of the time, Pallas kernels for 0%

profile of v5, /device:TPU:1, one launch (start us, length us, event | category | flops | bytes accessed | tf_op | source)
XLA Modules:
  0.0 184.3 jit_solution(7585344226891393413)
XLA Ops:
  6.6 1.7 maximum_maximum_fusion
  9.1 31.5 %all-gather.1 = s32[32,1,64]{2,1,0:T(1,128)S(1)} all-gather(s32[1,1,64]{2,1,0:T(1,128)S(1)} %get-tuple-element.33), channel_id=1, replica_groups=mesh['seg'=32,'sec'=16] {'seg'}, dimensions={0}, use_global_device_ids=true | all-gather | bytes 8448 | tf_op jit(solution)/shard_map/all_gather | solution.py:41
  40.7 0.8 compare_and_fusion.1
  41.5 0.8 and_select_fusion
  42.3 16.1 %all-gather.4.cloned.1.call-done = bf16[8448,128]{1,0:T(8,128)(2,1)} async-done(((bf16[528,128]{1,0:T(8,128)(2,1)}), bf16[8448,128]{1,0:T(8,128)(2,1)}) %all-gather.4.cloned.1.call-update) | async-done | bytes 2162704 | tf_op jit(solution)/shard_map/all_gather | solution.py:33
  58.4 0.9 fusion.105
  59.3 6.2 %conditional.1 = (bf16[16,4,128,128]{2,3,0,1:T(8,128)(2,1)S(1)}) conditional(s32[]{:T(128)} %convert_element_type.72, bf16[16,528,128]{2,1,0:T(8,128)(2,1)} %bitcast.196, bf16[16,528,128]{2,1,0:T(8,128)(2,1)} %bitcast.197), branch_computations={%region_2.4_spmd, %region_3.5_spmd} | conditional | bytes 10485792 | solution.py:67
  59.3 3.1 %slice.27 = bf16[16,512,128]{2,1,0:T(8,128)(2,1)} slice(bf16[16,528,128]{2,1,0:T(8,128)(2,1)} %param.5), slice={[0:16], [0:512], [0:128]} | slice | bytes 4194304 | tf_op jit(solution)/shard_map/cond/branch_1_fun/slice | solution.py:62
  62.4 3.0 %copy.101 = bf16[16,4,128,128]{2,3,0,1:T(8,128)(2,1)S(1)} copy(bf16[16,4,128,128]{3,2,1,0:T(8,128)(2,1)} %bitcast.199) | data formatting | bytes 4194304 | tf_op jit(solution)/shard_map/cond | solution.py:67
  66.8 0.8 fusion.31
  67.6 3.1 %collective-permute-start = (bf16[64,128]{1,0:T(8,128)(2,1)S(1)}, bf16[64,128]{1,0:T(8,128)(2,1)S(1)}, u32[]{:S(2)}, u32[]{:S(2)}) collective-permute-start(bf16[64,128]{1,0:T(8,128)(2,1)S(1)} %fusion.31), channel_id=1, source_target_pairs={{0,16},{496,480},{1,17},{497,481},{2,18},{498,482},{3,19},{499,483... | collective-permute-start | bytes 49160 | tf_op jit(solution)/shard_map/ppermute | solution.py:85
  70.7 0.9 collective-permute-done
  74.4 0.8 fusion.28
  75.9 0.8 fusion.27
  77.3 0.8 fusion.26
  78.7 0.8 fusion.25
  80.2 0.8 fusion.24
  81.6 0.8 fusion.23
  83.1 0.8 fusion.22
  84.5 0.8 fusion.21
  85.9 0.8 fusion.20
  93.3 16.6 %all_gather.22 = f32[16,8,128]{2,1,0:T(8,128)S(1)} all-gather(f32[1,8,128]{2,1,0:T(8,128)S(1)} %scatter.4), channel_id=1, replica_groups=mesh['seg'=32,'sec'=16] {'sec'}, dimensions={0}, use_global_device_ids=true | all-gather | bytes 69632 | tf_op jit(solution)/shard_map/all_gather | solution.py:94
  112.1 1.3 collective-permute-start.21
  114.7 62.1 %collective-permute-done.21 = f32[1024]{0:T(1024)S(1)} collective-permute-done((f32[1024]{0:T(1024)S(1)}, f32[1024]{0:T(1024)S(1)}, u32[]{:S(2)}, u32[]{:S(2)}) %collective-permute-start.21) | collective-permute-done | bytes 4128 | tf_op jit(solution)/shard_map/ppermute | solution.py:11
  (67 shorter events, 20.9 us)
Async XLA Ops:
  6.5 51.9 %all-gather.4.cloned.1.call-start = ((), (), s32[]{:S(2)}) async-start(), calls=%async_computation | async-start | bytes 2297856 | tf_op jit(solution)/shard_map/all_gather | solution.py:33
  67.6 4.0 %collective-permute-start = (bf16[64,128]{1,0:T(8,128)(2,1)S(1)}, bf16[64,128]{1,0:T(8,128)(2,1)S(1)}, u32[]{:S(2)}, u32[]{:S(2)}) collective-permute-start(bf16[64,128]{1,0:T(8,128)(2,1)S(1)} %fusion.31), channel_id=1, source_target_pairs={{0,16},{496,480},{1,17},{497,481},{2,18},{498,482},{3,19},{499,483... | collective-permute-start | bytes 49160 | tf_op jit(solution)/shard_map/ppermute | solution.py:85
  72.3 0.7 collective-permute-start.1
  73.7 0.7 collective-permute-start.2
  75.2 0.7 collective-permute-start.3
  76.6 0.7 collective-permute-start.4
  78.1 0.7 collective-permute-start.5
  79.5 0.7 collective-permute-start.6
  80.9 0.7 collective-permute-start.7
  82.4 0.7 collective-permute-start.8
  83.8 0.7 collective-permute-start.9
  85.3 0.7 collective-permute-start.10
  86.7 0.7 collective-permute-start.11
  88.1 0.7 collective-permute-start.12
  89.6 0.7 collective-permute-start.13
  91.0 0.7 collective-permute-start.14
  92.5 0.7 collective-permute-start.15
  110.0 2.0 %collective-permute-start.18 = (f32[1024]{0:T(1024)S(1)}, f32[1024]{0:T(1024)S(1)}, u32[]{:S(2)}, u32[]{:S(2)}) collective-permute-start(f32[1024]{0:T(1024)S(1)} %reshape_squeeze.7), channel_id=1, source_target_pairs={{240,192},{256,304},{241,193},{257,305},{242,194},{258,306},{243,1... | collective-permute-start | bytes 12296 | tf_op jit(solution)/shard_map/ppermute | solution.py:11
  110.7 1.4 collective-permute-start.17
  111.4 0.7 collective-permute-start.16
  112.1 64.7 %collective-permute-start.21 = (f32[1024]{0:T(1024)S(1)}, f32[1024]{0:T(1024)S(1)}, u32[]{:S(2)}, u32[]{:S(2)}) collective-permute-start(f32[1024]{0:T(1024)S(1)} %add_add_fusion.1), channel_id=1, source_target_pairs={{192,0},{208,16},{224,32},{240,48},{256,448},{272,464},{288,480},{... | collective-permute-start | bytes 12296 | tf_op jit(solution)/shard_map/ppermute | solution.py:11
  113.4 63.5 %collective-permute-start.20 = (f32[1024]{0:T(1024)S(1)}, f32[1024]{0:T(1024)S(1)}, u32[]{:S(2)}, u32[]{:S(2)}) collective-permute-start(f32[1024]{0:T(1024)S(1)} %add_add_fusion.1), channel_id=1, source_target_pairs={{192,64},{208,80},{224,96},{240,112},{256,384},{272,400},{288,416}... | collective-permute-start | bytes 12296 | tf_op jit(solution)/shard_map/ppermute | solution.py:11
  114.1 62.8 %collective-permute-start.19 = (f32[1024]{0:T(1024)S(1)}, f32[1024]{0:T(1024)S(1)}, u32[]{:S(2)}, u32[]{:S(2)}) collective-permute-start(f32[1024]{0:T(1024)S(1)} %add_add_fusion.1), channel_id=1, source_target_pairs={{192,128},{208,144},{224,160},{240,176},{256,320},{272,336},{288,3... | collective-permute-start | bytes 12296 | tf_op jit(solution)/shard_map/ppermute | solution.py:11
Sparse Core Ops, SparseCore 0:
  9.5 48.9 all-gather.3

commit v6 on v5

--- a/solution.py
+++ b/solution.py
@@ -27,14 +27,16 @@
     width = blocks.shape[-1]
     local_states = blocks.shape[1]
 
-    rows = blocks[0, :, 0].reshape(local_states * width, width)
-    pad = jnp.zeros((14, width), blocks.dtype)
-    packed = jnp.concatenate([rows, left_edge, right_edge, pad], axis=0)
-    gathered = lax.all_gather(packed, "sec", axis=0, tiled=False)
-    nsec = gathered.shape[0]
-    body = local_states * width
-    lefts = gathered[:, body]
-    rights = gathered[:, body + 1]
+    local = blocks[0, :, 0]
+    local = jnp.where(is_left, local, jnp.swapaxes(local, 1, 2))
+    edges = jnp.concatenate(
+        [left_edge, right_edge, jnp.zeros((width - 2, width), blocks.dtype)], axis=0
+    )
+    packed = jnp.concatenate([local, edges[None]], axis=0)
+    oriented = lax.all_gather(packed, "sec", axis=0, tiled=False)
+    nsec = oriented.shape[0]
+    lefts = oriented[:, local_states, 0]
+    rights = oriented[:, local_states, 1]
 
     row0 = sec_index * group
     occ_mine = lax.dynamic_slice_in_dim(occupation, row0, group, axis=0)
@@ -53,18 +55,9 @@
     sector_hot = (sector_here[:, None] == jnp.arange(nsec, dtype=jnp.int32)[None, :]).astype(
         jnp.bfloat16
     )
-    state_hot = (occ_here[:, None] == jnp.arange(local_states, dtype=jnp.int32)[None, :]).astype(
+    state_hot = (occ_here[:, None] == jnp.arange(local_states + 1, dtype=jnp.int32)[None, :]).astype(
         jnp.float32
     )
-
-    def arrange(transpose):
-        def build(rows_all):
-            site_blocks = rows_all[:, :body].reshape(nsec, local_states, width, width)
-            return jnp.swapaxes(site_blocks, 2, 3) if transpose else site_blocks
-
-        return build
-
-    oriented = lax.cond(is_left, arrange(False), arrange(True), gathered)
 
     def apply(vector):
         spread = vector[:, None, :] * sector_hot[:, :, None]

time: 187 us -> 182 us (0.973)
  local copies, waits for them, and re-layouts: 9.19 us -> 4.16 us
    cond x1 -> x0, local copies, waits for them, and re-layouts: 3.03 us -> none  [per_device(): oriented = lax.cond(is_left, arrange(False), arrange(True), gathered)]
    slice x2 -> x1, local copies, waits for them, and re-layouts: 3.97 us -> 0.94 us  [per_device(): lefts = oriented[:, local_states, 0]]
where the time goes in v6:
time: 182 us; the launch traced here: 179 us
  waiting for transfers between devices  78.1 us (43%)
  blocking collectives  48.6 us (27%)
  starting transfers between devices  17.7 us (10%)
  between operations  13.9 us (8%)
  matrix products  11.7 us (6%)
  other arithmetic  4.82 us (3%)
  local copies, waits for them, and re-layouts  4.16 us (2%)
    ppermute x6, waiting for transfers between devices, exchange_rounds(): total = total + lax.ppermute(value, axis, pairs)  62.1 us
    all_gather x1, blocking collectives, per_device(): occ_group = lax.all_gather(occ_mine, 'seg', axis=1, tiled=True)  31.7 us
    all_gather x1, blocking collectives, per_device(): tiles = lax.all_gather(tile, 'sec', axis=0, tiled=False)  16.8 us
    all_gather x1, waiting for transfers between devices, per_device(): oriented = lax.all_gather(packed, 'sec', axis=0, tiled=False)  15.2 us
    ppermute x15, starting transfers between devices, per_device(): vector = lax.ppermute(vector, 'seg', hop)  12.4 us
    dot_general x16, matrix products, apply(): jnp.einsum('kqa,qnab->knb', spread, oriented, preferred_element_type=jnp....  11.7 us
    ppermute x6, starting transfers between devices, exchange_rounds(): total = total + lax.ppermute(value, axis, pairs)  4.59 us
  transfers between devices with their start and end apart: 23, of which 3 were waited for; matrix products, arithmetic and copies ran while one was open for 1% of the time, Pallas kernels for 0%

profile of v6, /device:TPU:1, one launch (start us, length us, event | category | flops | bytes accessed | tf_op | source)
XLA Modules:
  0.0 178.9 jit_solution(2923225929021777702)
XLA Ops:
  6.5 1.0 copy.29
  7.7 0.9 bitcast_select_fusion
  8.6 0.8 maximum_bitcast_fusion
  9.3 0.7 pad_maximum_fusion
  10.1 0.7 fusion.103
  10.8 31.7 %all-gather.1 = s32[32,1,64]{2,1,0:T(1,128)S(1)} all-gather(s32[1,1,64]{2,1,0:T(1,128)S(1)} %get-tuple-element.27), channel_id=1, replica_groups=mesh['seg'=32,'sec'=16] {'seg'}, dimensions={0}, use_global_device_ids=true | all-gather | bytes 8448 | tf_op jit(solution)/shard_map/all_gather | solution.py:43
  42.6 0.8 compare_and_fusion.1
  43.4 0.8 and_select_fusion
  44.2 15.2 %all-gather.4.cloned.1.call-done = bf16[80,128,128]{2,1,0:T(8,128)(2,1)} async-done(((bf16[5,128,128]{2,1,0:T(8,128)(2,1)}), bf16[80,128,128]{2,1,0:T(8,128)(2,1)}) %all-gather.4.cloned.1.call-update) | async-done | bytes 2621456 | tf_op jit(solution)/shard_map/all_gather | solution.py:36
  59.4 0.9 fusion.105
  61.7 2.4 %fusion.16 = bf16[64,128]{1,0:T(8,128)(2,1)S(1)} fusion(bf16[16,5,128,128]{3,2,1,0:T(8,128)(2,1)} %bitcast.263, bf16[64,16]{0,1:T(8,128)(2,1)S(1)} %fusion.97, bf16[64,128]{1,0:T(8,128)(2,1)S(1)} %fusion.96, f32[64,5]{0,1:T(8,128)S(1)} %fusion.99), kind=kOutput, calls=%fused_computation.34 | convolution fusion | flops 168370176 | bytes 2657536 | tf_op jit(solution)/shard_map/kqa,qnab->knb/dot_general | solution.py:64
  64.1 3.1 %collective-permute-start = (bf16[64,128]{1,0:T(8,128)(2,1)S(1)}, bf16[64,128]{1,0:T(8,128)(2,1)S(1)}, u32[]{:S(2)}, u32[]{:S(2)}) collective-permute-start(bf16[64,128]{1,0:T(8,128)(2,1)S(1)} %fusion.16), channel_id=1, source_target_pairs={{0,16},{496,480},{1,17},{497,481},{2,18},{498,482},{3,19},{499,483... | collective-permute-start | bytes 49160 | tf_op jit(solution)/shard_map/ppermute | solution.py:78
  67.2 0.9 collective-permute-done
  68.7 0.7 collective-permute-start.1
  70.0 0.7 collective-permute-start.2
  71.3 0.7 collective-permute-start.3
  72.6 0.7 collective-permute-start.4
  73.9 0.7 collective-permute-start.5
  79.1 0.7 collective-permute-start.9
  80.4 0.7 collective-permute-start.10
  86.9 0.7 collective-permute-start.15
  87.8 16.8 %all_gather.16 = f32[16,8,128]{2,1,0:T(8,128)S(1)} all-gather(f32[1,8,128]{2,1,0:T(8,128)S(1)} %scatter.4), channel_id=1, replica_groups=mesh['seg'=32,'sec'=16] {'sec'}, dimensions={0}, use_global_device_ids=true | all-gather | bytes 69632 | tf_op jit(solution)/shard_map/all_gather | solution.py:87
  106.8 1.3 collective-permute-start.21
  109.4 62.1 %collective-permute-done.21 = f32[1024]{0:T(1024)S(1)} collective-permute-done((f32[1024]{0:T(1024)S(1)}, f32[1024]{0:T(1024)S(1)}, u32[]{:S(2)}, u32[]{:S(2)}) %collective-permute-start.21) | collective-permute-done | bytes 4128 | tf_op jit(solution)/shard_map/ppermute | solution.py:11
  (69 shorter events, 19.7 us)
Async XLA Ops:
  6.5 52.8 %all-gather.4.cloned.1.call-start = ((), (), s32[]{:S(2)}) async-start(), calls=%async_computation | async-start | bytes 2785280 | tf_op jit(solution)/shard_map/all_gather | solution.py:36
  59.4 8.7 %copy-start = (bf16[80,128,128]{2,1,0:T(8,128)(2,1)S(1)}, bf16[80,128,128]{2,1,0:T(8,128)(2,1)}, u32[]{:S(2)}) copy-start(bf16[80,128,128]{2,1,0:T(8,128)(2,1)} %all-gather.4.cloned.1.call-done) | copy-start | bytes 7864324
  64.1 4.0 %collective-permute-start = (bf16[64,128]{1,0:T(8,128)(2,1)S(1)}, bf16[64,128]{1,0:T(8,128)(2,1)S(1)}, u32[]{:S(2)}, u32[]{:S(2)}) collective-permute-start(bf16[64,128]{1,0:T(8,128)(2,1)S(1)} %fusion.16), channel_id=1, source_target_pairs={{0,16},{496,480},{1,17},{497,481},{2,18},{498,482},{3,19},{499,483... | collective-permute-start | bytes 49160 | tf_op jit(solution)/shard_map/ppermute | solution.py:78
  68.7 0.7 collective-permute-start.1
  70.0 0.7 collective-permute-start.2
  71.3 0.7 collective-permute-start.3
  72.6 0.7 collective-permute-start.4
  73.9 0.7 collective-permute-start.5
  75.2 0.7 collective-permute-start.6
  76.5 0.7 collective-permute-start.7
  77.8 0.7 collective-permute-start.8
  79.1 0.7 collective-permute-start.9
  80.4 0.7 collective-permute-start.10
  81.7 0.7 collective-permute-start.11
  83.0 0.7 collective-permute-start.12
  84.3 0.7 collective-permute-start.13
  85.6 0.7 collective-permute-start.14
  86.9 0.7 collective-permute-start.15
  104.7 2.0 %collective-permute-start.18 = (f32[1024]{0:T(1024)S(1)}, f32[1024]{0:T(1024)S(1)}, u32[]{:S(2)}, u32[]{:S(2)}) collective-permute-start(f32[1024]{0:T(1024)S(1)} %reshape_squeeze.3), channel_id=1, source_target_pairs={{240,192},{256,304},{241,193},{257,305},{242,194},{258,306},{243,1... | collective-permute-start | bytes 12296 | tf_op jit(solution)/shard_map/ppermute | solution.py:11
  105.4 1.4 collective-permute-start.17
  106.0 0.7 collective-permute-start.16
  106.8 64.7 %collective-permute-start.21 = (f32[1024]{0:T(1024)S(1)}, f32[1024]{0:T(1024)S(1)}, u32[]{:S(2)}, u32[]{:S(2)}) collective-permute-start(f32[1024]{0:T(1024)S(1)} %add_add_fusion.1), channel_id=1, source_target_pairs={{192,0},{208,16},{224,32},{240,48},{256,448},{272,464},{288,480},{... | collective-permute-start | bytes 12296 | tf_op jit(solution)/shard_map/ppermute | solution.py:11
  108.1 63.4 %collective-permute-start.20 = (f32[1024]{0:T(1024)S(1)}, f32[1024]{0:T(1024)S(1)}, u32[]{:S(2)}, u32[]{:S(2)}) collective-permute-start(f32[1024]{0:T(1024)S(1)} %add_add_fusion.1), channel_id=1, source_target_pairs={{192,64},{208,80},{224,96},{240,112},{256,384},{272,400},{288,416}... | collective-permute-start | bytes 12296 | tf_op jit(solution)/shard_map/ppermute | solution.py:11
  108.7 62.7 %collective-permute-start.19 = (f32[1024]{0:T(1024)S(1)}, f32[1024]{0:T(1024)S(1)}, u32[]{:S(2)}, u32[]{:S(2)}) collective-permute-start(f32[1024]{0:T(1024)S(1)} %add_add_fusion.1), channel_id=1, source_target_pairs={{192,128},{208,144},{224,160},{240,176},{256,320},{272,336},{288,3... | collective-permute-start | bytes 12296 | tf_op jit(solution)/shard_map/ppermute | solution.py:11
Sparse Core Ops, SparseCore 0:
  10.2 49.1 all-gather.3

commit v7 on v6

--- a/solution.py
+++ b/solution.py
@@ -83,9 +83,27 @@
     at_meet = (seg_index == low) | (seg_index == high)
     amp = jnp.where(at_meet, amp, jnp.zeros_like(amp))
 
-    tile = jnp.zeros((8, width), jnp.float32).at[0, :group].set(amp)
-    tiles = lax.all_gather(tile, "sec", axis=0, tiled=False)
-    full = tiles[:, 0, :group].reshape(conf_count)
+    pieces = amp[None, :]
+    span = 1
+    while span < sec_count:
+        own_slot = (sec_index // span) % 4
+        parts = [pieces]
+        for t in (1, 2, 3):
+            pairs = [
+                (m * sec_count + i, m * sec_count + (i ^ (t * span)))
+                for m in (low, high)
+                for i in range(sec_count)
+            ]
+            parts.append(lax.ppermute(pieces, ("seg", "sec"), pairs))
+        slots = []
+        for r in range(4):
+            chosen = jnp.zeros_like(pieces)
+            for t in range(4):
+                chosen = chosen + jnp.where(own_slot ^ t == r, parts[t], jnp.zeros_like(pieces))
+            slots.append(chosen)
+        pieces = jnp.concatenate(slots, axis=0)
+        span *= 4
+    full = pieces.reshape(conf_count)
 
     def outward(offset, holders):
         pairs = []

time: 182 us -> 193 us (1.060)
  the two profiles are of different devices: /device:TPU:1 before, /device:TPU:42 now
where the time goes in v7:
time: 193 us; the launch traced here: 192 us
  waiting for transfers between devices  102 us (53%)
  blocking collectives  34.4 us (18%)
  starting transfers between devices  20.4 us (11%)
  between operations  14.2 us (7%)
  matrix products  11.6 us (6%)
  other arithmetic  4.9 us (3%)
  local copies, waits for them, and re-layouts  4.12 us (2%)
    ppermute x6, waiting for transfers between devices, exchange_rounds(): total = total + lax.ppermute(value, axis, pairs)  53.9 us
    ppermute x15, waiting for transfers between devices, per_device(): vector = lax.ppermute(vector, 'seg', hop)  37.4 us
    all_gather x1, blocking collectives, per_device(): occ_group = lax.all_gather(occ_mine, 'seg', axis=1, tiled=True)  34.4 us
    dot_general x16, matrix products, apply(): jnp.einsum('kqa,qnab->knb', spread, oriented, preferred_element_type=jnp....  11.6 us
    ppermute x15, starting transfers between devices, per_device(): vector = lax.ppermute(vector, 'seg', hop)  11.2 us
    all_gather x1, waiting for transfers between devices, per_device(): oriented = lax.all_gather(packed, 'sec', axis=0, tiled=False)  10.9 us
    ppermute x6, starting transfers between devices, exchange_rounds(): total = total + lax.ppermute(value, axis, pairs)  4.59 us
    ppermute x6, starting transfers between devices, per_device(): parts.append(lax.ppermute(pieces, ('seg', 'sec'), pairs))  3.97 us
  transfers between devices with their start and end apart: 29, of which 4 were waited for; matrix products, arithmetic and copies ran while one was open for 1% of the time, Pallas kernels for 0%

profile of v7, /device:TPU:42, one launch (start us, length us, event | category | flops | bytes accessed | tf_op | source)
XLA Modules:
  0.0 191.8 jit_solution(1015417598567437907)
XLA Ops:
  6.5 1.0 copy.29
  7.7 0.9 bitcast_select_fusion
  8.6 0.8 maximum_bitcast_fusion
  9.3 0.7 pad_maximum_fusion
  10.1 0.7 fusion.115
  10.8 34.4 %all-gather.1 = s32[32,1,64]{2,1,0:T(1,128)S(1)} all-gather(s32[1,1,64]{2,1,0:T(1,128)S(1)} %get-tuple-element.19), channel_id=1, replica_groups=mesh['seg'=32,'sec'=16] {'seg'}, dimensions={0}, use_global_device_ids=true | all-gather | bytes 8448 | tf_op jit(solution)/shard_map/all_gather | solution.py:43
  45.2 0.8 compare_and_fusion.1
  46.0 0.8 and_select_fusion
  46.8 10.9 %all-gather.4.cloned.1.call-done = bf16[80,128,128]{2,1,0:T(8,128)(2,1)} async-done(((bf16[5,128,128]{2,1,0:T(8,128)(2,1)}), bf16[80,128,128]{2,1,0:T(8,128)(2,1)}) %all-gather.4.cloned.1.call-update) | async-done | bytes 2621456 | tf_op jit(solution)/shard_map/all_gather | solution.py:36
  57.7 0.9 fusion.117
  60.1 2.4 %fusion.16 = bf16[64,128]{1,0:T(8,128)(2,1)S(1)} fusion(bf16[16,5,128,128]{3,2,1,0:T(8,128)(2,1)} %bitcast.267, bf16[64,16]{0,1:T(8,128)(2,1)S(1)} %fusion.97, bf16[64,128]{1,0:T(8,128)(2,1)S(1)} %fusion.96, f32[64,5]{0,1:T(8,128)S(1)} %fusion.99), kind=kOutput, calls=%fused_computation.34 | convolution fusion | flops 168370176 | bytes 2657536 | tf_op jit(solution)/shard_map/kqa,qnab->knb/dot_general | solution.py:64
  62.4 0.7 collective-permute-start
  63.7 0.7 collective-permute-start.1
  65.0 0.7 collective-permute-start.2
  66.3 0.7 collective-permute-start.3
  67.6 0.7 collective-permute-start.4
  74.2 1.3 collective-permute-start.9
  75.5 35.9 %collective-permute-done.9 = bf16[64,128]{1,0:T(8,128)(2,1)S(1)} collective-permute-done((bf16[64,128]{1,0:T(8,128)(2,1)S(1)}, bf16[64,128]{1,0:T(8,128)(2,1)S(1)}, u32[]{:S(2)}, u32[]{:S(2)}) %collective-permute-start.9) | collective-permute-done | bytes 16416 | tf_op jit(solution)/shard_map/ppermute | solution.py:78
  112.0 1.3 collective-permute-start.10
  113.3 1.4 collective-permute-done.10
  119.3 0.7 collective-permute-start.14
  120.6 0.7 collective-permute-start.15
  129.2 1.3 collective-permute-start.25
  130.5 53.9 %collective-permute-done.25 = f32[1024]{0:T(1024)S(1)} collective-permute-done((f32[1024]{0:T(1024)S(1)}, f32[1024]{0:T(1024)S(1)}, u32[]{:S(2)}, u32[]{:S(2)}) %collective-permute-start.25) | collective-permute-done | bytes 4128 | tf_op jit(solution)/shard_map/ppermute | solution.py:11
  (84 shorter events, 23.7 us)
Async XLA Ops:
  6.5 51.2 %all-gather.4.cloned.1.call-start = ((), (), s32[]{:S(2)}) async-start(), calls=%async_computation | async-start | bytes 2785280 | tf_op jit(solution)/shard_map/all_gather | solution.py:36
  62.4 0.7 collective-permute-start
  63.7 0.7 collective-permute-start.1
  65.0 0.7 collective-permute-start.2
  66.3 0.7 collective-permute-start.3
  67.6 0.7 collective-permute-start.4
  71.6 0.7 collective-permute-start.7
  72.9 0.7 collective-permute-start.8
  74.2 37.2 %collective-permute-start.9 = (bf16[64,128]{1,0:T(8,128)(2,1)S(1)}, bf16[64,128]{1,0:T(8,128)(2,1)S(1)}, u32[]{:S(2)}, u32[]{:S(2)}) collective-permute-start(bf16[64,128]{1,0:T(8,128)(2,1)S(1)} %fusion.25), channel_id=1, source_target_pairs={{144,160},{352,336},{145,161},{353,337},{146,162},{354,338},{147,1... | collective-permute-start | bytes 49160 | tf_op jit(solution)/shard_map/ppermute | solution.py:78
  112.0 2.7 %collective-permute-start.10 = (bf16[64,128]{1,0:T(8,128)(2,1)S(1)}, bf16[64,128]{1,0:T(8,128)(2,1)S(1)}, u32[]{:S(2)}, u32[]{:S(2)}) collective-permute-start(bf16[64,128]{1,0:T(8,128)(2,1)S(1)} %fusion.26), channel_id=1, source_target_pairs={{160,176},{336,320},{161,177},{337,321},{162,178},{338,322},{163,1... | collective-permute-start | bytes 49160 | tf_op jit(solution)/shard_map/ppermute | solution.py:78
  116.7 0.7 collective-permute-start.12
  120.6 0.7 collective-permute-start.15
  121.5 2.0 %collective-permute-start.16 = (f32[1,64]{1,0:T(1,128)S(1)}, f32[1,64]{1,0:T(1,128)S(1)}, u32[]{:S(2)}, u32[]{:S(2)}) collective-permute-start(f32[1,64]{1,0:T(1,128)S(1)} %fusion.103), channel_id=1, source_target_pairs={{240,241},{241,240},{242,243},{243,242},{244,245},{245,244},{246,2... | collective-permute-start | bytes 776 | tf_op jit(solution)/shard_map/ppermute | solution.py:97
  122.2 1.4 collective-permute-start.17
  122.8 0.7 collective-permute-start.18
  123.6 2.0 %collective-permute-start.21 = (f32[4,64]{1,0:T(4,128)S(1)}, f32[4,64]{1,0:T(4,128)S(1)}, u32[]{:S(2)}, u32[]{:S(2)}) collective-permute-start(f32[4,64]{1,0:T(4,128)S(1)} %pad_maximum_fusion.2), channel_id=1, source_target_pairs={{240,252},{241,253},{242,254},{243,255},{244,248},{245,249},{246,2... | collective-permute-start | bytes 3080 | tf_op jit(solution)/shard_map/ppermute | solution.py:97
  124.3 1.4 collective-permute-start.20
  124.9 0.7 collective-permute-start.19
  125.8 2.0 %collective-permute-start.24 = (f32[1024]{0:T(1024)S(1)}, f32[1024]{0:T(1024)S(1)}, u32[]{:S(2)}, u32[]{:S(2)}) collective-permute-start(f32[1024]{0:T(1024)S(1)} %reshape.116), channel_id=1, source_target_pairs={{240,192},{256,304},{241,193},{257,305},{242,194},{258,306},{243,1... | collective-permute-start | bytes 12296 | tf_op jit(solution)/shard_map/ppermute | solution.py:11
  126.5 1.4 collective-permute-start.23
  127.1 0.7 collective-permute-start.22
  127.8 2.6 %collective-permute-start.27 = (f32[1024]{0:T(1024)S(1)}, f32[1024]{0:T(1024)S(1)}, u32[]{:S(2)}, u32[]{:S(2)}) collective-permute-start(f32[1024]{0:T(1024)S(1)} %add_add_fusion.1), channel_id=1, source_target_pairs={{192,0},{208,16},{224,32},{240,48},{256,448},{272,464},{288,480},{... | collective-permute-start | bytes 12296 | tf_op jit(solution)/shard_map/ppermute | solution.py:11
  128.5 2.0 %collective-permute-start.26 = (f32[1024]{0:T(1024)S(1)}, f32[1024]{0:T(1024)S(1)}, u32[]{:S(2)}, u32[]{:S(2)}) collective-permute-start(f32[1024]{0:T(1024)S(1)} %add_add_fusion.1), channel_id=1, source_target_pairs={{192,64},{208,80},{224,96},{240,112},{256,384},{272,400},{288,416}... | collective-permute-start | bytes 12296 | tf_op jit(solution)/shard_map/ppermute | solution.py:11
  129.2 55.2 %collective-permute-start.25 = (f32[1024]{0:T(1024)S(1)}, f32[1024]{0:T(1024)S(1)}, u32[]{:S(2)}, u32[]{:S(2)}) collective-permute-start(f32[1024]{0:T(1024)S(1)} %add_add_fusion.1), channel_id=1, source_target_pairs={{192,128},{208,144},{224,160},{240,176},{256,320},{272,336},{288,3... | collective-permute-start | bytes 12296 | tf_op jit(solution)/shard_map/ppermute | solution.py:11
  (6 other events, 8.7 us)
Sparse Core Ops, SparseCore 0:
  10.2 47.5 all-gather.3

commit v8 on v6

--- a/solution.py
+++ b/solution.py
@@ -29,14 +29,14 @@
 
     local = blocks[0, :, 0]
     local = jnp.where(is_left, local, jnp.swapaxes(local, 1, 2))
-    edges = jnp.concatenate(
-        [left_edge, right_edge, jnp.zeros((width - 2, width), blocks.dtype)], axis=0
-    )
-    packed = jnp.concatenate([local, edges[None]], axis=0)
+    rows = local.reshape(local_states * width, width)
+    tail = jnp.zeros((14, width), blocks.dtype)
+    packed = jnp.concatenate([rows, left_edge, right_edge, tail], axis=0)
     oriented = lax.all_gather(packed, "sec", axis=0, tiled=False)
     nsec = oriented.shape[0]
-    lefts = oriented[:, local_states, 0]
-    rights = oriented[:, local_states, 1]
+    body = local_states * width
+    lefts = oriented[:, body]
+    rights = oriented[:, body + 1]
 
     row0 = sec_index * group
     occ_mine = lax.dynamic_slice_in_dim(occupation, row0, group, axis=0)
@@ -55,16 +55,19 @@
     sector_hot = (sector_here[:, None] == jnp.arange(nsec, dtype=jnp.int32)[None, :]).astype(
         jnp.bfloat16
     )
-    state_hot = (occ_here[:, None] == jnp.arange(local_states + 1, dtype=jnp.int32)[None, :]).astype(
-        jnp.float32
+    state_hot = (occ_here[:, None] == jnp.arange(local_states, dtype=jnp.int32)[None, :]).astype(
+        jnp.bfloat16
     )
+    slot_hot = sector_hot[:, :, None] * state_hot[:, None, :]
 
     def apply(vector):
-        spread = vector[:, None, :] * sector_hot[:, :, None]
+        spread = slot_hot[:, :, :, None] * vector[:, None, None, :]
+        spread = spread.reshape(group, nsec, body)
+        spread = jnp.pad(spread, ((0, 0), (0, 0), (0, oriented.shape[1] - body)))
         products = jnp.einsum(
-            "kqa,qnab->knb", spread, oriented, preferred_element_type=jnp.float32
+            "kqr,qrb->kb", spread, oriented, preferred_element_type=jnp.float32
         )
-        return jnp.sum(products * state_hot[:, :, None], axis=1).astype(jnp.bfloat16)
+        return products.astype(jnp.bfloat16)
 
     first_left = jnp.take(lefts, start_group, axis=0)
     first_right = jnp.take(rights, sector_end, axis=0)

time: 182 us -> 182 us (level)
  local copies, waits for them, and re-layouts: 4.16 us -> 6.36 us
  waiting for transfers between devices: 78.1 us -> 75.9 us
  matrix products: 11.7 us -> 9.75 us
    all_gather x1, waiting for transfers between devices: 15.2 us -> 13.1 us  [per_device(): oriented = lax.all_gather(packed, 'sec', axis=0, tiled=False)]
    mul x0 -> x18, local copies, waits for them, and re-layouts: none -> 2.01 us  [apply(): spread = slot_hot[:, :, :, None] * vector[:, None, None, :]]
    dot_general x16, matrix products: 11.7 us -> 9.75 us  [apply(): jnp.einsum('kqr,qrb->kb', spread, oriented, preferred_element_type=jnp.fl...]
  transfers between devices with their start and end apart: 23 -> 23, of which waited for: 3 -> 3; matrix products, arithmetic and copies ran while one was open for 1% -> 2% of each run, Pallas kernels for 0% -> 0%
where the time goes in v8:
time: 182 us; the launch traced here: 179 us
  waiting for transfers between devices  75.9 us (42%)
  blocking collectives  48.3 us (27%)
  starting transfers between devices  17.7 us (10%)
  between operations  14.3 us (8%)
  matrix products  9.75 us (5%)
  other arithmetic  6.42 us (4%)
  local copies, waits for them, and re-layouts  6.36 us (3%)
    ppermute x6, waiting for transfers between devices, exchange_rounds(): total = total + lax.ppermute(value, axis, pairs)  61.9 us
    all_gather x1, blocking collectives, per_device(): occ_group = lax.all_gather(occ_mine, 'seg', axis=1, tiled=True)  31.6 us
    all_gather x1, blocking collectives, per_device(): tiles = lax.all_gather(tile, 'sec', axis=0, tiled=False)  16.8 us
    all_gather x1, waiting for transfers between devices, per_device(): oriented = lax.all_gather(packed, 'sec', axis=0, tiled=False)  13.1 us
    ppermute x15, starting transfers between devices, per_device(): vector = lax.ppermute(vector, 'seg', hop)  12.5 us
    dot_general x16, matrix products, apply(): jnp.einsum('kqr,qrb->kb', spread, oriented, preferred_element_type=jnp.fl...  9.75 us
    ppermute x6, starting transfers between devices, exchange_rounds(): total = total + lax.ppermute(value, axis, pairs)  4.59 us
  transfers between devices with their start and end apart: 23, of which 3 were waited for; matrix products, arithmetic and copies ran while one was open for 2% of the time, Pallas kernels for 0%

profile of v8, /device:TPU:1, one launch (start us, length us, event | category | flops | bytes accessed | tf_op | source)
XLA Modules:
  0.0 178.7 jit_solution(16245761668679650861)
XLA Ops:
  6.5 1.0 copy.9
  7.7 0.9 bitcast_select_fusion
  8.6 1.5 maximum_maximum_fusion
  10.1 0.7 fusion.136
  10.8 31.6 %all-gather.1 = s32[32,1,64]{2,1,0:T(1,128)S(1)} all-gather(s32[1,1,64]{2,1,0:T(1,128)S(1)} %get-tuple-element.28), channel_id=1, replica_groups=mesh['seg'=32,'sec'=16] {'seg'}, dimensions={0}, use_global_device_ids=true | all-gather | bytes 8448 | tf_op jit(solution)/shard_map/all_gather | solution.py:43
  42.5 0.8 and_select_fusion.1
  43.6 1.3 mul.287
  45.3 0.8 compare_and_fusion.1
  46.1 13.1 %all-gather.4.cloned.1.call-done = bf16[8448,128]{1,0:T(8,128)(2,1)} async-done(((bf16[528,128]{1,0:T(8,128)(2,1)}), bf16[8448,128]{1,0:T(8,128)(2,1)}) %all-gather.4.cloned.1.call-update) | async-done | bytes 2162704 | tf_op jit(solution)/shard_map/all_gather | solution.py:35
  59.2 0.9 fusion.153
  62.2 3.0 %collective-permute-start = (bf16[64,128]{1,0:T(8,128)(2,1)S(1)}, bf16[64,128]{1,0:T(8,128)(2,1)S(1)}, u32[]{:S(2)}, u32[]{:S(2)}) collective-permute-start(bf16[64,128]{1,0:T(8,128)(2,1)S(1)} %fusion.125), channel_id=1, source_target_pairs={{0,16},{496,480},{1,17},{497,481},{2,18},{498,482},{3,19},{499,483... | collective-permute-start | bytes 49160 | tf_op jit(solution)/shard_map/ppermute | solution.py:81
  65.2 0.9 collective-permute-done
  66.8 0.7 collective-permute-start.1
  68.3 0.7 collective-permute-start.2
  69.7 0.7 collective-permute-start.3
  71.1 0.7 collective-permute-start.4
  72.6 0.7 collective-permute-start.5
  74.0 0.7 collective-permute-start.6
  81.1 0.7 collective-permute-start.11
  82.6 0.8 collective-permute-start.12
  87.0 0.7 collective-permute-start.15
  87.9 16.8 %all_gather.16 = f32[16,8,128]{2,1,0:T(8,128)S(1)} all-gather(f32[1,8,128]{2,1,0:T(8,128)S(1)} %scatter.4), channel_id=1, replica_groups=mesh['seg'=32,'sec'=16] {'sec'}, dimensions={0}, use_global_device_ids=true | all-gather | bytes 69632 | tf_op jit(solution)/shard_map/all_gather | solution.py:90
  106.8 1.3 collective-permute-start.21
  109.4 61.8 %collective-permute-done.21 = f32[1024]{0:T(1024)S(1)} collective-permute-done((f32[1024]{0:T(1024)S(1)}, f32[1024]{0:T(1024)S(1)}, u32[]{:S(2)}, u32[]{:S(2)}) %collective-permute-start.21) | collective-permute-done | bytes 4128 | tf_op jit(solution)/shard_map/ppermute | solution.py:11
  (119 shorter events, 22.0 us)
Async XLA Ops:
  6.5 52.6 %all-gather.4.cloned.1.call-start = ((), (), s32[]{:S(2)}) async-start(), calls=%async_computation | async-start | bytes 2297856 | tf_op jit(solution)/shard_map/all_gather | solution.py:35
  59.1 2.5 %copy-start = (bf16[8448,128]{1,0:T(8,128)(2,1)S(1)}, bf16[8448,128]{1,0:T(8,128)(2,1)}, u32[]{:S(2)}) copy-start(bf16[8448,128]{1,0:T(8,128)(2,1)} %all-gather.4.cloned.1.call-done) | copy-start | bytes 6488068
  62.2 3.9 %collective-permute-start = (bf16[64,128]{1,0:T(8,128)(2,1)S(1)}, bf16[64,128]{1,0:T(8,128)(2,1)S(1)}, u32[]{:S(2)}, u32[]{:S(2)}) collective-permute-start(bf16[64,128]{1,0:T(8,128)(2,1)S(1)} %fusion.125), channel_id=1, source_target_pairs={{0,16},{496,480},{1,17},{497,481},{2,18},{498,482},{3,19},{499,483... | collective-permute-start | bytes 49160 | tf_op jit(solution)/shard_map/ppermute | solution.py:81
  66.8 0.7 collective-permute-start.1
  68.3 0.7 collective-permute-start.2
  69.7 0.7 collective-permute-start.3
  71.1 0.7 collective-permute-start.4
  72.6 0.7 collective-permute-start.5
  74.0 0.7 collective-permute-start.6
  75.4 0.7 collective-permute-start.7
  76.8 0.7 collective-permute-start.8
  78.3 0.7 collective-permute-start.9
  79.7 0.7 collective-permute-start.10
  81.1 0.7 collective-permute-start.11
  82.6 0.9 collective-permute-start.12
  84.2 0.7 collective-permute-start.13
  85.6 0.7 collective-permute-start.14
  87.0 0.7 collective-permute-start.15
  104.7 2.0 %collective-permute-start.18 = (f32[1024]{0:T(1024)S(1)}, f32[1024]{0:T(1024)S(1)}, u32[]{:S(2)}, u32[]{:S(2)}) collective-permute-start(f32[1024]{0:T(1024)S(1)} %reshape_squeeze.3), channel_id=1, source_target_pairs={{240,192},{256,304},{241,193},{257,305},{242,194},{258,306},{243,1... | collective-permute-start | bytes 12296 | tf_op jit(solution)/shard_map/ppermute | solution.py:11
  105.4 1.4 collective-permute-start.17
  106.0 0.7 collective-permute-start.16
  106.8 64.5 %collective-permute-start.21 = (f32[1024]{0:T(1024)S(1)}, f32[1024]{0:T(1024)S(1)}, u32[]{:S(2)}, u32[]{:S(2)}) collective-permute-start(f32[1024]{0:T(1024)S(1)} %add_add_fusion.1), channel_id=1, source_target_pairs={{192,0},{208,16},{224,32},{240,48},{256,448},{272,464},{288,480},{... | collective-permute-start | bytes 12296 | tf_op jit(solution)/shard_map/ppermute | solution.py:11
  108.0 63.2 %collective-permute-start.20 = (f32[1024]{0:T(1024)S(1)}, f32[1024]{0:T(1024)S(1)}, u32[]{:S(2)}, u32[]{:S(2)}) collective-permute-start(f32[1024]{0:T(1024)S(1)} %add_add_fusion.1), channel_id=1, source_target_pairs={{192,64},{208,80},{224,96},{240,112},{256,384},{272,400},{288,416}... | collective-permute-start | bytes 12296 | tf_op jit(solution)/shard_map/ppermute | solution.py:11
  108.7 62.5 %collective-permute-start.19 = (f32[1024]{0:T(1024)S(1)}, f32[1024]{0:T(1024)S(1)}, u32[]{:S(2)}, u32[]{:S(2)}) collective-permute-start(f32[1024]{0:T(1024)S(1)} %add_add_fusion.1), channel_id=1, source_target_pairs={{192,128},{208,144},{224,160},{240,176},{256,320},{272,336},{288,3... | collective-permute-start | bytes 12296 | tf_op jit(solution)/shard_map/ppermute | solution.py:11
Sparse Core Ops, SparseCore 0:
  10.2 48.8 all-gather.3

commit v9 on v3

v9 whole, which is shorter than its diff:
```python
import jax
import jax.numpy as jnp
from jax import lax
from jax.sharding import PartitionSpec as P


def spread_pairs(holders, count, fan):
    have = sorted(holders)
    rounds = []
    while len(have) < count:
        missing = [i for i in range(count) if i not in have]
        perms = []
        for _ in range(fan):
            pairs = []
            for h in have:
                if not missing:
                    break
                target = min(missing, key=lambda m: (abs(m - h), m))
                missing.remove(target)
                pairs.append((h, target))
            if pairs:
                perms.append(pairs)
        rounds.append(perms)
        have = sorted(set(have) | {t for perm in perms for _, t in perm})
    return rounds


def per_device(blocks, left_edge, right_edge, occupation, start_sector):
    seg_count = lax.axis_size("seg")
    sec_count = lax.axis_size("sec")
    half_count = seg_count // 2
    seg_index = lax.axis_index("seg")
    sec_index = lax.axis_index("sec")
    is_left = seg_index < half_count

    conf_count = occupation.shape[0]
    sites = seg_count * occupation.shape[1]
    group = conf_count // sec_count
    width = blocks.shape[-1]
    local_states = blocks.shape[1]

    partner = seg_index ^ 1
    depth = jnp.where(is_left, seg_index // 2, (seg_count - 1 - seg_index) // 2)

    local = blocks[0, :, 0]
    local = jnp.where(is_left, local, jnp.swapaxes(local, 1, 2))
    feed = [(2 * m + 1, 2 * m) for m in range(half_count // 2)] + [
        (2 * m, 2 * m + 1) for m in range(half_count // 2, seg_count // 2)
    ]
    partner_local = lax.ppermute(local, "seg", feed)
    tail = jnp.zeros((14, width), blocks.dtype)
    body = local_states * width

    def site_rows(part):
        rows = part.reshape(body, width)
        return jnp.concatenate([rows, left_edge, right_edge, tail], axis=0)

    packed = jnp.stack([site_rows(local), site_rows(partner_local)], axis=0)
    both = lax.all_gather(packed, "sec", axis=1, tiled=False)
    nsec = both.shape[1]
    lefts = both[0, :, body]
    rights = both[0, :, body + 1]

    row0 = sec_index * group
    occ_mine = lax.dynamic_slice_in_dim(occupation, row0, group, axis=0)
    occ_group = lax.all_gather(occ_mine, "seg", axis=1, tiled=True)
    start_group = lax.dynamic_slice_in_dim(start_sector, row0, group, axis=0)

    charge = jnp.array([0, 1, -1, 0], dtype=jnp.int32)
    steps = charge[occ_group]
    site_ids = jnp.arange(sites, dtype=jnp.int32)
    total = jnp.sum(steps, axis=1)
    sector_end = jnp.mod(start_group + total, nsec)
    sector_ids = jnp.arange(nsec, dtype=jnp.int32)
    state_ids = jnp.arange(local_states, dtype=jnp.int32)

    def site_slots(site):
        before = jnp.sum(jnp.where(site_ids[None, :] < site, steps, 0), axis=1)
        sector = jnp.mod(start_group + before, nsec)
        occ = jnp.sum(jnp.where(site_ids[None, :] == site, occ_group, 0), axis=1)
        sector_hot = (sector[:, None] == sector_ids[None, :]).astype(jnp.bfloat16)
        state_hot = (occ[:, None] == state_ids[None, :]).astype(jnp.bfloat16)
        return sector_hot[:, :, None] * state_hot[:, None, :]

    slots = [site_slots(seg_index), site_slots(partner)]

    def apply(vector, which):
        spread = slots[which][:, :, :, None] * vector[:, None, None, :]
        spread = spread.reshape(group, nsec, body)
        spread = jnp.pad(spread, ((0, 0), (0, 0), (0, both.shape[2] - body)))
        products = jnp.einsum(
            "kqr,qrb->kb", spread, both[which], preferred_element_type=jnp.float32
        )
        return products.astype(jnp.bfloat16)

    first_left = jnp.take(lefts, start_group, axis=0)
    first_right = jnp.take(rights, sector_end, axis=0)
    first = jnp.where(is_left, first_left, first_right)
    vector = jnp.where(depth == 0, first, jnp.zeros_like(first))

    chain_steps = half_count // 2
    for step in range(chain_steps):
        vector = apply(vector, 0)
        vector = apply(vector, 1)
        if step < chain_steps - 1:
            hop = [(2 * step, 2 * step + 2), (seg_count - 1 - 2 * step, seg_count - 3 - 2 * step)]
            vector = lax.ppermute(vector, "seg", hop)

    low, high = half_count - 2, half_count + 1
    other = lax.ppermute(vector, "seg", [(low, high), (high, low)])
    amp = jnp.sum(vector.astype(jnp.float32) * other.astype(jnp.float32), axis=1)
    at_meet = (seg_index == low) | (seg_index == high)
    amp = jnp.where(at_meet, amp, jnp.zeros_like(amp))

    tile = jnp.zeros((8, width), jnp.float32).at[0, :group].set(amp)
    tiles = lax.all_gather(tile, "sec", axis=0, tiled=False)
    full = tiles[:, 0, :group].reshape(conf_count)

    for perms in spread_pairs([low, high], seg_count, 3):
        received = [lax.ppermute(full, "seg", pairs) for pairs in perms]
        for value in received:
            full = full + value
    return full


def solution(mesh):
    in_specs = (
        P("seg", None, "sec", None, None),
        P("sec", None),
        P("sec", None),
        P(None, "seg"),
        P(),
    )
    out_specs = P()
    return jax.shard_map(
        per_device, mesh=mesh, in_specs=in_specs, out_specs=out_specs, check_vma=False
    )
```

time: 252 us -> 169 us (0.67)
  the two profiles are of different devices: /device:TPU:14 before, /device:TPU:1 now
where the time goes in v9:
time: 169 us
  waiting for transfers between devices  65 us (38%)
  blocking collectives  49 us (29%)
  starting transfers between devices  15.2 us (9%)
  between operations  14.3 us (8%)
  matrix products  9.73 us (6%)
  local copies, waits for them, and re-layouts  9.7 us (6%)
  other arithmetic  6.04 us (4%)
    ppermute x6, waiting for transfers between devices, per_device(): received = [lax.ppermute(full, 'seg', pairs) for pairs in perms]  44.4 us
    all_gather x1, blocking collectives, per_device(): occ_group = lax.all_gather(occ_mine, 'seg', axis=1, tiled=True)  32.1 us
    all_gather x1, blocking collectives, per_device(): tiles = lax.all_gather(tile, 'sec', axis=0, tiled=False)  16.9 us
    all_gather x1, waiting for transfers between devices, per_device(): both = lax.all_gather(packed, 'sec', axis=1, tiled=False)  15.3 us
    dot_general x16, matrix products, apply(): jnp.einsum('kqr,qrb->kb', spread, both[which], preferred_element_type=jnp...  9.73 us
    ppermute x7, starting transfers between devices, per_device(): vector = lax.ppermute(vector, 'seg', hop)  8.69 us
    ppermute x6, starting transfers between devices, per_device(): received = [lax.ppermute(full, 'seg', pairs) for pairs in perms]  4.59 us
    ppermute x1, waiting for transfers between devices, per_device(): partner_local = lax.ppermute(local, 'seg', feed)  4.32 us
  transfers between devices with their start and end apart: 16, of which 4 were waited for; matrix products, arithmetic and copies ran while one was open for 3% of the time, Pallas kernels for 0%

profile of v9, /device:TPU:1, one launch (start us, length us, event | category | flops | bytes accessed | tf_op | source)
XLA Modules:
  0.0 169.0 jit_solution(10704670263857878347)
XLA Ops:
  6.5 1.0 copy.11
  7.6 0.9 bitcast_select_fusion
  8.5 1.3 collective-permute-start
  9.9 4.3 %collective-permute-done = bf16[4,128,128]{2,1,0:T(8,128)(2,1)S(1)} collective-permute-done((bf16[4,128,128]{2,1,0:T(8,128)(2,1)S(1)}, bf16[4,128,128]{2,1,0:T(8,128)(2,1)S(1)}, u32[]{:S(2)}, u32[]{:S(2)}) %collective-permute-start) | collective-permute-done | bytes 131104 | tf_op jit(solution)/shard_map/ppermute | solution.py:50
  14.2 0.8 fusion.129
  15.0 0.7 pad_maximum_fusion
  15.9 32.1 %all-gather.1 = s32[32,1,64]{2,1,0:T(1,128)S(1)} all-gather(s32[1,1,64]{2,1,0:T(1,128)S(1)} %dynamic-slice_bitcast_fusion), channel_id=1, replica_groups=mesh['seg'=32,'sec'=16] {'seg'}, dimensions={0}, use_global_device_ids=true | all-gather | bytes 8448 | tf_op jit(solution)/shard_map/all_gather | solution.py:66
  48.0 0.8 compare_and_fusion.1
  49.2 1.3 mul.313
  51.2 1.3 mul.308
  53.0 15.3 %all-gather.4.cloned.1.call-done = bf16[2,8448,128]{2,1,0:T(8,128)(2,1)} async-done(((bf16[2,528,128]{2,1,0:T(8,128)(2,1)}), bf16[2,8448,128]{2,1,0:T(8,128)(2,1)}) %all-gather.4.cloned.1.call-update) | async-done | bytes 4325392 | tf_op jit(solution)/shard_map/all_gather | solution.py:59
  68.3 0.8 fusion.158
  70.7 2.4 %fusion.159 = (bf16[1,8448,128]{2,1,0:T(8,128)(2,1)S(1)}, bf16[1,8448,128]{2,1,0:T(8,128)(2,1)S(1)}) fusion(bf16[2,8448,128]{2,1,0:T(8,128)(2,1)} %all-gather.4.cloned.1.call-done), kind=kLoop, calls=%fused_computation.175 | loop fusion | bytes 8650752 | tf_op jit(solution)/shard_map/slice | solution.py:92
  74.4 4.5 %collective-permute-start.1 = (bf16[64,128]{1,0:T(8,128)(2,1)S(1)}, bf16[64,128]{1,0:T(8,128)(2,1)S(1)}, u32[]{:S(2)}, u32[]{:S(2)}) collective-permute-start(bf16[64,128]{1,0:T(8,128)(2,1)S(1)} %fusion.122), channel_id=1, source_target_pairs={{0,32},{496,464},{1,33},{497,465},{2,34},{498,466},{3,35},{499,467... | collective-permute-start | bytes 49160 | tf_op jit(solution)/shard_map/ppermute | solution.py:107
  79.0 0.9 collective-permute-done.1
  81.3 0.7 collective-permute-start.2
  83.5 0.7 collective-permute-start.3
  85.7 0.7 collective-permute-start.4
  87.8 0.7 collective-permute-start.5
  90.0 0.8 collective-permute-start.6
  92.4 0.7 collective-permute-start.7
  95.4 16.9 %all_gather.16 = f32[16,8,128]{2,1,0:T(8,128)S(1)} all-gather(f32[1,8,128]{2,1,0:T(8,128)S(1)} %scatter.4), channel_id=1, replica_groups=mesh['seg'=32,'sec'=16] {'sec'}, dimensions={0}, use_global_device_ids=true | all-gather | bytes 69632 | tf_op jit(solution)/shard_map/all_gather | solution.py:116
  115.8 1.3 collective-permute-start.14
  117.1 44.4 %collective-permute-done.14 = f32[1024]{0:T(1024)S(1)} collective-permute-done((f32[1024]{0:T(1024)S(1)}, f32[1024]{0:T(1024)S(1)}, u32[]{:S(2)}, u32[]{:S(2)}) %collective-permute-start.14) | collective-permute-done | bytes 4128 | tf_op jit(solution)/shard_map/ppermute | solution.py:120
  (115 shorter events, 19.5 us)
Async XLA Ops:
  6.5 9.3 %copy-start = (s32[1024,1]{0,1:T(1,128)S(1)}, s32[1024,1]{0,1:T(1,128)}, u32[]{:S(2)}) copy-start(s32[1024,1]{0,1:T(1,128)} %param.13) | copy-start | bytes 12292
  6.5 61.8 %all-gather.4.cloned.1.call-start = ((), (), s32[]{:S(2)}) async-start(), calls=%async_computation | async-start | bytes 4595712 | tf_op jit(solution)/shard_map/all_gather | solution.py:59
  8.5 5.7 %collective-permute-start = (bf16[4,128,128]{2,1,0:T(8,128)(2,1)S(1)}, bf16[4,128,128]{2,1,0:T(8,128)(2,1)S(1)}, u32[]{:S(2)}, u32[]{:S(2)}) collective-permute-start(bf16[4,128,128]{2,1,0:T(8,128)(2,1)S(1)} %bitcast_select_fusion), channel_id=1, source_target_pairs={{16,0},{48,32},{80,64},{112,96},{144,128},{176,160},{208,192},{240... | collective-permute-start | bytes 393224 | tf_op jit(solution)/shard_map/ppermute | solution.py:50
  74.4 5.4 %collective-permute-start.1 = (bf16[64,128]{1,0:T(8,128)(2,1)S(1)}, bf16[64,128]{1,0:T(8,128)(2,1)S(1)}, u32[]{:S(2)}, u32[]{:S(2)}) collective-permute-start(bf16[64,128]{1,0:T(8,128)(2,1)S(1)} %fusion.122), channel_id=1, source_target_pairs={{0,32},{496,464},{1,33},{497,465},{2,34},{498,466},{3,35},{499,467... | collective-permute-start | bytes 49160 | tf_op jit(solution)/shard_map/ppermute | solution.py:107
  81.3 0.7 collective-permute-start.2
  83.5 0.7 collective-permute-start.3
  85.7 0.7 collective-permute-start.4
  87.8 0.7 collective-permute-start.5
  90.0 0.9 collective-permute-start.6
  92.4 0.7 collective-permute-start.7
  94.5 0.7 collective-permute-start.8
  112.4 2.0 %collective-permute-start.10 = (f32[1024]{0:T(1024)S(1)}, f32[1024]{0:T(1024)S(1)}, u32[]{:S(2)}, u32[]{:S(2)}) collective-permute-start(f32[1024]{0:T(1024)S(1)} %reshape_squeeze.3), channel_id=1, source_target_pairs={{224,240},{272,288},{225,241},{273,289},{226,242},{274,290},{227,2... | collective-permute-start | bytes 12296 | tf_op jit(solution)/shard_map/ppermute | solution.py:120
  113.0 1.4 collective-permute-start.11
  113.7 0.7 collective-permute-start.9
  114.4 2.6 %collective-permute-start.12 = (f32[1024]{0:T(1024)S(1)}, f32[1024]{0:T(1024)S(1)}, u32[]{:S(2)}, u32[]{:S(2)}) collective-permute-start(f32[1024]{0:T(1024)S(1)} %add_add_fusion.1), channel_id=1, source_target_pairs={{192,176},{208,160},{224,144},{240,320},{256,336},{272,352},{288,3... | collective-permute-start | bytes 12296 | tf_op jit(solution)/shard_map/ppermute | solution.py:120
  115.1 2.0 %collective-permute-start.13 = (f32[1024]{0:T(1024)S(1)}, f32[1024]{0:T(1024)S(1)}, u32[]{:S(2)}, u32[]{:S(2)}) collective-permute-start(f32[1024]{0:T(1024)S(1)} %add_add_fusion.1), channel_id=1, source_target_pairs={{192,128},{208,112},{224,96},{240,80},{256,400},{272,416},{288,432... | collective-permute-start | bytes 12296 | tf_op jit(solution)/shard_map/ppermute | solution.py:120
  115.8 45.8 %collective-permute-start.14 = (f32[1024]{0:T(1024)S(1)}, f32[1024]{0:T(1024)S(1)}, u32[]{:S(2)}, u32[]{:S(2)}) collective-permute-start(f32[1024]{0:T(1024)S(1)} %add_add_fusion.1), channel_id=1, source_target_pairs={{192,64},{208,48},{224,32},{240,16},{256,464},{272,480},{288,496},... | collective-permute-start | bytes 12296 | tf_op jit(solution)/shard_map/ppermute | solution.py:120
Sparse Core Ops, SparseCore 0:
  15.9 52.3 all-gather.3

commit v10 on v9

--- a/solution.py
+++ b/solution.py
@@ -2,6 +2,8 @@
 import jax.numpy as jnp
 from jax import lax
 from jax.sharding import PartitionSpec as P
+
+SITES_PER_DEVICE = 4
 
 
 def spread_pairs(holders, count, fan):
@@ -39,15 +41,19 @@
     width = blocks.shape[-1]
     local_states = blocks.shape[1]
 
-    partner = seg_index ^ 1
-    depth = jnp.where(is_left, seg_index // 2, (seg_count - 1 - seg_index) // 2)
+    span = SITES_PER_DEVICE
+    direction = jnp.where(is_left, 1, -1)
+    depth = jnp.where(is_left, seg_index // span, (seg_count - 1 - seg_index) // span)
 
     local = blocks[0, :, 0]
     local = jnp.where(is_left, local, jnp.swapaxes(local, 1, 2))
-    feed = [(2 * m + 1, 2 * m) for m in range(half_count // 2)] + [
-        (2 * m, 2 * m + 1) for m in range(half_count // 2, seg_count // 2)
-    ]
-    partner_local = lax.ppermute(local, "seg", feed)
+    runs = seg_count // span
+    parts = [local]
+    for t in range(1, span):
+        feed = [(r * span + t, r * span) for r in range(runs // 2)] + [
+            (r * span + span - 1 - t, r * span + span - 1) for r in range(runs // 2, runs)
+        ]
+        parts.append(lax.ppermute(local, "seg", feed))
     tail = jnp.zeros((14, width), blocks.dtype)
     body = local_states * width
 
@@ -55,7 +61,7 @@
         rows = part.reshape(body, width)
         return jnp.concatenate([rows, left_edge, right_edge, tail], axis=0)
 
-    packed = jnp.stack([site_rows(local), site_rows(partner_local)], axis=0)
+    packed = jnp.stack([site_rows(part) for part in parts], axis=0)
     both = lax.all_gather(packed, "sec", axis=1, tiled=False)
     nsec = both.shape[1]
     lefts = both[0, :, body]
@@ -82,7 +88,7 @@
         state_hot = (occ[:, None] == state_ids[None, :]).astype(jnp.bfloat16)
         return sector_hot[:, :, None] * state_hot[:, None, :]
 
-    slots = [site_slots(seg_index), site_slots(partner)]
+    slots = [site_slots(seg_index + t * direction) for t in range(span)]
 
     def apply(vector, which):
         spread = slots[which][:, :, :, None] * vector[:, None, None, :]
@@ -98,15 +104,18 @@
     first = jnp.where(is_left, first_left, first_right)
     vector = jnp.where(depth == 0, first, jnp.zeros_like(first))
 
-    chain_steps = half_count // 2
+    chain_steps = half_count // span
     for step in range(chain_steps):
-        vector = apply(vector, 0)
-        vector = apply(vector, 1)
+        for t in range(span):
+            vector = apply(vector, t)
         if step < chain_steps - 1:
-            hop = [(2 * step, 2 * step + 2), (seg_count - 1 - 2 * step, seg_count - 3 - 2 * step)]
+            hop = [
+                (span * step, span * (step + 1)),
+                (seg_count - 1 - span * step, seg_count - 1 - span * (step + 1)),
+            ]
             vector = lax.ppermute(vector, "seg", hop)
 
-    low, high = half_count - 2, half_count + 1
+    low, high = half_count - span, half_count + span - 1
     other = lax.ppermute(vector, "seg", [(low, high), (high, low)])
     amp = jnp.sum(vector.astype(jnp.float32) * other.astype(jnp.float32), axis=1)
     at_meet = (seg_index == low) | (seg_index == high)

time: 169 us -> 167 us (0.988); the launches traced: 169 us -> 164 us
  waiting for transfers between devices: 65 us -> 49 us
  local copies, waits for them, and re-layouts: 9.7 us -> 19.6 us
  blocking collectives: 49 us -> 51 us
    ppermute x6, waiting for transfers between devices: 44.4 us -> 22.6 us  [per_device(): received = [lax.ppermute(full, 'seg', pairs) for pairs in perms]]
    mul x20 -> x24, local copies, waits for them, and re-layouts: 3.7 us -> 11.6 us  [apply(): spread = slots[which][:, :, :, None] * vector[:, None, None, :]]
    all_gather x1, waiting for transfers between devices: 15.3 us -> 20.9 us  [per_device(): both = lax.all_gather(packed, 'sec', axis=1, tiled=False)]
    ppermute x7 -> x3, starting transfers between devices: 8.69 us -> 4.61 us  [per_device(): vector = lax.ppermute(vector, 'seg', hop)]
    ppermute x1 -> x3, starting transfers between devices: 1.29 us -> 3.87 us  [per_device(): parts.append(lax.ppermute(local, 'seg', feed))]
    all_gather x1, blocking collectives: 32.1 us -> 34.5 us  [per_device(): occ_group = lax.all_gather(occ_mine, 'seg', axis=1, tiled=True)]
    ppermute x1 -> x3, waiting for transfers between devices: 4.32 us -> 4.64 us  [per_device(): parts.append(lax.ppermute(local, 'seg', feed))]
  transfers between devices with their start and end apart: 16 -> 14, of which waited for: 4 -> 5; matrix products, arithmetic and copies ran while one was open for 3% -> 8% of each run, Pallas kernels for 0% -> 0%
where the time goes in v10:
time: 167 us; the launch traced here: 164 us
  blocking collectives  51 us (31%)
  waiting for transfers between devices  49 us (29%)
  local copies, waits for them, and re-layouts  19.6 us (12%)
  between operations  14.3 us (9%)
  starting transfers between devices  13.7 us (8%)
  matrix products  9.37 us (6%)
  other arithmetic  6.82 us (4%)
    all_gather x1, blocking collectives, per_device(): occ_group = lax.all_gather(occ_mine, 'seg', axis=1, tiled=True)  34.5 us
    ppermute x6, waiting for transfers between devices, per_device(): received = [lax.ppermute(full, 'seg', pairs) for pairs in perms]  22.6 us
    all_gather x1, waiting for transfers between devices, per_device(): both = lax.all_gather(packed, 'sec', axis=1, tiled=False)  20.9 us
    all_gather x1, blocking collectives, per_device(): tiles = lax.all_gather(tile, 'sec', axis=0, tiled=False)  16.5 us
    mul x24, local copies, waits for them, and re-layouts, apply(): spread = slots[which][:, :, :, None] * vector[:, None, None, :]  11.6 us
    dot_general x16, matrix products, apply(): jnp.einsum('kqr,qrb->kb', spread, both[which], preferred_element_type=jnp...  9.37 us
    ppermute x3, waiting for transfers between devices, per_device(): parts.append(lax.ppermute(local, 'seg', feed))  4.64 us
    ppermute x3, starting transfers between devices, per_device(): vector = lax.ppermute(vector, 'seg', hop)  4.61 us
  transfers between devices with their start and end apart: 14, of which 5 were waited for; matrix products, arithmetic and copies ran while one was open for 8% of the time, Pallas kernels for 0%

profile of v10, /device:TPU:1, one launch (start us, length us, event | category | flops | bytes accessed | tf_op | source)
XLA Modules:
  0.0 163.9 jit_solution(12491290480686485183)
XLA Ops:
  6.5 1.0 copy.11
  7.6 0.9 bitcast_select_fusion
  8.5 1.3 collective-permute-start.1
  9.8 1.3 collective-permute-start.2
  11.1 1.3 collective-permute-start
  12.5 3.3 %collective-permute-done.1 = bf16[4,128,128]{2,1,0:T(8,128)(2,1)S(1)} collective-permute-done((bf16[4,128,128]{2,1,0:T(8,128)(2,1)S(1)}, bf16[4,128,128]{2,1,0:T(8,128)(2,1)S(1)}, u32[]{:S(2)}, u32[]{:S(2)}) %collective-permute-start.1) | collective-permute-done | bytes 131104 | tf_op jit(solution)/shard_map/ppermute | solution.py:56
  15.8 1.4 collective-permute-done.2
  17.1 0.8 fusion.129
  18.0 0.9 pad_maximum_fusion
  19.0 34.5 %all-gather.1 = s32[32,1,64]{2,1,0:T(1,128)S(1)} all-gather(s32[1,1,64]{2,1,0:T(1,128)S(1)} %dynamic-slice_bitcast_fusion), channel_id=1, replica_groups=mesh['seg'=32,'sec'=16] {'seg'}, dimensions={0}, use_global_device_ids=true | all-gather | bytes 8448 | tf_op jit(solution)/shard_map/all_gather | solution.py:72
  54.8 1.3 mul.365
  56.8 1.3 mul.360
  58.8 2.1 %mul.355 = bf16[64,16,4,128]{3,2,0,1:T(4,128)(2,1)} broadcast(bf16[64,16,4]{2,0,1:T(8,128)(2,1)S(1)} %broadcast_multiply_fusion.18), dimensions={0,1,2} | broadcast | bytes 1056768 | tf_op jit(solution)/shard_map/mul | solution.py:94
  60.9 1.5 mul.356
  62.7 2.1 %mul.350 = bf16[64,16,4,128]{3,2,0,1:T(4,128)(2,1)} broadcast(bf16[64,16,4]{2,0,1:T(8,128)(2,1)S(1)} %broadcast_multiply_fusion.19), dimensions={0,1,2} | broadcast | bytes 1056768 | tf_op jit(solution)/shard_map/mul | solution.py:94
  64.7 2.3 %mul.351 = bf16[64,16,512]{2,0,1:T(8,128)(2,1)} reshape(bf16[64,16,4,128]{3,2,0,1:T(4,128)(2,1)} %mul.350) | data formatting | bytes 2097152 | tf_op jit(solution)/shard_map/mul | solution.py:94
  67.1 20.9 %all-gather.4.cloned.1.call-done = bf16[4,8448,128]{2,1,0:T(8,128)(2,1)} async-done(((bf16[4,528,128]{2,1,0:T(8,128)(2,1)}), bf16[4,8448,128]{2,1,0:T(8,128)(2,1)}) %all-gather.4.cloned.1.call-update) | async-done | bytes 8650768 | tf_op jit(solution)/shard_map/all_gather | solution.py:65
  88.0 0.9 fusion.168
  90.4 3.8 %fusion.169 = (bf16[1,8448,128]{2,1,0:T(8,128)(2,1)S(1)}, bf16[1,8448,128]{2,1,0:T(8,128)(2,1)S(1)}, bf16[1,8448,128]{2,1,0:T(8,128)(2,1)S(1)}, bf16[1,8448,128]{2,1,0:T(8,128)(2,1)S(1)}) fusion(bf16[4,8448,128]{2,1,0:T(8,128)(2,1)} %all-gather.4.cloned.1.call-done), kind=kLoop, calls=%fused_computation.209 | loop fusion | bytes 17301504 | tf_op jit(solution)/shard_map/slice | solution.py:98
  97.5 3.1 %collective-permute-start.3 = (bf16[64,128]{1,0:T(8,128)(2,1)S(1)}, bf16[64,128]{1,0:T(8,128)(2,1)S(1)}, u32[]{:S(2)}, u32[]{:S(2)}) collective-permute-start(bf16[64,128]{1,0:T(8,128)(2,1)S(1)} %fusion.116), channel_id=1, source_target_pairs={{0,64},{496,432},{1,65},{497,433},{2,66},{498,434},{3,67},{499,435... | collective-permute-start | bytes 49160 | tf_op jit(solution)/shard_map/ppermute | solution.py:116
  100.6 0.9 collective-permute-done.3
  112.5 16.5 %all_gather.16 = f32[16,8,128]{2,1,0:T(8,128)S(1)} all-gather(f32[1,8,128]{2,1,0:T(8,128)S(1)} %scatter.4), channel_id=1, replica_groups=mesh['seg'=32,'sec'=16] {'sec'}, dimensions={0}, use_global_device_ids=true | all-gather | bytes 69632 | tf_op jit(solution)/shard_map/all_gather | solution.py:125
  132.6 1.3 collective-permute-start.12
  133.9 22.6 %collective-permute-done.12 = f32[1024]{0:T(1024)S(1)} collective-permute-done((f32[1024]{0:T(1024)S(1)}, f32[1024]{0:T(1024)S(1)}, u32[]{:S(2)}, u32[]{:S(2)}) %collective-permute-start.12) | collective-permute-done | bytes 4128 | tf_op jit(solution)/shard_map/ppermute | solution.py:129
  (125 shorter events, 22.6 us)
Async XLA Ops:
  6.5 12.4 %copy-start = (s32[1024,1]{0,1:T(1,128)S(1)}, s32[1024,1]{0,1:T(1,128)}, u32[]{:S(2)}) copy-start(s32[1024,1]{0,1:T(1,128)} %param.13) | copy-start | bytes 12292
  6.5 81.5 %all-gather.4.cloned.1.call-start = ((), (), s32[]{:S(2)}) async-start(), calls=%async_computation | async-start | bytes 9191424 | tf_op jit(solution)/shard_map/all_gather | solution.py:65
  8.5 7.3 %collective-permute-start.1 = (bf16[4,128,128]{2,1,0:T(8,128)(2,1)S(1)}, bf16[4,128,128]{2,1,0:T(8,128)(2,1)S(1)}, u32[]{:S(2)}, u32[]{:S(2)}) collective-permute-start(bf16[4,128,128]{2,1,0:T(8,128)(2,1)S(1)} %bitcast_select_fusion), channel_id=1, source_target_pairs={{32,0},{96,64},{160,128},{224,192},{272,304},{336,368},{400,432},{... | collective-permute-start | bytes 393224 | tf_op jit(solution)/shard_map/ppermute | solution.py:56
  9.8 7.3 %collective-permute-start.2 = (bf16[4,128,128]{2,1,0:T(8,128)(2,1)S(1)}, bf16[4,128,128]{2,1,0:T(8,128)(2,1)S(1)}, u32[]{:S(2)}, u32[]{:S(2)}) collective-permute-start(bf16[4,128,128]{2,1,0:T(8,128)(2,1)S(1)} %bitcast_select_fusion), channel_id=1, source_target_pairs={{48,0},{112,64},{176,128},{240,192},{256,304},{320,368},{384,432},... | collective-permute-start | bytes 393224 | tf_op jit(solution)/shard_map/ppermute | solution.py:56
  11.1 6.0 %collective-permute-start = (bf16[4,128,128]{2,1,0:T(8,128)(2,1)S(1)}, bf16[4,128,128]{2,1,0:T(8,128)(2,1)S(1)}, u32[]{:S(2)}, u32[]{:S(2)}) collective-permute-start(bf16[4,128,128]{2,1,0:T(8,128)(2,1)S(1)} %bitcast_select_fusion), channel_id=1, source_target_pairs={{16,0},{80,64},{144,128},{208,192},{288,304},{352,368},{416,432},{... | collective-permute-start | bytes 393224 | tf_op jit(solution)/shard_map/ppermute | solution.py:56
  95.6 1.2 copy-start.1
  97.5 4.0 %collective-permute-start.3 = (bf16[64,128]{1,0:T(8,128)(2,1)S(1)}, bf16[64,128]{1,0:T(8,128)(2,1)S(1)}, u32[]{:S(2)}, u32[]{:S(2)}) collective-permute-start(bf16[64,128]{1,0:T(8,128)(2,1)S(1)} %fusion.116), channel_id=1, source_target_pairs={{0,64},{496,432},{1,65},{497,433},{2,66},{498,434},{3,67},{499,435... | collective-permute-start | bytes 49160 | tf_op jit(solution)/shard_map/ppermute | solution.py:116
  104.4 0.9 collective-permute-start.4
  108.1 0.7 collective-permute-start.5
  111.7 0.7 collective-permute-start.6
  129.2 2.0 %collective-permute-start.7 = (f32[1024]{0:T(1024)S(1)}, f32[1024]{0:T(1024)S(1)}, u32[]{:S(2)}, u32[]{:S(2)}) collective-permute-start(f32[1024]{0:T(1024)S(1)} %reshape_squeeze.3), channel_id=1, source_target_pairs={{192,176},{304,288},{193,177},{305,289},{194,178},{306,290},{195,1... | collective-permute-start | bytes 12296 | tf_op jit(solution)/shard_map/ppermute | solution.py:129
  129.8 1.4 collective-permute-start.8
  130.5 0.7 collective-permute-start.9
  131.2 2.6 %collective-permute-start.10 = (f32[1024]{0:T(1024)S(1)}, f32[1024]{0:T(1024)S(1)}, u32[]{:S(2)}, u32[]{:S(2)}) collective-permute-start(f32[1024]{0:T(1024)S(1)} %add_add_fusion.1), channel_id=1, source_target_pairs={{160,144},{176,128},{192,224},{208,240},{272,256},{288,336},{304,3... | collective-permute-start | bytes 12296 | tf_op jit(solution)/shard_map/ppermute | solution.py:129
  131.9 2.0 %collective-permute-start.11 = (f32[1024]{0:T(1024)S(1)}, f32[1024]{0:T(1024)S(1)}, u32[]{:S(2)}, u32[]{:S(2)}) collective-permute-start(f32[1024]{0:T(1024)S(1)} %add_add_fusion.1), channel_id=1, source_target_pairs={{160,112},{176,96},{192,80},{208,64},{272,384},{288,400},{304,416}... | collective-permute-start | bytes 12296 | tf_op jit(solution)/shard_map/ppermute | solution.py:129
  132.6 23.9 %collective-permute-start.12 = (f32[1024]{0:T(1024)S(1)}, f32[1024]{0:T(1024)S(1)}, u32[]{:S(2)}, u32[]{:S(2)}) collective-permute-start(f32[1024]{0:T(1024)S(1)} %add_add_fusion.1), channel_id=1, source_target_pairs={{160,48},{176,32},{192,16},{208,0},{272,448},{288,464},{304,480},{... | collective-permute-start | bytes 12296 | tf_op jit(solution)/shard_map/ppermute | solution.py:129
Sparse Core Ops, SparseCore 0:
  19.0 68.9 all-gather.3

commit v11 on v10

--- a/solution.py
+++ b/solution.py
@@ -62,10 +62,11 @@
         return jnp.concatenate([rows, left_edge, right_edge, tail], axis=0)
 
     packed = jnp.stack([site_rows(part) for part in parts], axis=0)
-    both = lax.all_gather(packed, "sec", axis=1, tiled=False)
-    nsec = both.shape[1]
-    lefts = both[0, :, body]
-    rights = both[0, :, body + 1]
+    gathered = lax.all_gather(packed, "sec", axis=0, tiled=False)
+    nsec = gathered.shape[0]
+    both = [gathered[:, t] for t in range(span)]
+    lefts = gathered[:, 0, body]
+    rights = gathered[:, 0, body + 1]
 
     row0 = sec_index * group
     occ_mine = lax.dynamic_slice_in_dim(occupation, row0, group, axis=0)
@@ -93,7 +94,7 @@
     def apply(vector, which):
         spread = slots[which][:, :, :, None] * vector[:, None, None, :]
         spread = spread.reshape(group, nsec, body)
-        spread = jnp.pad(spread, ((0, 0), (0, 0), (0, both.shape[2] - body)))
+        spread = jnp.pad(spread, ((0, 0), (0, 0), (0, both[which].shape[1] - body)))
         products = jnp.einsum(
             "kqr,qrb->kb", spread, both[which], preferred_element_type=jnp.float32
         )

time: 167 us -> 166 us (level)
  the two profiles are of different devices: /device:TPU:1 before, /device:TPU:16 now
where the time goes in v11:
time: 166 us; the launch traced here: 165 us
  waiting for transfers between devices  50.9 us (31%)
  blocking collectives  50.9 us (31%)
  local copies, waits for them, and re-layouts  15.3 us (9%)
  between operations  14.3 us (9%)
  matrix products  13.3 us (8%)
  starting transfers between devices  12.6 us (8%)
  other arithmetic  8.05 us (5%)
    all_gather x1, blocking collectives, per_device(): occ_group = lax.all_gather(occ_mine, 'seg', axis=1, tiled=True)  35.3 us
    ppermute x6, waiting for transfers between devices, per_device(): received = [lax.ppermute(full, 'seg', pairs) for pairs in perms]  19.4 us
    all_gather x1, waiting for transfers between devices, per_device(): gathered = lax.all_gather(packed, 'sec', axis=0, tiled=False)  15.9 us
    all_gather x1, blocking collectives, per_device(): tiles = lax.all_gather(tile, 'sec', axis=0, tiled=False)  15.6 us
    dot_general x16, matrix products, apply(): jnp.einsum('kqr,qrb->kb', spread, both[which], preferred_element_type=jnp...  13.3 us
    mul x24, local copies, waits for them, and re-layouts, apply(): spread = slots[which][:, :, :, None] * vector[:, None, None, :]  11.6 us
    ppermute x3, waiting for transfers between devices, per_device(): vector = lax.ppermute(vector, 'seg', hop)  8.43 us
    ppermute x3, waiting for transfers between devices, per_device(): parts.append(lax.ppermute(local, 'seg', feed))  7.17 us
  transfers between devices with their start and end apart: 14, of which 5 were waited for; matrix products, arithmetic and copies ran while one was open for 8% of the time, Pallas kernels for 0%

profile of v11, /device:TPU:16, one launch (start us, length us, event | category | flops | bytes accessed | tf_op | source)
XLA Modules:
  0.0 165.3 jit_solution(15816358416580794730)
XLA Ops:
  6.5 1.0 copy.13
  7.6 0.9 bitcast_select_fusion
  8.5 1.3 collective-permute-start.2
  9.8 1.3 collective-permute-start.1
  11.1 1.3 collective-permute-start
  12.5 7.2 %collective-permute-done.2 = bf16[4,128,128]{2,1,0:T(8,128)(2,1)S(1)} collective-permute-done((bf16[4,128,128]{2,1,0:T(8,128)(2,1)S(1)}, bf16[4,128,128]{2,1,0:T(8,128)(2,1)S(1)}, u32[]{:S(2)}, u32[]{:S(2)}) %collective-permute-start.2) | collective-permute-done | bytes 131104 | tf_op jit(solution)/shard_map/ppermute | solution.py:56
  21.6 35.3 %all-gather.1 = s32[32,1,64]{2,1,0:T(1,128)S(1)} all-gather(s32[1,1,64]{2,1,0:T(1,128)S(1)} %dynamic-slice_bitcast_fusion), channel_id=1, replica_groups=mesh['seg'=32,'sec'=16] {'seg'}, dimensions={0}, use_global_device_ids=true | all-gather | bytes 8448 | tf_op jit(solution)/shard_map/all_gather | solution.py:73
  58.1 1.3 mul.355
  60.1 1.3 mul.350
  62.1 2.1 %mul.360 = bf16[64,16,4,128]{3,2,0,1:T(4,128)(2,1)} broadcast(bf16[64,16,4]{2,0,1:T(8,128)(2,1)S(1)} %broadcast_multiply_fusion.17), dimensions={0,1,2} | broadcast | bytes 1056768 | tf_op jit(solution)/shard_map/mul | solution.py:95
  64.2 1.5 mul.361
  66.0 2.1 %mul.365 = bf16[64,16,4,128]{3,2,0,1:T(4,128)(2,1)} broadcast(bf16[64,16,4]{2,0,1:T(8,128)(2,1)S(1)} %broadcast_multiply_fusion.16), dimensions={0,1,2} | broadcast | bytes 1056768 | tf_op jit(solution)/shard_map/mul | solution.py:95
  68.0 2.3 %mul.366 = bf16[64,16,512]{2,0,1:T(8,128)(2,1)} reshape(bf16[64,16,4,128]{3,2,0,1:T(4,128)(2,1)} %mul.365) | data formatting | bytes 2097152 | tf_op jit(solution)/shard_map/mul | solution.py:95
  70.4 15.9 %all-gather.4.cloned.1.call-done = bf16[64,528,128]{2,1,0:T(8,128)(2,1)} async-done(((bf16[4,528,128]{2,1,0:T(8,128)(2,1)}), bf16[64,528,128]{2,1,0:T(8,128)(2,1)}) %all-gather.4.cloned.1.call-update) | async-done | bytes 8650768 | tf_op jit(solution)/shard_map/all_gather | solution.py:65
  88.6 1.3 broadcast_multiply_fusion.15
  89.9 2.4 %fusion.89 = bf16[64,128]{1,0:T(8,128)(2,1)S(1)} fusion(bf16[16,4,528,128]{3,2,1,0:T(8,128)(2,1)} %bitcast.299, bf16[64,16,512]{2,0,1:T(8,128)(2,1)S(1)} %broadcast_multiply_fusion.15), kind=kOutput, calls=%fused_computation.57 | convolution fusion | flops 138420224 | bytes 3227648 | tf_op jit(solution)/shard_map/kqr,qrb->kb/dot_general | solution.py:98
  92.4 2.8 %fusion.101 = bf16[64,128]{1,0:T(8,128)(2,1)S(1)} fusion(bf16[16,4,528,128]{3,2,1,0:T(8,128)(2,1)} %bitcast.300, bf16[64,16,512]{2,0,1:T(8,128)(2,1)S(1)} %broadcast_multiply_fusion.14), kind=kOutput, calls=%fused_computation.61 | convolution fusion | flops 138420224 | bytes 3227648 | tf_op jit(solution)/shard_map/kqr,qrb->kb/dot_general | solution.py:98
  100.3 1.5 collective-permute-start.4
  101.7 7.0 %collective-permute-done.4 = bf16[64,128]{1,0:T(8,128)(2,1)S(1)} collective-permute-done((bf16[64,128]{1,0:T(8,128)(2,1)S(1)}, bf16[64,128]{1,0:T(8,128)(2,1)S(1)}, u32[]{:S(2)}, u32[]{:S(2)}) %collective-permute-start.4) | collective-permute-done | bytes 16416 | tf_op jit(solution)/shard_map/ppermute | solution.py:117
  111.6 1.3 collective-permute-start.5
  112.9 1.4 collective-permute-done.5
  118.1 15.6 %all_gather.16 = f32[16,8,128]{2,1,0:T(8,128)S(1)} all-gather(f32[1,8,128]{2,1,0:T(8,128)S(1)} %scatter.4), channel_id=1, replica_groups=mesh['seg'=32,'sec'=16] {'sec'}, dimensions={0}, use_global_device_ids=true | all-gather | bytes 69632 | tf_op jit(solution)/shard_map/all_gather | solution.py:126
  137.1 1.3 collective-permute-start.10
  138.4 19.4 %collective-permute-done.10 = f32[1024]{0:T(1024)S(1)} collective-permute-done((f32[1024]{0:T(1024)S(1)}, f32[1024]{0:T(1024)S(1)}, u32[]{:S(2)}, u32[]{:S(2)}) %collective-permute-start.10) | collective-permute-done | bytes 4128 | tf_op jit(solution)/shard_map/ppermute | solution.py:130
  (126 shorter events, 22.5 us)
Async XLA Ops:
  6.5 14.9 %copy-start = (s32[1024,1]{0,1:T(1,128)S(1)}, s32[1024,1]{0,1:T(1,128)}, u32[]{:S(2)}) copy-start(s32[1024,1]{0,1:T(1,128)} %param.13) | copy-start | bytes 12292
  6.5 79.8 %all-gather.4.cloned.1.call-start = ((), (), s32[]{:S(2)}) async-start(), calls=%async_computation | async-start | bytes 9191424 | tf_op jit(solution)/shard_map/all_gather | solution.py:65
  8.5 11.1 %collective-permute-start.2 = (bf16[4,128,128]{2,1,0:T(8,128)(2,1)S(1)}, bf16[4,128,128]{2,1,0:T(8,128)(2,1)S(1)}, u32[]{:S(2)}, u32[]{:S(2)}) collective-permute-start(bf16[4,128,128]{2,1,0:T(8,128)(2,1)S(1)} %bitcast_select_fusion), channel_id=1, source_target_pairs={{48,0},{112,64},{176,128},{240,192},{256,304},{320,368},{384,432},... | collective-permute-start | bytes 393224 | tf_op jit(solution)/shard_map/ppermute | solution.py:56
  9.8 9.9 %collective-permute-start.1 = (bf16[4,128,128]{2,1,0:T(8,128)(2,1)S(1)}, bf16[4,128,128]{2,1,0:T(8,128)(2,1)S(1)}, u32[]{:S(2)}, u32[]{:S(2)}) collective-permute-start(bf16[4,128,128]{2,1,0:T(8,128)(2,1)S(1)} %bitcast_select_fusion), channel_id=1, source_target_pairs={{32,0},{96,64},{160,128},{224,192},{272,304},{336,368},{400,432},{... | collective-permute-start | bytes 393224 | tf_op jit(solution)/shard_map/ppermute | solution.py:56
  11.1 8.6 %collective-permute-start = (bf16[4,128,128]{2,1,0:T(8,128)(2,1)S(1)}, bf16[4,128,128]{2,1,0:T(8,128)(2,1)S(1)}, u32[]{:S(2)}, u32[]{:S(2)}) collective-permute-start(bf16[4,128,128]{2,1,0:T(8,128)(2,1)S(1)} %bitcast_select_fusion), channel_id=1, source_target_pairs={{16,0},{80,64},{144,128},{208,192},{288,304},{352,368},{416,432},{... | collective-permute-start | bytes 393224 | tf_op jit(solution)/shard_map/ppermute | solution.py:56
  89.9 5.4 %copy-start.2 = (bf16[64,528,128]{2,1,0:T(8,128)(2,1)S(1)}, bf16[64,528,128]{2,1,0:T(8,128)(2,1)}, u32[]{:S(2)}) copy-start(bf16[64,528,128]{2,1,0:T(8,128)(2,1)} %all-gather.4.cloned.1.call-done) | copy-start | bytes 25952260
  96.1 1.3 copy-start.1
  96.7 0.7 collective-permute-start.3
  100.3 8.5 %collective-permute-start.4 = (bf16[64,128]{1,0:T(8,128)(2,1)S(1)}, bf16[64,128]{1,0:T(8,128)(2,1)S(1)}, u32[]{:S(2)}, u32[]{:S(2)}) collective-permute-start(bf16[64,128]{1,0:T(8,128)(2,1)S(1)} %fusion.122), channel_id=1, source_target_pairs={{64,128},{432,368},{65,129},{433,369},{66,130},{434,370},{67,131},... | collective-permute-start | bytes 49160 | tf_op jit(solution)/shard_map/ppermute | solution.py:117
  111.6 2.7 %collective-permute-start.5 = (bf16[64,128]{1,0:T(8,128)(2,1)S(1)}, bf16[64,128]{1,0:T(8,128)(2,1)S(1)}, u32[]{:S(2)}, u32[]{:S(2)}) collective-permute-start(bf16[64,128]{1,0:T(8,128)(2,1)S(1)} %fusion.119), channel_id=1, source_target_pairs={{128,192},{368,304},{129,193},{369,305},{130,194},{370,306},{131,1... | collective-permute-start | bytes 49160 | tf_op jit(solution)/shard_map/ppermute | solution.py:117
  117.2 0.7 collective-permute-start.6
  133.7 2.0 %collective-permute-start.9 = (f32[1024]{0:T(1024)S(1)}, f32[1024]{0:T(1024)S(1)}, u32[]{:S(2)}, u32[]{:S(2)}) collective-permute-start(f32[1024]{0:T(1024)S(1)} %reshape_squeeze.3), channel_id=1, source_target_pairs={{192,160},{304,272},{193,161},{305,273},{194,162},{306,274},{195,1... | collective-permute-start | bytes 12296 | tf_op jit(solution)/shard_map/ppermute | solution.py:130
  134.4 1.4 collective-permute-start.8
  135.1 0.7 collective-permute-start.7
  135.8 2.6 %collective-permute-start.12 = (f32[1024]{0:T(1024)S(1)}, f32[1024]{0:T(1024)S(1)}, u32[]{:S(2)}, u32[]{:S(2)}) collective-permute-start(f32[1024]{0:T(1024)S(1)} %add_add_fusion.1), channel_id=1, source_target_pairs={{160,48},{176,32},{192,16},{208,0},{272,448},{288,464},{304,480},{... | collective-permute-start | bytes 12296 | tf_op jit(solution)/shard_map/ppermute | solution.py:130
  136.5 2.0 %collective-permute-start.11 = (f32[1024]{0:T(1024)S(1)}, f32[1024]{0:T(1024)S(1)}, u32[]{:S(2)}, u32[]{:S(2)}) collective-permute-start(f32[1024]{0:T(1024)S(1)} %add_add_fusion.1), channel_id=1, source_target_pairs={{160,112},{176,96},{192,80},{208,64},{272,384},{288,400},{304,416}... | collective-permute-start | bytes 12296 | tf_op jit(solution)/shard_map/ppermute | solution.py:130
  137.1 20.7 %collective-permute-start.10 = (f32[1024]{0:T(1024)S(1)}, f32[1024]{0:T(1024)S(1)}, u32[]{:S(2)}, u32[]{:S(2)}) collective-permute-start(f32[1024]{0:T(1024)S(1)} %add_add_fusion.1), channel_id=1, source_target_pairs={{160,144},{176,128},{192,224},{208,240},{272,256},{288,336},{304,3... | collective-permute-start | bytes 12296 | tf_op jit(solution)/shard_map/ppermute | solution.py:130
Sparse Core Ops, SparseCore 0:
  21.5 64.7 all-gather.3

commit v12 on v11

--- a/solution.py
+++ b/solution.py
@@ -100,9 +100,12 @@
         )
         return products.astype(jnp.bfloat16)
 
-    first_left = jnp.take(lefts, start_group, axis=0)
-    first_right = jnp.take(rights, sector_end, axis=0)
-    first = jnp.where(is_left, first_left, first_right)
+    first_sector = jnp.where(is_left, start_group, sector_end)
+    first_hot = (first_sector[:, None] == sector_ids[None, :]).astype(jnp.bfloat16)
+    edge_rows = jnp.where(is_left, lefts, rights)
+    first = jnp.einsum(
+        "kq,qa->ka", first_hot, edge_rows, preferred_element_type=jnp.float32
+    ).astype(jnp.bfloat16)
     vector = jnp.where(depth == 0, first, jnp.zeros_like(first))
 
     chain_steps = half_count // span

time: 166 us -> 165 us (level)
  local copies, waits for them, and re-layouts: 15.3 us -> 13.1 us
where the time goes in v12:
time: 165 us; the launch traced here: 164 us
  waiting for transfers between devices  51 us (31%)
  blocking collectives  50.8 us (31%)
  between operations  14.3 us (9%)
  matrix products  13.5 us (8%)
  local copies, waits for them, and re-layouts  13.1 us (8%)
  starting transfers between devices  12.6 us (8%)
  other arithmetic  8.79 us (5%)
    all_gather x1, blocking collectives, per_device(): occ_group = lax.all_gather(occ_mine, 'seg', axis=1, tiled=True)  35.3 us
    ppermute x6, waiting for transfers between devices, per_device(): received = [lax.ppermute(full, 'seg', pairs) for pairs in perms]  19.4 us
    all_gather x1, waiting for transfers between devices, per_device(): gathered = lax.all_gather(packed, 'sec', axis=0, tiled=False)  15.9 us
    all_gather x1, blocking collectives, per_device(): tiles = lax.all_gather(tile, 'sec', axis=0, tiled=False)  15.5 us
    dot_general x16, matrix products, apply(): jnp.einsum('kqr,qrb->kb', spread, both[which], preferred_element_type=jnp...  13.4 us
    mul x24, local copies, waits for them, and re-layouts, apply(): spread = slots[which][:, :, :, None] * vector[:, None, None, :]  11.6 us
    ppermute x3, waiting for transfers between devices, per_device(): vector = lax.ppermute(vector, 'seg', hop)  8.43 us
    ppermute x3, waiting for transfers between devices, per_device(): parts.append(lax.ppermute(local, 'seg', feed))  7.17 us
  transfers between devices with their start and end apart: 14, of which 5 were waited for; matrix products, arithmetic and copies ran while one was open for 8% of the time, Pallas kernels for 0%

profile of v12, /device:TPU:16, one launch (start us, length us, event | category | flops | bytes accessed | tf_op | source)
XLA Modules:
  0.0 164.1 jit_solution(13460668027096481548)
XLA Ops:
  6.5 1.0 copy.13
  7.6 0.9 bitcast_select_fusion
  8.5 1.3 collective-permute-start.2
  9.8 1.3 collective-permute-start.1
  11.1 1.3 collective-permute-start
  12.5 7.2 %collective-permute-done.2 = bf16[4,128,128]{2,1,0:T(8,128)(2,1)S(1)} collective-permute-done((bf16[4,128,128]{2,1,0:T(8,128)(2,1)S(1)}, bf16[4,128,128]{2,1,0:T(8,128)(2,1)S(1)}, u32[]{:S(2)}, u32[]{:S(2)}) %collective-permute-start.2) | collective-permute-done | bytes 131104 | tf_op jit(solution)/shard_map/ppermute | solution.py:56
  21.6 35.3 %all-gather.1 = s32[32,1,64]{2,1,0:T(1,128)S(1)} all-gather(s32[1,1,64]{2,1,0:T(1,128)S(1)} %dynamic-slice_bitcast_fusion), channel_id=1, replica_groups=mesh['seg'=32,'sec'=16] {'seg'}, dimensions={0}, use_global_device_ids=true | all-gather | bytes 8448 | tf_op jit(solution)/shard_map/all_gather | solution.py:73
  58.1 1.3 mul.355
  60.1 1.3 mul.350
  62.1 2.1 %mul.360 = bf16[64,16,4,128]{3,2,0,1:T(4,128)(2,1)} broadcast(bf16[64,16,4]{2,0,1:T(8,128)(2,1)S(1)} %broadcast_multiply_fusion.17), dimensions={0,1,2} | broadcast | bytes 1056768 | tf_op jit(solution)/shard_map/mul | solution.py:95
  64.2 1.5 mul.361
  66.0 2.1 %mul.365 = bf16[64,16,4,128]{3,2,0,1:T(4,128)(2,1)} broadcast(bf16[64,16,4]{2,0,1:T(8,128)(2,1)S(1)} %broadcast_multiply_fusion.16), dimensions={0,1,2} | broadcast | bytes 1056768 | tf_op jit(solution)/shard_map/mul | solution.py:95
  68.0 2.3 %mul.366 = bf16[64,16,512]{2,0,1:T(8,128)(2,1)} reshape(bf16[64,16,4,128]{3,2,0,1:T(4,128)(2,1)} %mul.365) | data formatting | bytes 2097152 | tf_op jit(solution)/shard_map/mul | solution.py:95
  70.4 15.9 %all-gather.4.cloned.1.call-done = bf16[64,528,128]{2,1,0:T(8,128)(2,1)} async-done(((bf16[4,528,128]{2,1,0:T(8,128)(2,1)}), bf16[64,528,128]{2,1,0:T(8,128)(2,1)}) %all-gather.4.cloned.1.call-update) | async-done | bytes 8650768 | tf_op jit(solution)/shard_map/all_gather | solution.py:65
  87.4 1.3 broadcast_multiply_fusion.15
  88.7 2.4 %fusion.89 = bf16[64,128]{1,0:T(8,128)(2,1)S(1)} fusion(bf16[16,4,528,128]{3,2,1,0:T(8,128)(2,1)} %bitcast.298, bf16[64,16,512]{2,0,1:T(8,128)(2,1)S(1)} %broadcast_multiply_fusion.15), kind=kOutput, calls=%fused_computation.55 | convolution fusion | flops 138420224 | bytes 3227648 | tf_op jit(solution)/shard_map/kqr,qrb->kb/dot_general | solution.py:98
  91.2 2.8 %fusion.101 = bf16[64,128]{1,0:T(8,128)(2,1)S(1)} fusion(bf16[16,4,528,128]{3,2,1,0:T(8,128)(2,1)} %bitcast.299, bf16[64,16,512]{2,0,1:T(8,128)(2,1)S(1)} %broadcast_multiply_fusion.14), kind=kOutput, calls=%fused_computation.59 | convolution fusion | flops 138420224 | bytes 3227648 | tf_op jit(solution)/shard_map/kqr,qrb->kb/dot_general | solution.py:98
  99.1 1.5 collective-permute-start.4
  100.6 7.0 %collective-permute-done.4 = bf16[64,128]{1,0:T(8,128)(2,1)S(1)} collective-permute-done((bf16[64,128]{1,0:T(8,128)(2,1)S(1)}, bf16[64,128]{1,0:T(8,128)(2,1)S(1)}, u32[]{:S(2)}, u32[]{:S(2)}) %collective-permute-start.4) | collective-permute-done | bytes 16416 | tf_op jit(solution)/shard_map/ppermute | solution.py:120
  110.5 1.3 collective-permute-start.5
  111.7 1.4 collective-permute-done.5
  116.9 15.5 %all_gather.16 = f32[16,8,128]{2,1,0:T(8,128)S(1)} all-gather(f32[1,8,128]{2,1,0:T(8,128)S(1)} %scatter.4), channel_id=1, replica_groups=mesh['seg'=32,'sec'=16] {'sec'}, dimensions={0}, use_global_device_ids=true | all-gather | bytes 69632 | tf_op jit(solution)/shard_map/all_gather | solution.py:129
  135.9 1.3 collective-permute-start.10
  137.2 19.4 %collective-permute-done.10 = f32[1024]{0:T(1024)S(1)} collective-permute-done((f32[1024]{0:T(1024)S(1)}, f32[1024]{0:T(1024)S(1)}, u32[]{:S(2)}, u32[]{:S(2)}) %collective-permute-start.10) | collective-permute-done | bytes 4128 | tf_op jit(solution)/shard_map/ppermute | solution.py:133
  (120 shorter events, 21.3 us)
Async XLA Ops:
  6.5 14.9 %copy-start = (s32[1024,1]{0,1:T(1,128)S(1)}, s32[1024,1]{0,1:T(1,128)}, u32[]{:S(2)}) copy-start(s32[1024,1]{0,1:T(1,128)} %param.11) | copy-start | bytes 12292
  6.5 79.8 %all-gather.4.cloned.1.call-start = ((), (), s32[]{:S(2)}) async-start(), calls=%async_computation | async-start | bytes 9191424 | tf_op jit(solution)/shard_map/all_gather | solution.py:65
  8.5 11.1 %collective-permute-start.2 = (bf16[4,128,128]{2,1,0:T(8,128)(2,1)S(1)}, bf16[4,128,128]{2,1,0:T(8,128)(2,1)S(1)}, u32[]{:S(2)}, u32[]{:S(2)}) collective-permute-start(bf16[4,128,128]{2,1,0:T(8,128)(2,1)S(1)} %bitcast_select_fusion), channel_id=1, source_target_pairs={{48,0},{112,64},{176,128},{240,192},{256,304},{320,368},{384,432},... | collective-permute-start | bytes 393224 | tf_op jit(solution)/shard_map/ppermute | solution.py:56
  9.8 9.9 %collective-permute-start.1 = (bf16[4,128,128]{2,1,0:T(8,128)(2,1)S(1)}, bf16[4,128,128]{2,1,0:T(8,128)(2,1)S(1)}, u32[]{:S(2)}, u32[]{:S(2)}) collective-permute-start(bf16[4,128,128]{2,1,0:T(8,128)(2,1)S(1)} %bitcast_select_fusion), channel_id=1, source_target_pairs={{32,0},{96,64},{160,128},{224,192},{272,304},{336,368},{400,432},{... | collective-permute-start | bytes 393224 | tf_op jit(solution)/shard_map/ppermute | solution.py:56
  11.1 8.6 %collective-permute-start = (bf16[4,128,128]{2,1,0:T(8,128)(2,1)S(1)}, bf16[4,128,128]{2,1,0:T(8,128)(2,1)S(1)}, u32[]{:S(2)}, u32[]{:S(2)}) collective-permute-start(bf16[4,128,128]{2,1,0:T(8,128)(2,1)S(1)} %bitcast_select_fusion), channel_id=1, source_target_pairs={{16,0},{80,64},{144,128},{208,192},{288,304},{352,368},{416,432},{... | collective-permute-start | bytes 393224 | tf_op jit(solution)/shard_map/ppermute | solution.py:56
  88.7 5.4 %copy-start.2 = (bf16[64,528,128]{2,1,0:T(8,128)(2,1)S(1)}, bf16[64,528,128]{2,1,0:T(8,128)(2,1)}, u32[]{:S(2)}) copy-start(bf16[64,528,128]{2,1,0:T(8,128)(2,1)} %all-gather.4.cloned.1.call-done) | copy-start | bytes 25952260
  94.9 1.3 copy-start.1
  95.5 0.7 collective-permute-start.3
  99.1 8.5 %collective-permute-start.4 = (bf16[64,128]{1,0:T(8,128)(2,1)S(1)}, bf16[64,128]{1,0:T(8,128)(2,1)S(1)}, u32[]{:S(2)}, u32[]{:S(2)}) collective-permute-start(bf16[64,128]{1,0:T(8,128)(2,1)S(1)} %fusion.122), channel_id=1, source_target_pairs={{64,128},{432,368},{65,129},{433,369},{66,130},{434,370},{67,131},... | collective-permute-start | bytes 49160 | tf_op jit(solution)/shard_map/ppermute | solution.py:120
  110.5 2.7 %collective-permute-start.5 = (bf16[64,128]{1,0:T(8,128)(2,1)S(1)}, bf16[64,128]{1,0:T(8,128)(2,1)S(1)}, u32[]{:S(2)}, u32[]{:S(2)}) collective-permute-start(bf16[64,128]{1,0:T(8,128)(2,1)S(1)} %fusion.119), channel_id=1, source_target_pairs={{128,192},{368,304},{129,193},{369,305},{130,194},{370,306},{131,1... | collective-permute-start | bytes 49160 | tf_op jit(solution)/shard_map/ppermute | solution.py:120
  116.1 0.7 collective-permute-start.6
  132.5 2.0 %collective-permute-start.9 = (f32[1024]{0:T(1024)S(1)}, f32[1024]{0:T(1024)S(1)}, u32[]{:S(2)}, u32[]{:S(2)}) collective-permute-start(f32[1024]{0:T(1024)S(1)} %reshape_squeeze.3), channel_id=1, source_target_pairs={{192,160},{304,272},{193,161},{305,273},{194,162},{306,274},{195,1... | collective-permute-start | bytes 12296 | tf_op jit(solution)/shard_map/ppermute | solution.py:133
  133.2 1.4 collective-permute-start.8
  133.9 0.7 collective-permute-start.7
  134.6 2.6 %collective-permute-start.12 = (f32[1024]{0:T(1024)S(1)}, f32[1024]{0:T(1024)S(1)}, u32[]{:S(2)}, u32[]{:S(2)}) collective-permute-start(f32[1024]{0:T(1024)S(1)} %add_add_fusion.1), channel_id=1, source_target_pairs={{160,48},{176,32},{192,16},{208,0},{272,448},{288,464},{304,480},{... | collective-permute-start | bytes 12296 | tf_op jit(solution)/shard_map/ppermute | solution.py:133
  135.2 2.0 %collective-permute-start.11 = (f32[1024]{0:T(1024)S(1)}, f32[1024]{0:T(1024)S(1)}, u32[]{:S(2)}, u32[]{:S(2)}) collective-permute-start(f32[1024]{0:T(1024)S(1)} %add_add_fusion.1), channel_id=1, source_target_pairs={{160,112},{176,96},{192,80},{208,64},{272,384},{288,400},{304,416}... | collective-permute-start | bytes 12296 | tf_op jit(solution)/shard_map/ppermute | solution.py:133
  135.9 20.7 %collective-permute-start.10 = (f32[1024]{0:T(1024)S(1)}, f32[1024]{0:T(1024)S(1)}, u32[]{:S(2)}, u32[]{:S(2)}) collective-permute-start(f32[1024]{0:T(1024)S(1)} %add_add_fusion.1), channel_id=1, source_target_pairs={{160,144},{176,128},{192,224},{208,240},{272,256},{288,336},{304,3... | collective-permute-start | bytes 12296 | tf_op jit(solution)/shard_map/ppermute | solution.py:133
Sparse Core Ops, SparseCore 0:
  21.5 64.7 all-gather.3

commit v13 on v12

--- a/solution.py
+++ b/solution.py
@@ -62,11 +62,11 @@
         return jnp.concatenate([rows, left_edge, right_edge, tail], axis=0)
 
     packed = jnp.stack([site_rows(part) for part in parts], axis=0)
-    gathered = lax.all_gather(packed, "sec", axis=0, tiled=False)
-    nsec = gathered.shape[0]
-    both = [gathered[:, t] for t in range(span)]
-    lefts = gathered[:, 0, body]
-    rights = gathered[:, 0, body + 1]
+    gathered = lax.all_gather(packed, "sec", axis=1, tiled=False)
+    nsec = gathered.shape[1]
+    both = [gathered[t] for t in range(span)]
+    lefts = gathered[0, :, body]
+    rights = gathered[0, :, body + 1]
 
     row0 = sec_index * group
     occ_mine = lax.dynamic_slice_in_dim(occupation, row0, group, axis=0)

time: 165 us -> 166 us (level)
  the two profiles are of different devices: /device:TPU:16 before, /device:TPU:1 now
where the time goes in v13:
time: 166 us; the launch traced here: 163 us
  blocking collectives  51 us (31%)
  waiting for transfers between devices  49 us (30%)
  local copies, waits for them, and re-layouts  17.5 us (11%)
  between operations  14.3 us (9%)
  starting transfers between devices  13.7 us (8%)
  matrix products  9.57 us (6%)
  other arithmetic  7.58 us (5%)
    all_gather x1, blocking collectives, per_device(): occ_group = lax.all_gather(occ_mine, 'seg', axis=1, tiled=True)  34.5 us
    ppermute x6, waiting for transfers between devices, per_device(): received = [lax.ppermute(full, 'seg', pairs) for pairs in perms]  22.6 us
    all_gather x1, waiting for transfers between devices, per_device(): gathered = lax.all_gather(packed, 'sec', axis=1, tiled=False)  20.9 us
    all_gather x1, blocking collectives, per_device(): tiles = lax.all_gather(tile, 'sec', axis=0, tiled=False)  16.5 us
    mul x24, local copies, waits for them, and re-layouts, apply(): spread = slots[which][:, :, :, None] * vector[:, None, None, :]  11.6 us
    dot_general x16, matrix products, apply(): jnp.einsum('kqr,qrb->kb', spread, both[which], preferred_element_type=jnp...  9.38 us
    ppermute x3, waiting for transfers between devices, per_device(): parts.append(lax.ppermute(local, 'seg', feed))  4.64 us
    ppermute x3, starting transfers between devices, per_device(): vector = lax.ppermute(vector, 'seg', hop)  4.61 us
  transfers between devices with their start and end apart: 14, of which 5 were waited for; matrix products, arithmetic and copies ran while one was open for 8% of the time, Pallas kernels for 0%

profile of v13, /device:TPU:1, one launch (start us, length us, event | category | flops | bytes accessed | tf_op | source)
XLA Modules:
  0.0 162.7 jit_solution(15432370876767590141)
XLA Ops:
  6.5 1.0 copy.10
  7.6 0.9 bitcast_select_fusion
  8.5 1.3 collective-permute-start.1
  9.8 1.3 collective-permute-start.2
  11.1 1.3 collective-permute-start
  12.5 3.3 %collective-permute-done.1 = bf16[4,128,128]{2,1,0:T(8,128)(2,1)S(1)} collective-permute-done((bf16[4,128,128]{2,1,0:T(8,128)(2,1)S(1)}, bf16[4,128,128]{2,1,0:T(8,128)(2,1)S(1)}, u32[]{:S(2)}, u32[]{:S(2)}) %collective-permute-start.1) | collective-permute-done | bytes 131104 | tf_op jit(solution)/shard_map/ppermute | solution.py:56
  15.8 1.4 collective-permute-done.2
  17.1 0.8 fusion.130
  18.0 0.9 pad_maximum_fusion
  19.0 34.5 %all-gather.1 = s32[32,1,64]{2,1,0:T(1,128)S(1)} all-gather(s32[1,1,64]{2,1,0:T(1,128)S(1)} %dynamic-slice_bitcast_fusion), channel_id=1, replica_groups=mesh['seg'=32,'sec'=16] {'seg'}, dimensions={0}, use_global_device_ids=true | all-gather | bytes 8448 | tf_op jit(solution)/shard_map/all_gather | solution.py:73
  54.8 1.3 mul.365
  56.8 1.3 mul.360
  58.9 2.1 %mul.355 = bf16[64,16,4,128]{3,2,0,1:T(4,128)(2,1)} broadcast(bf16[64,16,4]{2,0,1:T(8,128)(2,1)S(1)} %broadcast_multiply_fusion.18), dimensions={0,1,2} | broadcast | bytes 1056768 | tf_op jit(solution)/shard_map/mul | solution.py:95
  60.9 1.5 mul.356
  62.7 2.1 %mul.350 = bf16[64,16,4,128]{3,2,0,1:T(4,128)(2,1)} broadcast(bf16[64,16,4]{2,0,1:T(8,128)(2,1)S(1)} %broadcast_multiply_fusion.19), dimensions={0,1,2} | broadcast | bytes 1056768 | tf_op jit(solution)/shard_map/mul | solution.py:95
  64.7 2.3 %mul.351 = bf16[64,16,512]{2,0,1:T(8,128)(2,1)} reshape(bf16[64,16,4,128]{3,2,0,1:T(4,128)(2,1)} %mul.350) | data formatting | bytes 2097152 | tf_op jit(solution)/shard_map/mul | solution.py:95
  67.0 20.9 %all-gather.4.cloned.1.call-done = bf16[4,8448,128]{2,1,0:T(8,128)(2,1)} async-done(((bf16[4,528,128]{2,1,0:T(8,128)(2,1)}), bf16[4,8448,128]{2,1,0:T(8,128)(2,1)}) %all-gather.4.cloned.1.call-update) | async-done | bytes 8650768 | tf_op jit(solution)/shard_map/all_gather | solution.py:65
  88.0 0.9 broadcast_select_fusion
  89.2 3.8 %fusion.171 = (bf16[1,8448,128]{2,1,0:T(8,128)(2,1)S(1)}, bf16[1,8448,128]{2,1,0:T(8,128)(2,1)S(1)}, bf16[1,8448,128]{2,1,0:T(8,128)(2,1)S(1)}, bf16[1,8448,128]{2,1,0:T(8,128)(2,1)S(1)}) fusion(bf16[4,8448,128]{2,1,0:T(8,128)(2,1)} %all-gather.4.cloned.1.call-done), kind=kLoop, calls=%fused_computation.204 | loop fusion | bytes 17301504 | tf_op jit(solution)/shard_map/slice | solution.py:67
  96.3 3.1 %collective-permute-start.3 = (bf16[64,128]{1,0:T(8,128)(2,1)S(1)}, bf16[64,128]{1,0:T(8,128)(2,1)S(1)}, u32[]{:S(2)}, u32[]{:S(2)}) collective-permute-start(bf16[64,128]{1,0:T(8,128)(2,1)S(1)} %fusion.116), channel_id=1, source_target_pairs={{0,64},{496,432},{1,65},{497,433},{2,66},{498,434},{3,67},{499,435... | collective-permute-start | bytes 49160 | tf_op jit(solution)/shard_map/ppermute | solution.py:120
  99.5 0.9 collective-permute-done.3
  111.4 16.5 %all_gather.16 = f32[16,8,128]{2,1,0:T(8,128)S(1)} all-gather(f32[1,8,128]{2,1,0:T(8,128)S(1)} %scatter.4), channel_id=1, replica_groups=mesh['seg'=32,'sec'=16] {'sec'}, dimensions={0}, use_global_device_ids=true | all-gather | bytes 69632 | tf_op jit(solution)/shard_map/all_gather | solution.py:129
  131.4 1.3 collective-permute-start.12
  132.7 22.6 %collective-permute-done.12 = f32[1024]{0:T(1024)S(1)} collective-permute-done((f32[1024]{0:T(1024)S(1)}, f32[1024]{0:T(1024)S(1)}, u32[]{:S(2)}, u32[]{:S(2)}) %collective-permute-start.12) | collective-permute-done | bytes 4128 | tf_op jit(solution)/shard_map/ppermute | solution.py:133
  (119 shorter events, 21.4 us)
Async XLA Ops:
  6.5 12.4 %copy-start = (s32[1024,1]{0,1:T(1,128)S(1)}, s32[1024,1]{0,1:T(1,128)}, u32[]{:S(2)}) copy-start(s32[1024,1]{0,1:T(1,128)} %param.11) | copy-start | bytes 12292
  6.5 81.5 %all-gather.4.cloned.1.call-start = ((), (), s32[]{:S(2)}) async-start(), calls=%async_computation | async-start | bytes 9191424 | tf_op jit(solution)/shard_map/all_gather | solution.py:65
  8.5 7.3 %collective-permute-start.1 = (bf16[4,128,128]{2,1,0:T(8,128)(2,1)S(1)}, bf16[4,128,128]{2,1,0:T(8,128)(2,1)S(1)}, u32[]{:S(2)}, u32[]{:S(2)}) collective-permute-start(bf16[4,128,128]{2,1,0:T(8,128)(2,1)S(1)} %bitcast_select_fusion), channel_id=1, source_target_pairs={{32,0},{96,64},{160,128},{224,192},{272,304},{336,368},{400,432},{... | collective-permute-start | bytes 393224 | tf_op jit(solution)/shard_map/ppermute | solution.py:56
  9.8 7.3 %collective-permute-start.2 = (bf16[4,128,128]{2,1,0:T(8,128)(2,1)S(1)}, bf16[4,128,128]{2,1,0:T(8,128)(2,1)S(1)}, u32[]{:S(2)}, u32[]{:S(2)}) collective-permute-start(bf16[4,128,128]{2,1,0:T(8,128)(2,1)S(1)} %bitcast_select_fusion), channel_id=1, source_target_pairs={{48,0},{112,64},{176,128},{240,192},{256,304},{320,368},{384,432},... | collective-permute-start | bytes 393224 | tf_op jit(solution)/shard_map/ppermute | solution.py:56
  11.1 6.0 %collective-permute-start = (bf16[4,128,128]{2,1,0:T(8,128)(2,1)S(1)}, bf16[4,128,128]{2,1,0:T(8,128)(2,1)S(1)}, u32[]{:S(2)}, u32[]{:S(2)}) collective-permute-start(bf16[4,128,128]{2,1,0:T(8,128)(2,1)S(1)} %bitcast_select_fusion), channel_id=1, source_target_pairs={{16,0},{80,64},{144,128},{208,192},{288,304},{352,368},{416,432},{... | collective-permute-start | bytes 393224 | tf_op jit(solution)/shard_map/ppermute | solution.py:56
  94.4 1.2 copy-start.1
  96.3 4.0 %collective-permute-start.3 = (bf16[64,128]{1,0:T(8,128)(2,1)S(1)}, bf16[64,128]{1,0:T(8,128)(2,1)S(1)}, u32[]{:S(2)}, u32[]{:S(2)}) collective-permute-start(bf16[64,128]{1,0:T(8,128)(2,1)S(1)} %fusion.116), channel_id=1, source_target_pairs={{0,64},{496,432},{1,65},{497,433},{2,66},{498,434},{3,67},{499,435... | collective-permute-start | bytes 49160 | tf_op jit(solution)/shard_map/ppermute | solution.py:120
  103.2 0.9 collective-permute-start.4
  107.0 0.7 collective-permute-start.5
  110.5 0.7 collective-permute-start.6
  128.0 2.0 %collective-permute-start.7 = (f32[1024]{0:T(1024)S(1)}, f32[1024]{0:T(1024)S(1)}, u32[]{:S(2)}, u32[]{:S(2)}) collective-permute-start(f32[1024]{0:T(1024)S(1)} %reshape_squeeze.3), channel_id=1, source_target_pairs={{192,176},{304,288},{193,177},{305,289},{194,178},{306,290},{195,1... | collective-permute-start | bytes 12296 | tf_op jit(solution)/shard_map/ppermute | solution.py:133
  128.6 1.4 collective-permute-start.8
  129.3 0.7 collective-permute-start.9
  130.0 2.6 %collective-permute-start.10 = (f32[1024]{0:T(1024)S(1)}, f32[1024]{0:T(1024)S(1)}, u32[]{:S(2)}, u32[]{:S(2)}) collective-permute-start(f32[1024]{0:T(1024)S(1)} %add_add_fusion.1), channel_id=1, source_target_pairs={{160,144},{176,128},{192,224},{208,240},{272,256},{288,336},{304,3... | collective-permute-start | bytes 12296 | tf_op jit(solution)/shard_map/ppermute | solution.py:133
  130.7 2.0 %collective-permute-start.11 = (f32[1024]{0:T(1024)S(1)}, f32[1024]{0:T(1024)S(1)}, u32[]{:S(2)}, u32[]{:S(2)}) collective-permute-start(f32[1024]{0:T(1024)S(1)} %add_add_fusion.1), channel_id=1, source_target_pairs={{160,112},{176,96},{192,80},{208,64},{272,384},{288,400},{304,416}... | collective-permute-start | bytes 12296 | tf_op jit(solution)/shard_map/ppermute | solution.py:133
  131.4 23.9 %collective-permute-start.12 = (f32[1024]{0:T(1024)S(1)}, f32[1024]{0:T(1024)S(1)}, u32[]{:S(2)}, u32[]{:S(2)}) collective-permute-start(f32[1024]{0:T(1024)S(1)} %add_add_fusion.1), channel_id=1, source_target_pairs={{160,48},{176,32},{192,16},{208,0},{272,448},{288,464},{304,480},{... | collective-permute-start | bytes 12296 | tf_op jit(solution)/shard_map/ppermute | solution.py:133
Sparse Core Ops, SparseCore 0:
  19.0 68.9 all-gather.3

commit v14 on v12

--- a/solution.py
+++ b/solution.py
@@ -46,7 +46,7 @@
     depth = jnp.where(is_left, seg_index // span, (seg_count - 1 - seg_index) // span)
 
     local = blocks[0, :, 0]
-    local = jnp.where(is_left, local, jnp.swapaxes(local, 1, 2))
+    local = lax.cond(is_left, lambda x: x, lambda x: jnp.swapaxes(x, 1, 2), local)
     runs = seg_count // span
     parts = [local]
     for t in range(1, span):

time: 165 us -> 165 us (level)
  local copies, waits for them, and re-layouts: 13.1 us -> 15.2 us
where the time goes in v14:
time: 165 us
  waiting for transfers between devices  51.2 us (31%)
  blocking collectives  49.9 us (30%)
  local copies, waits for them, and re-layouts  15.2 us (9%)
  between operations  14.3 us (9%)
  matrix products  13.5 us (8%)
  starting transfers between devices  12.6 us (8%)
  other arithmetic  7.87 us (5%)
    all_gather x1, blocking collectives, per_device(): occ_group = lax.all_gather(occ_mine, 'seg', axis=1, tiled=True)  34.4 us
    ppermute x6, waiting for transfers between devices, per_device(): received = [lax.ppermute(full, 'seg', pairs) for pairs in perms]  19.4 us
    all_gather x1, waiting for transfers between devices, per_device(): gathered = lax.all_gather(packed, 'sec', axis=0, tiled=False)  15.9 us
    all_gather x1, blocking collectives, per_device(): tiles = lax.all_gather(tile, 'sec', axis=0, tiled=False)  15.6 us
    dot_general x16, matrix products, apply(): jnp.einsum('kqr,qrb->kb', spread, both[which], preferred_element_type=jnp...  13.3 us
    mul x24, local copies, waits for them, and re-layouts, apply(): spread = slots[which][:, :, :, None] * vector[:, None, None, :]  11.6 us
    ppermute x3, waiting for transfers between devices, per_device(): vector = lax.ppermute(vector, 'seg', hop)  8.43 us
    ppermute x3, waiting for transfers between devices, per_device(): parts.append(lax.ppermute(local, 'seg', feed))  7.38 us
  transfers between devices with their start and end apart: 14, of which 5 were waited for; matrix products, arithmetic and copies ran while one was open for 8% of the time, Pallas kernels for 0%

profile of v14, /device:TPU:16, one launch (start us, length us, event | category | flops | bytes accessed | tf_op | source)
XLA Modules:
  0.0 164.6 jit_solution(17715565625755970540)
XLA Ops:
  6.5 1.0 copy.27
  7.6 1.7 %conditional.1 = (bf16[4,128,128]{1,2,0:T(8,128)(2,1)}, bf16[512,128]{1,0:T(8,128)(2,1)S(1)}) conditional(s32[]{:T(128)} %convert_element_type.142, bf16[4,128,128]{1,2,0:T(8,128)(2,1)S(1)} %copy.100, bf16[4,128,128]{1,2,0:T(8,128)(2,1)S(1)} %copy.100), branch_computations={%region_9.10_spmd, %region_10.11_spmd} | conditional | bytes 524304 | solution.py:49
  9.3 1.3 collective-permute-start.2
  10.6 1.3 collective-permute-start.1
  11.9 1.3 collective-permute-start
  13.3 7.4 %collective-permute-done.2 = bf16[4,128,128]{1,2,0:T(8,128)(2,1)S(1)} collective-permute-done((bf16[4,128,128]{1,2,0:T(8,128)(2,1)}, bf16[4,128,128]{1,2,0:T(8,128)(2,1)S(1)}, u32[]{:S(2)}, u32[]{:S(2)}) %collective-permute-start.2) | collective-permute-done | bytes 131104 | tf_op jit(solution)/shard_map/ppermute | solution.py:56
  23.0 34.4 %all-gather.1 = s32[32,1,64]{2,1,0:T(1,128)S(1)} all-gather(s32[1,1,64]{2,1,0:T(1,128)S(1)} %dynamic-slice_bitcast_fusion), channel_id=1, replica_groups=mesh['seg'=32,'sec'=16] {'seg'}, dimensions={0}, use_global_device_ids=true | all-gather | bytes 8448 | tf_op jit(solution)/shard_map/all_gather | solution.py:73
  58.6 1.3 mul.355
  60.6 1.3 mul.350
  62.6 2.1 %mul.360 = bf16[64,16,4,128]{3,2,0,1:T(4,128)(2,1)} broadcast(bf16[64,16,4]{2,0,1:T(8,128)(2,1)S(1)} %broadcast_multiply_fusion.17), dimensions={0,1,2} | broadcast | bytes 1056768 | tf_op jit(solution)/shard_map/mul | solution.py:95
  64.7 1.5 mul.361
  66.5 2.1 %mul.365 = bf16[64,16,4,128]{3,2,0,1:T(4,128)(2,1)} broadcast(bf16[64,16,4]{2,0,1:T(8,128)(2,1)S(1)} %broadcast_multiply_fusion.16), dimensions={0,1,2} | broadcast | bytes 1056768 | tf_op jit(solution)/shard_map/mul | solution.py:95
  68.5 2.3 %mul.366 = bf16[64,16,512]{2,0,1:T(8,128)(2,1)} reshape(bf16[64,16,4,128]{3,2,0,1:T(4,128)(2,1)} %mul.365) | data formatting | bytes 2097152 | tf_op jit(solution)/shard_map/mul | solution.py:95
  70.9 15.9 %all-gather.4.cloned.1.call-done = bf16[64,528,128]{2,1,0:T(8,128)(2,1)} async-done(((bf16[4,528,128]{2,1,0:T(8,128)(2,1)}), bf16[64,528,128]{2,1,0:T(8,128)(2,1)}) %all-gather.4.cloned.1.call-update) | async-done | bytes 8650768 | tf_op jit(solution)/shard_map/all_gather | solution.py:65
  87.9 1.3 broadcast_multiply_fusion.15
  89.2 2.4 %fusion.89 = bf16[64,128]{1,0:T(8,128)(2,1)S(1)} fusion(bf16[16,4,528,128]{3,2,1,0:T(8,128)(2,1)} %bitcast.300, bf16[64,16,512]{2,0,1:T(8,128)(2,1)S(1)} %broadcast_multiply_fusion.15), kind=kOutput, calls=%fused_computation.55 | convolution fusion | flops 138420224 | bytes 3227648 | tf_op jit(solution)/shard_map/kqr,qrb->kb/dot_general | solution.py:98
  91.7 2.8 %fusion.101 = bf16[64,128]{1,0:T(8,128)(2,1)S(1)} fusion(bf16[16,4,528,128]{3,2,1,0:T(8,128)(2,1)} %bitcast.301, bf16[64,16,512]{2,0,1:T(8,128)(2,1)S(1)} %broadcast_multiply_fusion.14), kind=kOutput, calls=%fused_computation.59 | convolution fusion | flops 138420224 | bytes 3227648 | tf_op jit(solution)/shard_map/kqr,qrb->kb/dot_general | solution.py:98
  99.6 1.5 collective-permute-start.4
  101.0 7.0 %collective-permute-done.4 = bf16[64,128]{1,0:T(8,128)(2,1)S(1)} collective-permute-done((bf16[64,128]{1,0:T(8,128)(2,1)S(1)}, bf16[64,128]{1,0:T(8,128)(2,1)S(1)}, u32[]{:S(2)}, u32[]{:S(2)}) %collective-permute-start.4) | collective-permute-done | bytes 16416 | tf_op jit(solution)/shard_map/ppermute | solution.py:120
  110.9 1.3 collective-permute-start.5
  112.2 1.4 collective-permute-done.5
  117.4 15.6 %all_gather.16 = f32[16,8,128]{2,1,0:T(8,128)S(1)} all-gather(f32[1,8,128]{2,1,0:T(8,128)S(1)} %scatter.4), channel_id=1, replica_groups=mesh['seg'=32,'sec'=16] {'sec'}, dimensions={0}, use_global_device_ids=true | all-gather | bytes 69632 | tf_op jit(solution)/shard_map/all_gather | solution.py:129
  136.4 1.3 collective-permute-start.10
  137.7 19.4 %collective-permute-done.10 = f32[1024]{0:T(1024)S(1)} collective-permute-done((f32[1024]{0:T(1024)S(1)}, f32[1024]{0:T(1024)S(1)}, u32[]{:S(2)}, u32[]{:S(2)}) %collective-permute-start.10) | collective-permute-done | bytes 4128 | tf_op jit(solution)/shard_map/ppermute | solution.py:133
  (126 shorter events, 23.4 us)
Async XLA Ops:
  6.5 16.4 %copy-start = (s32[1024,1]{0,1:T(1,128)S(1)}, s32[1024,1]{0,1:T(1,128)}, u32[]{:S(2)}) copy-start(s32[1024,1]{0,1:T(1,128)} %param.13) | copy-start | bytes 12292
  6.5 80.2 %all-gather.4.cloned.1.call-start = ((), (), s32[]{:S(2)}) async-start(), calls=%async_computation | async-start | bytes 9191424 | tf_op jit(solution)/shard_map/all_gather | solution.py:65
  9.3 11.4 %collective-permute-start.2 = (bf16[4,128,128]{1,2,0:T(8,128)(2,1)}, bf16[4,128,128]{1,2,0:T(8,128)(2,1)S(1)}, u32[]{:S(2)}, u32[]{:S(2)}) collective-permute-start(bf16[4,128,128]{1,2,0:T(8,128)(2,1)} %get-tuple-element.25), channel_id=1, source_target_pairs={{48,0},{112,64},{176,128},{240,192},{256,304},{320,368},{384,432},... | collective-permute-start | bytes 393224 | tf_op jit(solution)/shard_map/ppermute | solution.py:56
  10.6 10.2 %collective-permute-start.1 = (bf16[4,128,128]{1,2,0:T(8,128)(2,1)}, bf16[4,128,128]{1,2,0:T(8,128)(2,1)S(1)}, u32[]{:S(2)}, u32[]{:S(2)}) collective-permute-start(bf16[4,128,128]{1,2,0:T(8,128)(2,1)} %get-tuple-element.25), channel_id=1, source_target_pairs={{32,0},{96,64},{160,128},{224,192},{272,304},{336,368},{400,432},{... | collective-permute-start | bytes 393224 | tf_op jit(solution)/shard_map/ppermute | solution.py:56
  11.9 9.0 %collective-permute-start = (bf16[4,128,128]{1,2,0:T(8,128)(2,1)}, bf16[4,128,128]{1,2,0:T(8,128)(2,1)S(1)}, u32[]{:S(2)}, u32[]{:S(2)}) collective-permute-start(bf16[4,128,128]{1,2,0:T(8,128)(2,1)} %get-tuple-element.25), channel_id=1, source_target_pairs={{16,0},{80,64},{144,128},{208,192},{288,304},{352,368},{416,432},{... | collective-permute-start | bytes 393224 | tf_op jit(solution)/shard_map/ppermute | solution.py:56
  89.2 5.4 %copy-start.2 = (bf16[64,528,128]{2,1,0:T(8,128)(2,1)S(1)}, bf16[64,528,128]{2,1,0:T(8,128)(2,1)}, u32[]{:S(2)}) copy-start(bf16[64,528,128]{2,1,0:T(8,128)(2,1)} %all-gather.4.cloned.1.call-done) | copy-start | bytes 25952260
  95.4 1.3 copy-start.1
  96.0 0.7 collective-permute-start.3
  99.6 8.5 %collective-permute-start.4 = (bf16[64,128]{1,0:T(8,128)(2,1)S(1)}, bf16[64,128]{1,0:T(8,128)(2,1)S(1)}, u32[]{:S(2)}, u32[]{:S(2)}) collective-permute-start(bf16[64,128]{1,0:T(8,128)(2,1)S(1)} %fusion.122), channel_id=1, source_target_pairs={{64,128},{432,368},{65,129},{433,369},{66,130},{434,370},{67,131},... | collective-permute-start | bytes 49160 | tf_op jit(solution)/shard_map/ppermute | solution.py:120
  110.9 2.7 %collective-permute-start.5 = (bf16[64,128]{1,0:T(8,128)(2,1)S(1)}, bf16[64,128]{1,0:T(8,128)(2,1)S(1)}, u32[]{:S(2)}, u32[]{:S(2)}) collective-permute-start(bf16[64,128]{1,0:T(8,128)(2,1)S(1)} %fusion.119), channel_id=1, source_target_pairs={{128,192},{368,304},{129,193},{369,305},{130,194},{370,306},{131,1... | collective-permute-start | bytes 49160 | tf_op jit(solution)/shard_map/ppermute | solution.py:120
  116.5 0.7 collective-permute-start.6
  133.0 2.0 %collective-permute-start.9 = (f32[1024]{0:T(1024)S(1)}, f32[1024]{0:T(1024)S(1)}, u32[]{:S(2)}, u32[]{:S(2)}) collective-permute-start(f32[1024]{0:T(1024)S(1)} %reshape_squeeze.3), channel_id=1, source_target_pairs={{192,160},{304,272},{193,161},{305,273},{194,162},{306,274},{195,1... | collective-permute-start | bytes 12296 | tf_op jit(solution)/shard_map/ppermute | solution.py:133
  133.7 1.4 collective-permute-start.8
  134.4 0.7 collective-permute-start.7
  135.1 2.6 %collective-permute-start.12 = (f32[1024]{0:T(1024)S(1)}, f32[1024]{0:T(1024)S(1)}, u32[]{:S(2)}, u32[]{:S(2)}) collective-permute-start(f32[1024]{0:T(1024)S(1)} %add_add_fusion.1), channel_id=1, source_target_pairs={{160,48},{176,32},{192,16},{208,0},{272,448},{288,464},{304,480},{... | collective-permute-start | bytes 12296 | tf_op jit(solution)/shard_map/ppermute | solution.py:133
  135.8 2.0 %collective-permute-start.11 = (f32[1024]{0:T(1024)S(1)}, f32[1024]{0:T(1024)S(1)}, u32[]{:S(2)}, u32[]{:S(2)}) collective-permute-start(f32[1024]{0:T(1024)S(1)} %add_add_fusion.1), channel_id=1, source_target_pairs={{160,112},{176,96},{192,80},{208,64},{272,384},{288,400},{304,416}... | collective-permute-start | bytes 12296 | tf_op jit(solution)/shard_map/ppermute | solution.py:133
  136.4 20.7 %collective-permute-start.10 = (f32[1024]{0:T(1024)S(1)}, f32[1024]{0:T(1024)S(1)}, u32[]{:S(2)}, u32[]{:S(2)}) collective-permute-start(f32[1024]{0:T(1024)S(1)} %add_add_fusion.1), channel_id=1, source_target_pairs={{160,144},{176,128},{192,224},{208,240},{272,256},{288,336},{304,3... | collective-permute-start | bytes 12296 | tf_op jit(solution)/shard_map/ppermute | solution.py:133
Sparse Core Ops, SparseCore 0:
  23.0 63.7 all-gather.3
